TPU v7x, 32 devices: a whole 2x2x4 slice. The times are simulated.
32 devices in a mesh: dp: 16 (over z, x, core), vocab: 2 (over y).
Axes of the slice: x: 2, y: 2, z: 4, core: 2. Of those that a mesh axis runs over, the one named last changes fastest.
Arguments:
- hidden: bfloat16 [2048, 8192], P('dp', 'vocab')
- rank_factor: bfloat16 [256, 8192], P(None, 'vocab'), may hold values from -0.0625 to 0.0625
- vocab_factor: bfloat16 [256, 77824], P('dp', 'vocab')
- lengths: int32 [2048], P('dp'), may hold values from 0 to 4096, as said below
- targets: int32 [2048], P('dp'), may hold values from 0 to 77823
- cotangent: bfloat16 [2048], P('dp'), may hold values from -96 to 96
- grammar: int32 [64, 22], P('dp', 'vocab'), may hold values from 0 to 1073741823, as said below
- assign: int32 [2048], P('dp'), may hold values from 0 to 127, as said below
Outputs:
- grad_hidden: bfloat16 [2048, 8192], P('dp', 'vocab')
- grad_factor: float32 [256, 8192], P('dp', 'vocab')
Inputs may be any that keep to these rules, and one draw needn't show every extreme that they name: `lengths`: in each aligned block of 128 rows the rows with a length above 0 come first; in every draw one such block has all 128 rows above 0 and a row of length 4096. `grammar`: only bits 0 to 29 of a word are used. `assign`: each aligned block of 128 entries is a permutation of 0 to 127.
All inputs are finite; a program needn't handle non-finite values.
Results may differ from a plain program's by a relative error of at most 0.0085.
Values may be sent and summed in bfloat16 or wider, within the bound.
No kernel may reach another device: no remote copies, remote signals or barrier semaphores. Data moves between devices by JAX's collectives and lax.ppermute only.
A program may use at most 128 MiB of HBM per device.

v0:
```python
import jax
import jax.numpy as jnp
from jax import lax
from jax.sharding import PartitionSpec as P

PREFIX_MAX = 4096


far_below = -1e30


def row_grads(hidden_rows, weight, target_rows, word_rows, live_count, rank_factor, factor, first):
    row_count = hidden_rows.shape[0]
    rank = rank_factor.shape[0]
    block_rows = min(128, row_count)
    width = factor.shape[1]
    tiles = width // 128
    partial_latent = lax.dot_general(
        hidden_rows, rank_factor, (((1,), (1,)), ((), ())), preferred_element_type=jnp.float32
    )
    latent = lax.psum(partial_latent, "vocab").astype(jnp.bfloat16)
    target_local = target_rows - first
    columns = jnp.arange(width, dtype=jnp.int32)
    shifts = jnp.arange(30, dtype=jnp.int32)
    blocks_live = (live_count + block_rows - 1) // block_rows

    def block_terms():
        logits = jnp.dot(latent, factor, preferred_element_type=jnp.float32)
        bits = jnp.right_shift(word_rows[:, :, None], shifts) & 1
        bits = bits.reshape(block_rows, -1)[:, :tiles]
        tile_on = jnp.broadcast_to((bits == 1)[:, :, None], (block_rows, tiles, 128)).reshape(
            block_rows, width
        )
        target_hit = columns[None, :] == target_local[:, None]
        allowed = tile_on | target_hit
        masked = jnp.where(allowed, logits, far_below)
        local_peak = jnp.max(masked, axis=1)
        peak = lax.pmax(local_peak, "vocab")
        powers = jnp.where(allowed, jnp.exp(masked - peak[:, None]), 0.0)
        total = lax.psum(jnp.sum(powers, axis=1), "vocab")
        row_probs = powers / total[:, None]
        score_grad = (weight[:, None] * (row_probs - target_hit.astype(jnp.float32))).astype(
            jnp.bfloat16
        )
        return lax.dot_general(
            score_grad, factor, (((1,), (1,)), ((), ())), preferred_element_type=jnp.float32
        )

    def step(index, carry):
        summed = lax.psum(block_terms(), "vocab").astype(jnp.bfloat16)
        return summed

    rank_grad = lax.fori_loop(0, blocks_live, step, jnp.zeros((row_count, rank), jnp.bfloat16))
    grad_rows = jnp.dot(rank_grad, rank_factor, preferred_element_type=jnp.float32).astype(
        jnp.bfloat16
    )
    return (rank_grad, grad_rows)


def body(hidden, rank_factor, vocab_factor, lengths, targets, cotangent, grammar, assign):
    row_count = hidden.shape[0]
    groups = lax.axis_size("dp")
    share = row_count // groups
    width = vocab_factor.shape[1]
    first = lax.axis_index("vocab") * width
    factor = lax.all_gather(vocab_factor, "dp", axis=0, tiled=True)
    row_words = jnp.repeat(grammar, row_count // grammar.shape[0], axis=0)
    weight = cotangent.astype(jnp.float32) * lengths.astype(jnp.float32) / PREFIX_MAX
    live_count = jnp.sum((lengths > 0).astype(jnp.int32))
    rank_used, grad_rows = row_grads(
        hidden, weight, targets, row_words, live_count, rank_factor, factor, first
    )
    picked = jnp.take(grad_rows, assign, axis=0).reshape(groups, share, -1)
    grad_hidden = lax.all_to_all(picked, "dp", split_axis=0, concat_axis=0, tiled=True).reshape(
        row_count, -1
    )
    grad_factor = lax.psum_scatter(
        lax.dot_general(
            rank_used, hidden, (((0,), (0,)), ((), ())), preferred_element_type=jnp.float32
        ),
        "dp",
        scatter_dimension=0,
        tiled=True,
    )
    return (grad_hidden, grad_factor)


def solution(mesh):
    return jax.shard_map(
        body,
        mesh=mesh,
        in_specs=(
            P("dp", "vocab"),
            P(None, "vocab"),
            P("dp", "vocab"),
            P("dp"),
            P("dp"),
            P("dp"),
            P("dp", "vocab"),
            P("dp"),
        ),
        out_specs=(P("dp", "vocab"), P("dp", "vocab")),
        check_vma=False,
    )
```

profile of v0, /device:TPU:0, one launch (start us, length us, event | category | flops | bytes accessed | tf_op | source)
XLA Modules:
  0.0 280.0 jit_solution(16738621352985855964)
XLA Ops:
  7.2 0.7 all-gather.2.cloned.1.call-update
  8.0 1.3 fusion.6
  9.9 0.8 copy.10
  11.3 2.1 fusion.9
  13.4 11.4 %all-reduce.2 = bf16[128,256]{1,0:T(8,128)(2,1)S(1)} all-reduce(f32[128,256]{1,0:T(8,128)S(1)} %fusion.9), channel_id=1, replica_groups=mesh['dp'=16,'vocab'=2] {'vocab'}, use_global_device_ids=true, to_apply=%region_1.0 | all-reduce | flops 32768 | bytes 196608 | tf_op jit(solution)/shard_map/psum | solution.py:21
  24.8 0.7 broadcast_subtract_fusion
  25.5 0.7 multiply_multiply_fusion
  26.2 90.0 %all-gather.2.cloned.1.call-done = bf16[256,38912]{1,0:T(8,128)(2,1)} async-done(((bf16[16,38912]{1,0:T(8,128)(2,1)}), bf16[256,38912]{1,0:T(8,128)(2,1)}) %all-gather.2.cloned.1.call-update) | async-done | bytes 19922960 | tf_op jit(solution)/shard_map/all_gather | solution.py:66
  116.2 6.6 %broadcast_in_dim.55 = pred[128,304,128]{2,1,0:T(8,128)(4,1)S(1)} broadcast(pred[128,304]{1,0:T(8,128)(4,1)S(1)} %copy.11), dimensions={0,1} | broadcast | bytes 5019648 | tf_op jit(solution)/shard_map/while/body/broadcast_in_dim | solution.py:31
  122.9 17.7 %fusion = (f32[128]{0:T(128)S(1)}, f32[128,38912]{1,0:T(8,128)}) fusion(s32[128]{0:T(128)S(1)} %broadcast_subtract_fusion, s32[38912]{0:T(1024)S(1)} %add_bitcast_fusion, pred[16,8,304,128]{3,2,1,0:T(8,128)(4,1)S(1)} %bitcast.28, bf16[128,256]{1,0:T(8,128)(2,1)S(1)} %all-reduce.2, bf16[256,38912]{1,0:T(8,128)(2,1)} %all-gather.2.cloned.1.call-done), kind=kOutput, calls=%fused_computation.6 | convolution fusion | flops 2570059776 | bytes 45048832 | tf_op jit(solution)/shard_map/while/body/dot_general | solution.py:28
  140.6 4.9 %pmax.11 = f32[128]{0:T(128)S(1)} all-reduce(f32[128]{0:T(128)S(1)} %get-tuple-element.205), channel_id=1, replica_groups=mesh['dp'=16,'vocab'=2] {'vocab'}, use_global_device_ids=true, to_apply=%region_3.4 | all-reduce | flops 128 | bytes 1024 | tf_op jit(solution)/shard_map/while/body/pmax | solution.py:38
  145.5 15.0 %select_reduce_fusion = f32[128]{0:T(128)S(1)} fusion(f32[128]{0:T(128)S(1)} %pmax.11, f32[128,38912]{1,0:T(8,128)} %get-tuple-element.206, s32[128]{0:T(128)S(1)} %broadcast_subtract_fusion, s32[38912]{0:T(1024)S(1)} %add_bitcast_fusion, pred[16,8,304,128]{3,2,1,0:T(8,128)(4,1)} %bitcast.29), kind=kLoop, calls=%fused_computation.2 | loop fusion | flops 29884288 | bytes 25060864 | tf_op jit(solution)/shard_map/while/body/reduce_sum | solution.py:40
  160.5 5.1 %psum.32 = f32[128]{0:T(128)S(1)} all-reduce(f32[128]{0:T(128)S(1)} %select_reduce_fusion), channel_id=1, replica_groups=mesh['dp'=16,'vocab'=2] {'vocab'}, use_global_device_ids=true, to_apply=%region_5.6 | all-reduce | flops 128 | bytes 1024 | tf_op jit(solution)/shard_map/while/body/psum | solution.py:40
  165.7 18.5 %fusion.1 = f32[128,256]{1,0:T(8,128)S(1)} fusion(bf16[256,38912]{1,0:T(8,128)(2,1)} %all-gather.2.cloned.1.call-done, f32[128,38912]{1,0:T(8,128)} %get-tuple-element.206, pred[16,8,304,128]{3,2,1,0:T(8,128)(4,1)} %bitcast.30, f32[128]{0:T(128)S(1)} %psum.32, f32[128]{0:T(128)S(1)} %pmax.11, f32[128]{0:T(128)S(1)} %multiply_multiply_fusion, ...), kind=kOutput, calls=%fused_computation.7 | convolution fusion | flops 2599944192 | bytes 44959744 | tf_op jit(solution)/shard_map/while/body/dot_general | solution.py:45
  184.1 9.7 %all-reduce.3 = bf16[128,256]{1,0:T(8,128)(2,1)S(1)} all-reduce(f32[128,256]{1,0:T(8,128)S(1)} %fusion.1), channel_id=1, replica_groups=mesh['dp'=16,'vocab'=2] {'vocab'}, use_global_device_ids=true, to_apply=%region_6.7 | all-reduce | flops 32768 | bytes 196608 | tf_op jit(solution)/shard_map/while/body/psum | solution.py:50
  193.8 0.6 broadcast_in_dim.53
  194.5 0.6 while.16
  195.1 3.5 %fusion.10 = f32[256,4096]{1,0:T(8,128)} fusion(bf16[128,256]{1,0:T(8,128)(2,1)} %get-tuple-element.196, bf16[128,4096]{1,0:T(8,128)(2,1)S(1)} %copy-done.2), kind=kOutput, calls=%fused_computation.26 | convolution fusion | flops 268435456 | bytes 5308416 | tf_op jit(solution)/shard_map/dot_general | solution.py:78
  198.8 1.3 convolution_convert_fusion
  200.1 2.2 gather_fusion
  202.2 1.4 bitcast_select_fusion
  203.6 31.9 %all_to_all.5 = bf16[16,8,4096]{2,1,0:T(8,128)(2,1)S(1)} all-to-all(bf16[16,8,4096]{2,1,0:T(8,128)(2,1)S(1)} %bitcast_select_fusion), channel_id=1, replica_groups=mesh['dp'=16,'vocab'=2] {'dp'}, dimensions={0} | all-to-all | bytes 2097152 | tf_op jit(solution)/shard_map/all_to_all | solution.py:74
  235.5 36.7 %reduce-scatter.2.cloned.1.call-done = f32[16,4096]{1,0:T(8,128)} async-done(((f32[256,4096]{1,0:T(8,128)}), f32[16,4096]{1,0:T(8,128)}) %reduce-scatter.2.cloned.1.call-update) | async-done | bytes 262160 | tf_op jit(solution)/shard_map/reduce_scatter | solution.py:77
  272.2 1.0 copy.33
  (25 shorter events, 1.4 us)
Async XLA Ops:
  7.2 4.1 %copy-start = (bf16[256,4096]{1,0:T(8,128)(2,1)S(1)}, bf16[256,4096]{1,0:T(8,128)(2,1)}, u32[]{:S(2)}) copy-start(bf16[256,4096]{1,0:T(8,128)(2,1)} %param.11) | copy-start | bytes 6291460
  7.2 109.1 %all-gather.2.cloned.1.call-start = ((), (), s32[]{:S(2)}) async-start(), calls=%async_computation.2 | async-start | bytes 21168128 | tf_op jit(solution)/shard_map/all_gather | solution.py:66
  7.9 264.3 %reduce-scatter.2.cloned.1.call-start = ((), (), s32[]{:S(2)}) async-start(), calls=%async_computation.3 | async-start | bytes 4456448 | tf_op jit(solution)/shard_map/reduce_scatter | solution.py:77
  122.9 17.7 %copy-start.1 = (pred[128,304,128]{2,1,0:T(8,128)(4,1)}, pred[128,304,128]{2,1,0:T(8,128)(4,1)S(1)}, u32[]{:S(2)}) copy-start(pred[128,304,128]{2,1,0:T(8,128)(4,1)S(1)} %broadcast_in_dim.55) | copy-start | bytes 14942212
  165.6 29.5 %copy-start.2 = (bf16[128,4096]{1,0:T(8,128)(2,1)S(1)}, bf16[128,4096]{1,0:T(8,128)(2,1)}, u32[]{:S(2)}) copy-start(bf16[128,4096]{1,0:T(8,128)(2,1)} %param.10) | copy-start | bytes 3145732
  165.6 33.0 %copy-start.3 = (s32[128]{0:T(128)S(1)}, s32[128]{0:T(128)}, u32[]{:S(2)}) copy-start(s32[128]{0:T(128)} %param.17) | copy-start | bytes 1540
Sparse Core Ops, SparseCore 0:
  9.6 106.5 all-gather.1
  198.8 73.4 reduce-scatter.1
where the time goes:
time: 281 us; the launch traced here: 280 us
  waiting for transfers between devices  127 us (45%)
  blocking collectives  63.1 us (22%)
  matrix products  43 us (15%)
  other arithmetic  19.2 us (7%)
  between operations  14.9 us (5%)
  local copies, waits for them, and re-layouts  12.3 us (4%)
    all_gather x1, waiting for transfers between devices, body(): factor = lax.all_gather(vocab_factor, 'dp', axis=0, tiled=True)  90 us
    reduce_scatter x1, waiting for transfers between devices, body(): lax.psum_scatter(lax.dot_general(rank_used, hidden, (((0,), (0,)), ((), (...  36.7 us
    all_to_all x1, blocking collectives, body(): lax.all_to_all(picked, 'dp', split_axis=0, concat_axis=0, tiled=True)  31.9 us
    dot_general x1, matrix products, block_terms(): lax.dot_general(score_grad, factor, (((1,), (1,)), ((), ())), preferred_e...  18.5 us
    dot_general x1, matrix products, block_terms(): logits = jnp.dot(latent, factor, preferred_element_type=jnp.float32)  17.7 us
    reduce_sum x1, other arithmetic, block_terms(): total = lax.psum(jnp.sum(powers, axis=1), 'vocab')  15 us
    psum x1, blocking collectives, row_grads(): latent = lax.psum(partial_latent, 'vocab').astype(jnp.bfloat16)  11.4 us
    psum x1, blocking collectives, step(): summed = lax.psum(block_terms(), 'vocab').astype(jnp.bfloat16)  9.72 us
  transfers between devices with their start and end apart: 2, of which 2 were waited for; matrix products, arithmetic and copies ran while one was open for 4% of the time, Pallas kernels for 0%

commit v1 on v0

v1 whole, which is shorter than its diff:
```python
import jax
import jax.numpy as jnp
from jax import lax
from jax.sharding import PartitionSpec as P

PREFIX_MAX = 4096
TILE = 128
WORD_BITS = 30


far_below = -1e30


def body(hidden, rank_factor, vocab_factor, lengths, targets, cotangent, grammar, assign):
    row_count = hidden.shape[0]
    rank = rank_factor.shape[0]
    groups = lax.axis_size("dp")
    share = row_count // groups
    width = vocab_factor.shape[1]
    cols = width // groups
    dp_index = lax.axis_index("dp")
    vocab_index = lax.axis_index("vocab")

    partial_latent = lax.dot_general(
        hidden, rank_factor, (((1,), (1,)), ((), ())), preferred_element_type=jnp.float32
    )
    latent = lax.psum(partial_latent, "vocab").astype(jnp.bfloat16)
    weight = cotangent.astype(jnp.float32) * lengths.astype(jnp.float32) / PREFIX_MAX

    latent_all = lax.all_gather(latent, "dp", axis=0, tiled=True)
    weight_all = lax.all_gather(weight, "dp", axis=0, tiled=True)
    target_all = lax.all_gather(targets, "dp", axis=0, tiled=True)
    words_all = lax.all_gather(grammar, "dp", axis=0, tiled=True)
    factor = lax.all_to_all(vocab_factor, "dp", split_axis=1, concat_axis=0, tiled=True)

    total_rows = latent_all.shape[0]
    row_block = total_rows // words_all.shape[0]
    first_col = dp_index * cols
    col_ids = first_col + jnp.arange(cols, dtype=jnp.int32)
    tile_ids = col_ids // TILE
    words = jnp.take(words_all, tile_ids // WORD_BITS, axis=1)
    block_on = (jnp.right_shift(words, (tile_ids % WORD_BITS)[None, :]) & 1) == 1
    tile_on = jnp.broadcast_to(block_on[:, None, :], (words_all.shape[0], row_block, cols)).reshape(
        total_rows, cols
    )
    target_local = target_all - vocab_index * width - first_col
    target_hit = jnp.arange(cols, dtype=jnp.int32)[None, :] == target_local[:, None]
    allowed = tile_on | target_hit

    logits = jnp.dot(latent_all, factor, preferred_element_type=jnp.float32)
    masked = jnp.where(allowed, logits, far_below)
    local_peak = jnp.max(masked, axis=1)
    local_total = jnp.sum(jnp.where(allowed, jnp.exp(masked - local_peak[:, None]), 0.0), axis=1)
    stats = lax.all_gather(jnp.stack([local_peak, local_total]), ("dp", "vocab"), axis=0)
    peak = jnp.max(stats[:, 0], axis=0)
    total = jnp.sum(stats[:, 1] * jnp.exp(stats[:, 0] - peak[None, :]), axis=0)

    powers = jnp.where(allowed, jnp.exp(masked - peak[:, None]), 0.0)
    row_probs = powers / total[:, None]
    score_grad = (weight_all[:, None] * (row_probs - target_hit.astype(jnp.float32))).astype(jnp.bfloat16)
    rank_partial = lax.dot_general(
        score_grad, factor, (((1,), (1,)), ((), ())), preferred_element_type=jnp.float32
    )
    rank_rows = lax.psum_scatter(rank_partial, "dp", scatter_dimension=0, tiled=True)
    rank_grad = lax.psum(rank_rows, "vocab").astype(jnp.bfloat16)

    grad_factor = lax.psum_scatter(
        lax.dot_general(
            rank_grad, hidden, (((0,), (0,)), ((), ())), preferred_element_type=jnp.float32
        ),
        "dp",
        scatter_dimension=0,
        tiled=True,
    )
    picked = jnp.take(rank_grad, assign, axis=0).reshape(groups, share, rank)
    slot_rank = lax.all_to_all(picked, "dp", split_axis=0, concat_axis=0, tiled=True).reshape(
        row_count, rank
    )
    grad_hidden = jnp.dot(slot_rank, rank_factor, preferred_element_type=jnp.float32).astype(
        jnp.bfloat16
    )
    return (grad_hidden, grad_factor)


def solution(mesh):
    return jax.shard_map(
        body,
        mesh=mesh,
        in_specs=(
            P("dp", "vocab"),
            P(None, "vocab"),
            P("dp", "vocab"),
            P("dp"),
            P("dp"),
            P("dp"),
            P("dp", "vocab"),
            P("dp"),
        ),
        out_specs=(P("dp", "vocab"), P("dp", "vocab")),
        check_vma=False,
    )
```

time: 281 us -> 365 us (1.30)
  blocking collectives: 63.1 us -> 166 us
  matrix products: 43 us -> 23.1 us
  waiting for transfers between devices: 127 us -> 116 us
  other arithmetic: 19.2 us -> 27.6 us
  starting transfers between devices: 0.08 us -> 7.48 us
    all_gather x0 -> x4, blocking collectives: none -> 135 us  [the longest x1 69 us: body(): lax.all_gather(jnp.stack([local_peak, local_total]), ('dp', 'vocab'), axi...]
    all_gather x1, waiting for transfers between devices: 90 us -> 0.01 us  [body(): latent_all = lax.all_gather(latent, 'dp', axis=0, tiled=True)]
    reduce_scatter x1 -> x2, waiting for transfers between devices: 36.7 us -> 116 us  [the longest x1 58.3 us: body(): lax.psum_scatter(lax.dot_general(rank_grad, hidden, (((0,), (0,)), ((), (...]
    all_to_all x1, blocking collectives: 31.9 us -> 10.4 us  [body(): lax.all_to_all(picked, 'dp', split_axis=0, concat_axis=0, tiled=True)]
    dot_general x5, matrix products: 43 us -> 23.1 us  [the longest x1 8.07 us: body(): lax.dot_general(score_grad, factor, (((1,), (1,)), ((), ())), preferred_e...]
    convert_element_type x0 -> x1, other arithmetic: none -> 14.6 us  [body(): (weight_all[:, None] * (row_probs - target_hit.astype(jnp.float32))).asty...]
    reduce_sum x2, other arithmetic: 16.3 us -> 8.13 us  [the longest x1 7.95 us: body(): jnp.sum(jnp.where(allowed, jnp.exp(masked - local_peak[:, None]), 0.0), a...]
    all_to_all x0 -> x1, starting transfers between devices: none -> 7.36 us  [body(): lax.all_to_all(vocab_factor, 'dp', split_axis=1, concat_axis=0, tiled=True)]
  transfers between devices with their start and end apart: 2 -> 4, of which waited for: 2 -> 2; matrix products, arithmetic and copies ran while one was open for 4% -> 4% of each run, Pallas kernels for 0% -> 0%
where the time goes in v1:
time: 365 us; the launch traced here: 364 us
  blocking collectives  166 us (45%)
  waiting for transfers between devices  116 us (32%)
  other arithmetic  27.6 us (8%)
  matrix products  23.1 us (6%)
  between operations  13.9 us (4%)
  local copies, waits for them, and re-layouts  10.6 us (3%)
  starting transfers between devices  7.48 us (2%)
    all_gather x1, blocking collectives, body(): lax.all_gather(jnp.stack([local_peak, local_total]), ('dp', 'vocab'), axi...  69 us
    reduce_scatter x1, waiting for transfers between devices, body(): lax.psum_scatter(lax.dot_general(rank_grad, hidden, (((0,), (0,)), ((), (...  58.3 us
    reduce_scatter x1, waiting for transfers between devices, body(): lax.psum_scatter(rank_partial, 'dp', scatter_dimension=0, tiled=True)  57.5 us
    all_gather x1, blocking collectives, body(): words_all = lax.all_gather(grammar, 'dp', axis=0, tiled=True)  24.2 us
    all_gather x1, blocking collectives, body(): target_all = lax.all_gather(targets, 'dp', axis=0, tiled=True)  24.1 us
    all_gather x1, blocking collectives, body(): weight_all = lax.all_gather(weight, 'dp', axis=0, tiled=True)  17.3 us
    convert_element_type x1, other arithmetic, body(): (weight_all[:, None] * (row_probs - target_hit.astype(jnp.float32))).asty...  14.6 us
    psum x1, blocking collectives, body(): latent = lax.psum(partial_latent, 'vocab').astype(jnp.bfloat16)  10.4 us
  transfers between devices with their start and end apart: 4, of which 2 were waited for; matrix products, arithmetic and copies ran while one was open for 4% of the time, Pallas kernels for 0%

profile of v1, /device:TPU:0, one launch (start us, length us, event | category | flops | bytes accessed | tf_op | source)
XLA Modules:
  0.0 364.4 jit_solution(7488139474883811638)
XLA Ops:
  7.2 2.6 copy.34
  9.8 7.4 %all-to-all-start = ((bf16[16,16,2432]{2,0,1:T(8,128)(2,1)}), bf16[16,16,2432]{2,0,1:T(8,128)(2,1)S(1)}, u32[]{:S(2)}, u32[]{:S(2)}) async-start(bf16[16,16,2432]{2,0,1:T(8,128)(2,1)} %bitcast.58), calls=%async_computation | async-start | bytes 2490368 | tf_op jit(solution)/shard_map/all_to_all | solution.py:34
  17.2 2.1 fusion.13
  19.3 10.4 %all-reduce.2 = bf16[128,256]{1,0:T(8,128)(2,1)} all-reduce(f32[128,256]{1,0:T(8,128)S(1)} %fusion.13), channel_id=1, replica_groups=mesh['dp'=16,'vocab'=2] {'vocab'}, use_global_device_ids=true, to_apply=%region_0.0 | all-reduce | flops 32768 | bytes 196608 | tf_op jit(solution)/shard_map/psum | solution.py:27
  29.8 24.2 %all-gather.2 = s32[16,4,11]{2,1,0:T(4,128)S(1)} all-gather(s32[1,4,11]{2,1,0:T(4,128)S(1)} %bitcast.68), channel_id=1, replica_groups=mesh['dp'=16,'vocab'=2] {'dp'}, dimensions={0}, use_global_device_ids=true | all-gather | bytes 2992 | tf_op jit(solution)/shard_map/all_gather | solution.py:33
  54.2 5.6 %gather_fusion = s32[2432,64]{1,0:T(8,128)} fusion(s32[64,11]{0,1:T(8,128)S(1)} %copy.20, s32[3072]{0:T(1024)S(1)} %pad_clamp_fusion), kind=kCustom, calls=%fused_computation | custom fusion | bytes 1254912 | tf_op jit(solution)/shard_map/jit(_take)/gather | solution.py:41
  59.8 4.1 %fusion.2 = pred[64,2432]{0,1:T(8,128)(4,1)} fusion(s32[2432,64]{1,0:T(8,128)} %gather_fusion, s32[2432]{0:T(1024)S(1)} %add_select_fusion, pred[2432]{0:T(1024)(128)(4,1)S(1)} %compare_and_fusion), kind=kLoop, calls=%fused_computation.10 | loop fusion | flops 622592 | bytes 790400 | tf_op jit(solution)/shard_map/eq | solution.py:42
  63.9 1.4 copy.21
  65.3 24.1 %all-gather.3 = s32[16,1,128]{2,1,0:T(1,128)S(1)} all-gather(s32[1,1,128]{2,1,0:T(1,128)S(1)} %bitcast.69), channel_id=1, replica_groups=mesh['dp'=16,'vocab'=2] {'dp'}, dimensions={0}, use_global_device_ids=true | all-gather | bytes 8704 | tf_op jit(solution)/shard_map/all_gather | solution.py:32
  89.5 17.3 %all-gather.1 = f32[16,1,128]{2,1,0:T(1,128)S(1)} all-gather(f32[1,1,128]{2,1,0:T(1,128)S(1)} %multiply_bitcast_fusion), channel_id=1, replica_groups=mesh['dp'=16,'vocab'=2] {'dp'}, dimensions={0}, use_global_device_ids=true | all-gather | bytes 8704 | tf_op jit(solution)/shard_map/all_gather | solution.py:31
  106.8 7.6 %fusion.12 = (f32[2048]{0:T(1024)S(1)}, f32[2048,2432]{1,0:T(8,128)S(1)}) fusion(bf16[2048,256]{1,0:T(8,128)(2,1)} %all-gather.7.cloned.1.call-done, bf16[256,2432]{1,0:T(8,128)(2,1)S(1)} %bitcast.56, s32[2048]{0:T(1024)S(1)} %bitcast.60, pred[64,2432]{1,0:T(8,128)(4,1)S(1)} %copy.21), kind=kOutput, calls=%fused_computation.49 | convolution fusion | flops 2570057728 | bytes 22388736 | tf_op jit(solution)/shard_map/dot_general | solution.py:50
  114.5 7.9 %select_reduce_fusion = f32[2048]{0:T(1024)S(1)} fusion(f32[2048,2432]{1,0:T(8,128)S(1)} %get-tuple-element.6, f32[2048]{0:T(1024)S(1)} %get-tuple-element.5, s32[2048]{0:T(1024)S(1)} %bitcast.61, pred[64,2432]{1,0:T(8,128)(4,1)S(1)} %copy.21), kind=kLoop, calls=%fused_computation.3 | loop fusion | flops 24901632 | bytes 20103168 | tf_op jit(solution)/shard_map/reduce_sum | solution.py:53
  122.4 69.0 %all-gather.4 = f32[32,2,2048]{2,1,0:T(2,128)S(1)} all-gather(f32[1,2,2048]{2,1,0:T(2,128)S(1)} %maximum_bitcast_fusion), channel_id=2, replica_groups=mesh['dp'=16,'vocab'=2] {'dp','vocab'}, dimensions={0}, use_global_device_ids=true | all-gather | bytes 540672 | tf_op jit(solution)/shard_map/all_gather | solution.py:54
  191.4 0.5 slice_reduce_fusion
  191.9 0.2 fusion.4
  192.1 14.6 %multiply_convert_fusion = bf16[2048,2432]{1,0:T(8,128)(2,1)} fusion(f32[2048,2432]{1,0:T(8,128)S(1)} %get-tuple-element.6, f32[2048]{0:T(1024)S(1)} %fusion.4, f32[2048]{0:T(1024)S(1)} %get-tuple-element.2, s32[2048]{0:T(1024)S(1)} %bitcast.62, f32[2048]{0:T(1024)S(1)} %bitcast.65, pred[64,2432]{1,0:T(8,128)(4,1)S(1)} %copy.21), kind=kLoop, calls=%fused_computation.2 | loop fusion | flops 44826624 | bytes 30072832 | tf_op jit(solution)/shard_map/convert_element_type | solution.py:60
  206.7 8.1 %fusion.14 = f32[2048,256]{1,0:T(8,128)} fusion(bf16[2048,2432]{1,0:T(8,128)(2,1)} %multiply_convert_fusion, bf16[256,2432]{1,0:T(8,128)(2,1)S(1)} %bitcast.57), kind=kOutput, calls=%fused_computation.51 | convolution fusion | flops 2550136832 | bytes 13303808 | tf_op jit(solution)/shard_map/dot_general | solution.py:61
  214.8 57.5 %reduce-scatter.3.cloned.1.call-done = f32[128,256]{1,0:T(8,128)} async-done(((f32[2048,256]{1,0:T(8,128)}), f32[128,256]{1,0:T(8,128)}) %reduce-scatter.3.cloned.1.call-update) | async-done | bytes 131088 | tf_op jit(solution)/shard_map/reduce_scatter | solution.py:64
  272.4 10.4 %all-reduce.3 = bf16[128,256]{1,0:T(8,128)(2,1)S(1)} all-reduce(f32[128,256]{1,0:T(8,128)} %reduce-scatter.3.cloned.1.call-done), channel_id=1, replica_groups=mesh['dp'=16,'vocab'=2] {'vocab'}, use_global_device_ids=true, to_apply=%region_6.7 | all-reduce | flops 32768 | bytes 196608 | tf_op jit(solution)/shard_map/psum | solution.py:65
  282.7 3.9 %fusion.15 = f32[256,4096]{1,0:T(8,128)} fusion(bf16[128,256]{1,0:T(8,128)(2,1)S(1)} %all-reduce.3, bf16[128,4096]{1,0:T(8,128)(2,1)} %param.8), kind=kOutput, calls=%fused_computation.52 | convolution fusion | flops 268435456 | bytes 5308416 | tf_op jit(solution)/shard_map/dot_general | solution.py:68
  286.8 0.8 gather_fusion.1
  287.7 10.4 %all_to_all.24 = bf16[16,8,256]{2,1,0:T(8,128)(2,1)S(1)} all-to-all(bf16[16,8,256]{2,1,0:T(8,128)(2,1)S(1)} %bitcast_select_fusion), channel_id=1, replica_groups=mesh['dp'=16,'vocab'=2] {'dp'}, dimensions={0} | all-to-all | bytes 131072 | tf_op jit(solution)/shard_map/all_to_all | solution.py:76
  298.1 1.4 convolution_convert_fusion
  299.6 58.3 %reduce-scatter.5.cloned.1.call-done = f32[16,4096]{1,0:T(8,128)} async-done(((f32[256,4096]{1,0:T(8,128)}), f32[16,4096]{1,0:T(8,128)}) %reduce-scatter.5.cloned.1.call-update) | async-done | bytes 262160 | tf_op jit(solution)/shard_map/reduce_scatter | solution.py:67
  (33 shorter events, 0.7 us)
Async XLA Ops:
  7.2 10.0 %copy-start = (bf16[256,4096]{1,0:T(8,128)(2,1)S(1)}, bf16[256,4096]{1,0:T(8,128)(2,1)}, u32[]{:S(2)}) copy-start(bf16[256,4096]{1,0:T(8,128)(2,1)} %param.9) | copy-start | bytes 6291460
  7.2 22.6 %copy-start.1 = (s32[4,11]{1,0:T(4,128)S(1)}, s32[4,11]{1,0:T(4,128)}, u32[]{:S(2)}) copy-start(s32[4,11]{1,0:T(4,128)} %param.14) | copy-start | bytes 532
  9.8 97.0 %all-to-all-start = ((bf16[16,16,2432]{2,0,1:T(8,128)(2,1)}), bf16[16,16,2432]{2,0,1:T(8,128)(2,1)S(1)}, u32[]{:S(2)}, u32[]{:S(2)}) async-start(bf16[16,16,2432]{2,0,1:T(8,128)(2,1)} %bitcast.58), calls=%async_computation | async-start | bytes 2490368 | tf_op jit(solution)/shard_map/all_to_all | solution.py:34
  17.1 48.2 %copy-start.2 = (s32[128]{0:T(128)S(1)}, s32[128]{0:T(128)}, u32[]{:S(2)}) copy-start(s32[128]{0:T(128)} %param.12) | copy-start | bytes 1540
  17.1 72.4 %copy-start.3 = (s32[128]{0:T(128)S(1)}, s32[128]{0:T(128)}, u32[]{:S(2)}) copy-start(s32[128]{0:T(128)} %param.11) | copy-start | bytes 1540
  17.1 72.3 %copy-start.4 = (bf16[128]{0:T(256)(128)(2,1)S(1)}, bf16[128]{0:T(256)(128)(2,1)}, u32[]{:S(2)}) copy-start(bf16[128]{0:T(256)(128)(2,1)} %param.13) | copy-start | bytes 772
  17.2 89.6 %all-gather.7.cloned.1.call-start = ((), (), s32[]{:S(2)}) async-start(), calls=%async_computation.4 | async-start | bytes 1114112 | tf_op jit(solution)/shard_map/all_gather | solution.py:30
  29.7 242.6 %reduce-scatter.3.cloned.1.call-start = ((), (), s32[]{:S(2)}) async-start(), calls=%async_computation.5 | async-start | bytes 2228224 | tf_op jit(solution)/shard_map/reduce_scatter | solution.py:64
  214.8 71.9 %copy-start.5 = (s32[128]{0:T(128)S(1)}, s32[128]{0:T(128)}, u32[]{:S(2)}) copy-start(s32[128]{0:T(128)} %param.15) | copy-start | bytes 1540
  214.8 143.1 %reduce-scatter.5.cloned.1.call-start = ((), (), s32[]{:S(2)}) async-start(), calls=%async_computation.6 | async-start | bytes 4456448 | tf_op jit(solution)/shard_map/reduce_scatter | solution.py:67
Sparse Core Ops, SparseCore 0:
  29.8 39.2 all-gather.6
  214.9 57.4 reduce-scatter.2
  286.8 71.0 reduce-scatter.4

commit v2 on v1

--- a/solution.py
+++ b/solution.py
@@ -27,20 +27,40 @@
     latent = lax.psum(partial_latent, "vocab").astype(jnp.bfloat16)
     weight = cotangent.astype(jnp.float32) * lengths.astype(jnp.float32) / PREFIX_MAX
 
-    latent_all = lax.all_gather(latent, "dp", axis=0, tiled=True)
-    weight_all = lax.all_gather(weight, "dp", axis=0, tiled=True)
-    target_all = lax.all_gather(targets, "dp", axis=0, tiled=True)
-    words_all = lax.all_gather(grammar, "dp", axis=0, tiled=True)
+    words_local = grammar.shape[0]
+    row_block = row_count // words_local
+    mask_words = grammar.shape[1]
+    row_words = jnp.repeat(grammar, row_block, axis=0)
+    packed = jnp.concatenate(
+        [
+            latent.astype(jnp.float32),
+            weight[:, None],
+            targets.astype(jnp.float32)[:, None],
+            jnp.right_shift(row_words, 15).astype(jnp.float32),
+            (row_words & 32767).astype(jnp.float32),
+        ],
+        axis=1,
+    )
+    packed_all = lax.all_gather(packed, "dp", axis=0, tiled=True)
     factor = lax.all_to_all(vocab_factor, "dp", split_axis=1, concat_axis=0, tiled=True)
 
-    total_rows = latent_all.shape[0]
-    row_block = total_rows // words_all.shape[0]
+    total_rows = packed_all.shape[0]
+    blocks = total_rows // row_block
+    latent_all = packed_all[:, :rank].astype(jnp.bfloat16)
+    weight_all = packed_all[:, rank]
+    target_all = packed_all[:, rank + 1].astype(jnp.int32)
+    block_rows = packed_all.reshape(blocks, row_block, -1)[:, 0, rank + 2 :].astype(jnp.int32)
+    words_all = jnp.left_shift(block_rows[:, :mask_words], 15) | block_rows[:, mask_words:]
+
     first_col = dp_index * cols
     col_ids = first_col + jnp.arange(cols, dtype=jnp.int32)
     tile_ids = col_ids // TILE
-    words = jnp.take(words_all, tile_ids // WORD_BITS, axis=1)
+    word_ids = tile_ids // WORD_BITS
+    words = jnp.zeros((blocks, cols), jnp.int32)
+    for w in range(mask_words):
+        words = jnp.where(word_ids[None, :] == w, words_all[:, w : w + 1], words)
     block_on = (jnp.right_shift(words, (tile_ids % WORD_BITS)[None, :]) & 1) == 1
-    tile_on = jnp.broadcast_to(block_on[:, None, :], (words_all.shape[0], row_block, cols)).reshape(
+    tile_on = jnp.broadcast_to(block_on[:, None, :], (blocks, row_block, cols)).reshape(
         total_rows, cols
     )
     target_local = target_all - vocab_index * width - first_col
@@ -49,13 +69,9 @@
 
     logits = jnp.dot(latent_all, factor, preferred_element_type=jnp.float32)
     masked = jnp.where(allowed, logits, far_below)
-    local_peak = jnp.max(masked, axis=1)
-    local_total = jnp.sum(jnp.where(allowed, jnp.exp(masked - local_peak[:, None]), 0.0), axis=1)
-    stats = lax.all_gather(jnp.stack([local_peak, local_total]), ("dp", "vocab"), axis=0)
-    peak = jnp.max(stats[:, 0], axis=0)
-    total = jnp.sum(stats[:, 1] * jnp.exp(stats[:, 0] - peak[None, :]), axis=0)
-
+    peak = lax.pmax(jnp.max(masked, axis=1), ("dp", "vocab"))
     powers = jnp.where(allowed, jnp.exp(masked - peak[:, None]), 0.0)
+    total = lax.psum(jnp.sum(powers, axis=1), ("dp", "vocab"))
     row_probs = powers / total[:, None]
     score_grad = (weight_all[:, None] * (row_probs - target_hit.astype(jnp.float32))).astype(jnp.bfloat16)
     rank_partial = lax.dot_general(

time: 365 us -> 365 us (level)
  blocking collectives: 166 us -> 113 us
  waiting for transfers between devices: 116 us -> 169 us
  other arithmetic: 27.6 us -> 32.4 us
    all_gather x4 -> x0, blocking collectives: 135 us -> none  [the longest x1 69 us: body(): lax.all_gather(jnp.stack([local_peak, local_total]), ('dp', 'vocab'), axi...]
    all_gather x1, waiting for transfers between devices: 0.01 us -> 49.3 us  [body(): packed_all = lax.all_gather(packed, 'dp', axis=0, tiled=True)]
    psum x0 -> x1, blocking collectives: none -> 40.8 us  [body(): total = lax.psum(jnp.sum(powers, axis=1), ('dp', 'vocab'))]
    pmax x0 -> x1, blocking collectives: none -> 39.7 us  [body(): peak = lax.pmax(jnp.max(masked, axis=1), ('dp', 'vocab'))]
    gather x1 -> x0, local copies, waits for them, and re-layouts: 5.57 us -> none  [body(): words = jnp.take(words_all, tile_ids // WORD_BITS, axis=1)]
    dot_general x1, matrix products: 8.07 us -> 4.36 us  [body(): lax.dot_general(score_grad, factor, (((1,), (1,)), ((), ())), preferred_e...]
    reduce_sum x2 -> x1, other arithmetic: 8.13 us -> 11.4 us  [body(): total = lax.psum(jnp.sum(powers, axis=1), ('dp', 'vocab'))]
  transfers between devices with their start and end apart: 4 -> 4, of which waited for: 2 -> 3; matrix products, arithmetic and copies ran while one was open for 4% -> 3% of each run, Pallas kernels for 0% -> 0%
where the time goes in v2:
time: 365 us; the launch traced here: 364 us
  waiting for transfers between devices  169 us (46%)
  blocking collectives  113 us (31%)
  other arithmetic  32.4 us (9%)
  matrix products  22.4 us (6%)
  between operations  13.9 us (4%)
  local copies, waits for them, and re-layouts  7.85 us (2%)
  starting transfers between devices  5.77 us (2%)
    reduce_scatter x1, waiting for transfers between devices, body(): lax.psum_scatter(rank_partial, 'dp', scatter_dimension=0, tiled=True)  60.9 us
    reduce_scatter x1, waiting for transfers between devices, body(): lax.psum_scatter(lax.dot_general(rank_grad, hidden, (((0,), (0,)), ((), (...  58.4 us
    all_gather x1, waiting for transfers between devices, body(): packed_all = lax.all_gather(packed, 'dp', axis=0, tiled=True)  49.3 us
    psum x1, blocking collectives, body(): total = lax.psum(jnp.sum(powers, axis=1), ('dp', 'vocab'))  40.8 us
    pmax x1, blocking collectives, body(): peak = lax.pmax(jnp.max(masked, axis=1), ('dp', 'vocab'))  39.7 us
    convert_element_type x1, other arithmetic, body(): (weight_all[:, None] * (row_probs - target_hit.astype(jnp.float32))).asty...  14.3 us
    psum x1, blocking collectives, body(): latent = lax.psum(partial_latent, 'vocab').astype(jnp.bfloat16)  11.4 us
    reduce_sum x1, other arithmetic, body(): total = lax.psum(jnp.sum(powers, axis=1), ('dp', 'vocab'))  11.4 us
  transfers between devices with their start and end apart: 4, of which 3 were waited for; matrix products, arithmetic and copies ran while one was open for 3% of the time, Pallas kernels for 0%

profile of v2, /device:TPU:0, one launch (start us, length us, event | category | flops | bytes accessed | tf_op | source)
XLA Modules:
  0.0 363.7 jit_solution(1812839883864206838)
XLA Ops:
  7.2 0.8 and_convert_fusion
  8.8 2.1 fusion.13
  10.8 11.4 %all-reduce.2 = bf16[128,256]{1,0:T(8,128)(2,1)S(1)} all-reduce(f32[128,256]{1,0:T(8,128)S(1)} %fusion.13), channel_id=1, replica_groups=mesh['dp'=16,'vocab'=2] {'vocab'}, use_global_device_ids=true, to_apply=%region_0.0 | all-reduce | flops 32768 | bytes 196608 | tf_op jit(solution)/shard_map/psum | solution.py:27
  23.9 0.8 concatenate.3
  24.7 2.4 copy.27
  27.1 5.6 %all-to-all-start = ((bf16[16,16,2432]{2,0,1:T(8,128)(2,1)}), bf16[16,16,2432]{2,0,1:T(8,128)(2,1)S(1)}, u32[]{:S(2)}, u32[]{:S(2)}) async-start(bf16[16,16,2432]{2,0,1:T(8,128)(2,1)} %bitcast.67), calls=%async_computation | async-start | bytes 2490368 | tf_op jit(solution)/shard_map/all_to_all | solution.py:45
  33.7 49.3 %all-gather.2.cloned.1.call-done = f32[2048,280]{1,0:T(8,128)} async-done(((f32[128,280]{1,0:T(8,128)}), f32[2048,280]{1,0:T(8,128)}) %all-gather.2.cloned.1.call-update) | async-done | bytes 2293776 | tf_op jit(solution)/shard_map/all_gather | solution.py:44
  83.0 1.1 slice.72
  84.1 1.9 fusion.7
  86.1 1.8 and_compare_fusion
  87.9 10.7 %fusion.2 = (f32[2048]{0:T(1024)S(1)}, f32[2048,2432]{1,0:T(8,128)}) fusion(s32[2048]{0:T(1024)S(1)} %fusion.7, pred[64,2432]{1,0:T(8,128)(4,1)S(1)} %and_compare_fusion, bf16[256,2432]{1,0:T(8,128)(2,1)S(1)} %bitcast.65, f32[2048,280]{1,0:T(8,128)} %all-gather.2.cloned.1.call-done), kind=kOutput, calls=%fused_computation.6 | convolution fusion | flops 2570057728 | bytes 22388736 | tf_op jit(solution)/shard_map/dot_general | solution.py:70
  98.6 39.7 %pmax.7 = f32[2048]{0:T(1024)S(1)} all-reduce(f32[2048]{0:T(1024)S(1)} %get-tuple-element.15), channel_id=1, replica_groups=mesh['dp'=16,'vocab'=2] {'dp','vocab'}, use_global_device_ids=true, to_apply=%region_2.3 | all-reduce | flops 2048 | bytes 16384 | tf_op jit(solution)/shard_map/pmax | solution.py:72
  138.3 11.4 %fusion.3 = f32[2048]{0:T(1024)S(1)} fusion(f32[2048,2432]{1,0:T(8,128)} %get-tuple-element.16, f32[2048]{0:T(1024)S(1)} %pmax.7, s32[2048]{0:T(1024)S(1)} %fusion.7, pred[64,2432]{1,0:T(8,128)(4,1)S(1)} %and_compare_fusion), kind=kLoop, calls=%fused_computation.7 | loop fusion | flops 29882368 | bytes 20103168 | tf_op jit(solution)/shard_map/reduce_sum | solution.py:74
  149.7 40.8 %psum.22 = f32[2048]{0:T(1024)S(1)} all-reduce(f32[2048]{0:T(1024)S(1)} %fusion.3), channel_id=1, replica_groups=mesh['dp'=16,'vocab'=2] {'dp','vocab'}, use_global_device_ids=true, to_apply=%region_4.5 | all-reduce | flops 2048 | bytes 16384 | tf_op jit(solution)/shard_map/psum | solution.py:74
  190.5 1.6 slice_reduce_fusion
  192.1 14.3 %multiply_convert_fusion = bf16[2048,2432]{1,0:T(8,128)(2,1)S(1)} fusion(f32[2048,2432]{1,0:T(8,128)} %get-tuple-element.16, f32[2048]{0:T(1024)S(1)} %psum.22, f32[2048]{0:T(1024)S(1)} %pmax.7, s32[2048]{0:T(1024)S(1)} %fusion.7, f32[2048]{0:T(1024)S(1)} %slice_reduce_fusion, pred[64,2432]{1,0:T(8,128)(4,1)S(1)} %and_compare_fusion), kind=kLoop, calls=%fused_computation.1 | loop fusion | flops 49807360 | bytes 30072832 | tf_op jit(solution)/shard_map/convert_element_type | solution.py:76
  206.3 4.4 %fusion.14 = f32[2048,256]{1,0:T(8,128)} fusion(bf16[2048,2432]{1,0:T(8,128)(2,1)S(1)} %multiply_convert_fusion, bf16[256,2432]{1,0:T(8,128)(2,1)S(1)} %bitcast.66), kind=kOutput, calls=%fused_computation.68 | convolution fusion | flops 2550136832 | bytes 13303808 | tf_op jit(solution)/shard_map/dot_general | solution.py:77
  210.8 60.9 %reduce-scatter.3.cloned.1.call-done = f32[128,256]{1,0:T(8,128)} async-done(((f32[2048,256]{1,0:T(8,128)}), f32[128,256]{1,0:T(8,128)}) %reduce-scatter.3.cloned.1.call-update) | async-done | bytes 131088 | tf_op jit(solution)/shard_map/reduce_scatter | solution.py:80
  271.7 10.3 %all-reduce.3 = bf16[128,256]{1,0:T(8,128)(2,1)S(1)} all-reduce(f32[128,256]{1,0:T(8,128)} %reduce-scatter.3.cloned.1.call-done), channel_id=1, replica_groups=mesh['dp'=16,'vocab'=2] {'vocab'}, use_global_device_ids=true, to_apply=%region_6.7 | all-reduce | flops 32768 | bytes 196608 | tf_op jit(solution)/shard_map/psum | solution.py:81
  282.0 3.9 %fusion.15 = f32[256,4096]{1,0:T(8,128)} fusion(bf16[128,256]{1,0:T(8,128)(2,1)S(1)} %all-reduce.3, bf16[128,4096]{1,0:T(8,128)(2,1)} %param.8), kind=kOutput, calls=%fused_computation.69 | convolution fusion | flops 268435456 | bytes 5308416 | tf_op jit(solution)/shard_map/dot_general | solution.py:84
  286.1 0.8 gather_fusion
  287.0 10.4 %all_to_all.24 = bf16[16,8,256]{2,1,0:T(8,128)(2,1)S(1)} all-to-all(bf16[16,8,256]{2,1,0:T(8,128)(2,1)S(1)} %bitcast_select_fusion), channel_id=1, replica_groups=mesh['dp'=16,'vocab'=2] {'dp'}, dimensions={0} | all-to-all | bytes 131072 | tf_op jit(solution)/shard_map/all_to_all | solution.py:92
  297.4 1.4 convolution_convert_fusion
  298.8 58.4 %reduce-scatter.5.cloned.1.call-done = f32[16,4096]{1,0:T(8,128)} async-done(((f32[256,4096]{1,0:T(8,128)}), f32[16,4096]{1,0:T(8,128)}) %reduce-scatter.5.cloned.1.call-update) | async-done | bytes 262160 | tf_op jit(solution)/shard_map/reduce_scatter | solution.py:83
  (33 shorter events, 3.6 us)
Async XLA Ops:
  7.2 1.6 copy-start
  7.2 75.8 %all-gather.2.cloned.1.call-start = ((), (), s32[]{:S(2)}) async-start(), calls=%async_computation.4 | async-start | bytes 3342336 | tf_op jit(solution)/shard_map/all_gather | solution.py:44
  27.1 60.8 %all-to-all-start = ((bf16[16,16,2432]{2,0,1:T(8,128)(2,1)}), bf16[16,16,2432]{2,0,1:T(8,128)(2,1)S(1)}, u32[]{:S(2)}, u32[]{:S(2)}) async-start(bf16[16,16,2432]{2,0,1:T(8,128)(2,1)} %bitcast.67), calls=%async_computation | async-start | bytes 2490368 | tf_op jit(solution)/shard_map/all_to_all | solution.py:45
  32.8 238.9 %reduce-scatter.3.cloned.1.call-start = ((), (), s32[]{:S(2)}) async-start(), calls=%async_computation.5 | async-start | bytes 2228224 | tf_op jit(solution)/shard_map/reduce_scatter | solution.py:80
  210.7 75.2 %copy-start.1 = (s32[128]{0:T(128)S(1)}, s32[128]{0:T(128)}, u32[]{:S(2)}) copy-start(s32[128]{0:T(128)} %param.15) | copy-start | bytes 1540
  210.7 146.5 %reduce-scatter.5.cloned.1.call-start = ((), (), s32[]{:S(2)}) async-start(), calls=%async_computation.6 | async-start | bytes 4456448 | tf_op jit(solution)/shard_map/reduce_scatter | solution.py:83
Sparse Core Ops, SparseCore 0:
  24.8 58.1 all-gather.1
  210.8 60.7 reduce-scatter.2
  286.0 71.0 reduce-scatter.4

commit v3 on v1

v3 whole, which is shorter than its diff:
```python
import jax
import jax.numpy as jnp
from jax import lax
from jax.sharding import PartitionSpec as P

PREFIX_MAX = 4096
TILE = 128
WORD_BITS = 30
CHUNKS = 4


far_below = -1e30


def chunk_count(tiles):
    for count in (CHUNKS, 2, 1):
        if tiles % count == 0:
            return count
    return 1


def body(hidden, rank_factor, vocab_factor, lengths, targets, cotangent, grammar, assign):
    row_count = hidden.shape[0]
    rank = rank_factor.shape[0]
    groups = lax.axis_size("dp")
    share = row_count // groups
    width = vocab_factor.shape[1]
    tiles = width // TILE
    chunks = chunk_count(tiles)
    chunk_cols = width // chunks
    chunk_tiles = tiles // chunks
    first = lax.axis_index("vocab") * width

    partial_latent = lax.dot_general(
        hidden, rank_factor, (((1,), (1,)), ((), ())), preferred_element_type=jnp.float32
    )
    latent = lax.psum(partial_latent, "vocab").astype(jnp.bfloat16)
    weight = cotangent.astype(jnp.float32) * lengths.astype(jnp.float32) / PREFIX_MAX
    target_local = targets - first
    row_words = jnp.repeat(grammar, row_count // grammar.shape[0], axis=0)

    peaks, sums, scores, hits = [], [], [], []
    for k in range(chunks):
        factor = lax.all_gather(
            vocab_factor[:, k * chunk_cols : (k + 1) * chunk_cols], "dp", axis=0, tiled=True
        )
        tile_ids = [k * chunk_tiles + t for t in range(chunk_tiles)]
        words = row_words[:, [t // WORD_BITS for t in tile_ids]]
        shifts = jnp.array([t % WORD_BITS for t in tile_ids], jnp.int32)
        bits = (jnp.right_shift(words, shifts[None, :]) & 1) == 1
        tile_on = jnp.broadcast_to(bits[:, :, None], (row_count, chunk_tiles, TILE)).reshape(
            row_count, chunk_cols
        )
        columns = k * chunk_cols + jnp.arange(chunk_cols, dtype=jnp.int32)
        target_hit = columns[None, :] == target_local[:, None]
        allowed = tile_on | target_hit
        logits = jnp.dot(latent, factor, preferred_element_type=jnp.float32)
        masked = jnp.where(allowed, logits, far_below)
        chunk_peak = jnp.max(masked, axis=1)
        powers = jnp.where(allowed, jnp.exp(masked - chunk_peak[:, None]), 0.0)
        peaks.append(chunk_peak)
        sums.append(jnp.sum(powers, axis=1))
        scores.append(
            lax.dot_general(
                powers.astype(jnp.bfloat16), factor, (((1,), (1,)), ((), ())),
                preferred_element_type=jnp.float32,
            )
        )
        hits.append(
            lax.dot_general(
                target_hit.astype(jnp.bfloat16), factor, (((1,), (1,)), ((), ())),
                preferred_element_type=jnp.float32,
            )
        )

    chunk_peaks = jnp.stack(peaks)
    peak = lax.pmax(jnp.max(chunk_peaks, axis=0), "vocab")
    scales = jnp.exp(chunk_peaks - peak[None, :])
    total = lax.psum(jnp.sum(jnp.stack(sums) * scales, axis=0), "vocab")
    expected = sum(scales[k][:, None] * scores[k] for k in range(chunks))
    target_rows = sum(hits)
    rank_partial = (weight / total)[:, None] * expected - weight[:, None] * target_rows
    rank_grad = lax.psum(rank_partial, "vocab").astype(jnp.bfloat16)

    grad_factor = lax.psum_scatter(
        lax.dot_general(
            rank_grad, hidden, (((0,), (0,)), ((), ())), preferred_element_type=jnp.float32
        ),
        "dp",
        scatter_dimension=0,
        tiled=True,
    )
    picked = jnp.take(rank_grad, assign, axis=0).reshape(groups, share, rank)
    slot_rank = lax.all_to_all(picked, "dp", split_axis=0, concat_axis=0, tiled=True).reshape(
        row_count, rank
    )
    grad_hidden = jnp.dot(slot_rank, rank_factor, preferred_element_type=jnp.float32).astype(
        jnp.bfloat16
    )
    return (grad_hidden, grad_factor)


def solution(mesh):
    return jax.shard_map(
        body,
        mesh=mesh,
        in_specs=(
            P("dp", "vocab"),
            P(None, "vocab"),
            P("dp", "vocab"),
            P("dp"),
            P("dp"),
            P("dp"),
            P("dp", "vocab"),
            P("dp"),
        ),
        out_specs=(P("dp", "vocab"), P("dp", "vocab")),
        check_vma=False,
    )
```

time: 365 us -> 381 us (1.044)
  blocking collectives: 166 us -> 41.9 us
  waiting for transfers between devices: 116 us -> 236 us
  matrix products: 23.1 us -> 57.2 us
  other arithmetic: 27.6 us -> 13.4 us
  starting transfers between devices: 7.48 us -> 0.19 us
  local copies, waits for them, and re-layouts: 10.6 us -> 17.8 us
    all_gather x1 -> x4, waiting for transfers between devices: 0.01 us -> 175 us  [body(): lax.all_gather(vocab_factor[:, k * chunk_cols:(k + 1) * chunk_cols], 'dp'...]
    all_gather x4 -> x0, blocking collectives: 135 us -> none  [the longest x1 69 us: body(): lax.all_gather(jnp.stack([local_peak, local_total]), ('dp', 'vocab'), axi...]
    reduce_scatter x1 -> x0, waiting for transfers between devices: 57.5 us -> none  [body(): lax.psum_scatter(rank_partial, 'dp', scatter_dimension=0, tiled=True)]
    dot_general x2 -> x12, matrix products: 15.7 us -> 49.8 us  [the longest x4 26.1 us: body(): logits = jnp.dot(latent, factor, preferred_element_type=jnp.float32)]
    convert_element_type x1 -> x0, other arithmetic: 14.6 us -> none  [body(): (weight_all[:, None] * (row_probs - target_hit.astype(jnp.float32))).asty...]
    reshape x0 -> x5, local copies, waits for them, and re-layouts: none -> 8.71 us  [the longest x4 8.63 us: body(): jnp.broadcast_to(bits[:, :, None], (row_count, chunk_tiles, TILE))]
    all_to_all x1 -> x0, starting transfers between devices: 7.36 us -> none  [body(): lax.all_to_all(vocab_factor, 'dp', split_axis=1, concat_axis=0, tiled=True)]
    psum x1 -> x2, blocking collectives: 10.4 us -> 15.7 us  [the longest x1 10.5 us: body(): rank_grad = lax.psum(rank_partial, 'vocab').astype(jnp.bfloat16)]
  transfers between devices with their start and end apart: 4 -> 5, of which waited for: 2 -> 5; matrix products, arithmetic and copies ran while one was open for 4% -> 10% of each run, Pallas kernels for 0% -> 0%
where the time goes in v3:
time: 381 us; the launch traced here: 380 us
  waiting for transfers between devices  236 us (62%)
  matrix products  57.2 us (15%)
  blocking collectives  41.9 us (11%)
  local copies, waits for them, and re-layouts  17.8 us (5%)
  between operations  14.4 us (4%)
  other arithmetic  13.4 us (4%)
    all_gather x4, waiting for transfers between devices, body(): lax.all_gather(vocab_factor[:, k * chunk_cols:(k + 1) * chunk_cols], 'dp'...  175 us
    reduce_scatter x1, waiting for transfers between devices, body(): lax.psum_scatter(lax.dot_general(rank_grad, hidden, (((0,), (0,)), ((), (...  58.6 us
    dot_general x4, matrix products, body(): logits = jnp.dot(latent, factor, preferred_element_type=jnp.float32)  26.1 us
    dot_general x4, matrix products, body(): lax.dot_general(target_hit.astype(jnp.bfloat16), factor, (((1,), (1,)), (...  12.8 us
    reduce_sum x1, other arithmetic, body(): sums.append(jnp.sum(powers, axis=1))  11.5 us
    psum x1, blocking collectives, body(): latent = lax.psum(partial_latent, 'vocab').astype(jnp.bfloat16)  11.4 us
    dot_general x4, matrix products, body(): lax.dot_general(powers.astype(jnp.bfloat16), factor, (((1,), (1,)), ((),...  10.9 us
    psum x1, blocking collectives, body(): rank_grad = lax.psum(rank_partial, 'vocab').astype(jnp.bfloat16)  10.5 us
  transfers between devices with their start and end apart: 5, of which 5 were waited for; matrix products, arithmetic and copies ran while one was open for 10% of the time, Pallas kernels for 0%

profile of v3, /device:TPU:0, one launch (start us, length us, event | category | flops | bytes accessed | tf_op | source)
XLA Modules:
  0.0 380.5 jit_solution(4000046896999420409)
XLA Ops:
  7.2 2.4 fusion.84
  19.6 2.4 copy.26
  23.1 2.5 copy.25
  26.6 2.4 copy.24
  29.0 11.4 %all-reduce.2 = bf16[128,256]{1,0:T(8,128)(2,1)S(1)} all-reduce(f32[128,256]{1,0:T(8,128)S(1)} %fusion.89), channel_id=1, replica_groups=mesh['dp'=16,'vocab'=2] {'vocab'}, use_global_device_ids=true, to_apply=%region_0.0 | all-reduce | flops 32768 | bytes 196608 | tf_op jit(solution)/shard_map/psum | solution.py:37
  40.4 27.9 %all-gather.5.cloned.1.call-done = bf16[256,9728]{1,0:T(8,128)(2,1)} async-done(((bf16[16,9728]{1,0:T(8,128)(2,1)}), bf16[256,9728]{1,0:T(8,128)(2,1)}) %all-gather.5.cloned.1.call-update) | async-done | bytes 4980752 | tf_op jit(solution)/shard_map/all_gather | solution.py:44
  68.4 6.7 %fusion.85 = (f32[128]{0:T(128)S(1)}, f32[128,9728]{1,0:T(8,128)}) fusion(bf16[128,256]{1,0:T(8,128)(2,1)S(1)} %all-reduce.2, bf16[256,9728]{1,0:T(8,128)(2,1)} %all-gather.5.cloned.1.call-done, pred[128,9728]{1,0:T(32,128)(4,1)} %copy.24, s32[128]{0:T(128)S(1)} %broadcast_subtract_fusion), kind=kOutput, calls=%fused_computation.103 | convolution fusion | flops 642514816 | bytes 11273216 | tf_op jit(solution)/shard_map/dot_general | solution.py:57
  75.1 48.9 %all-gather.11.cloned.1.call-done = bf16[256,9728]{1,0:T(8,128)(2,1)} async-done(((bf16[16,9728]{1,0:T(8,128)(2,1)}), bf16[256,9728]{1,0:T(8,128)(2,1)}) %all-gather.11.cloned.1.call-update) | async-done | bytes 4980752 | tf_op jit(solution)/shard_map/all_gather | solution.py:44
  124.0 6.2 %fusion.86 = (f32[128]{0:T(128)S(1)}, f32[128,9728]{1,0:T(8,128)}) fusion(bf16[128,256]{1,0:T(8,128)(2,1)S(1)} %all-reduce.2, bf16[256,9728]{1,0:T(8,128)(2,1)} %all-gather.11.cloned.1.call-done, pred[128,9728]{1,0:T(32,128)(4,1)S(1)} %copy.27, s32[128]{0:T(128)S(1)} %broadcast_subtract_fusion, s32[9728]{0:T(1024)S(1)} %get-tuple-element.26), kind=kOutput, calls=%fused_computation.104 | convolution fusion | flops 642514816 | bytes 11312128 | tf_op jit(solution)/shard_map/dot_general | solution.py:57
  130.2 49.4 %all-gather.9.cloned.1.call-done = bf16[256,9728]{1,0:T(8,128)(2,1)} async-done(((bf16[16,9728]{1,0:T(8,128)(2,1)}), bf16[256,9728]{1,0:T(8,128)(2,1)}) %all-gather.9.cloned.1.call-update) | async-done | bytes 4980752 | tf_op jit(solution)/shard_map/all_gather | solution.py:44
  179.6 6.6 %fusion.87 = (f32[128]{0:T(128)S(1)}, f32[128,9728]{1,0:T(8,128)}) fusion(bf16[128,256]{1,0:T(8,128)(2,1)S(1)} %all-reduce.2, bf16[256,9728]{1,0:T(8,128)(2,1)} %all-gather.9.cloned.1.call-done, pred[128,9728]{1,0:T(32,128)(4,1)} %copy.26, s32[128]{0:T(128)S(1)} %broadcast_subtract_fusion, s32[9728]{0:T(1024)S(1)} %get-tuple-element.27), kind=kOutput, calls=%fused_computation.105 | convolution fusion | flops 642514816 | bytes 11312128 | tf_op jit(solution)/shard_map/dot_general | solution.py:57
  186.2 48.9 %all-gather.7.cloned.1.call-done = bf16[256,9728]{1,0:T(8,128)(2,1)} async-done(((bf16[16,9728]{1,0:T(8,128)(2,1)}), bf16[256,9728]{1,0:T(8,128)(2,1)}) %all-gather.7.cloned.1.call-update) | async-done | bytes 4980752 | tf_op jit(solution)/shard_map/all_gather | solution.py:44
  235.1 6.6 %fusion.88 = (f32[128]{0:T(128)S(1)}, f32[128,9728]{1,0:T(8,128)}) fusion(bf16[128,256]{1,0:T(8,128)(2,1)S(1)} %all-reduce.2, bf16[256,9728]{1,0:T(8,128)(2,1)} %all-gather.7.cloned.1.call-done, pred[128,9728]{1,0:T(32,128)(4,1)} %copy.25, s32[128]{0:T(128)S(1)} %broadcast_subtract_fusion, s32[9728]{0:T(1024)S(1)} %iota_add_fusion.2), kind=kOutput, calls=%fused_computation.106 | convolution fusion | flops 642514816 | bytes 11312128 | tf_op jit(solution)/shard_map/dot_general | solution.py:57
  241.7 4.9 %pmax.7 = f32[128]{0:T(128)S(1)} all-reduce(f32[128]{0:T(128)S(1)} %maximum_maximum_fusion), channel_id=1, replica_groups=mesh['dp'=16,'vocab'=2] {'vocab'}, use_global_device_ids=true, to_apply=%region_9.10 | all-reduce | flops 128 | bytes 1024 | tf_op jit(solution)/shard_map/pmax | solution.py:77
  246.7 11.5 %fusion.9 = (f32[128]{0:T(128)S(1)}, f32[128]{0:T(128)S(1)}, f32[128]{0:T(128)S(1)}, f32[128]{0:T(128)S(1)}) fusion(f32[128,9728]{1,0:T(8,128)} %get-tuple-element.19, f32[128]{0:T(128)S(1)} %get-tuple-element.18, pred[128,9728]{1,0:T(32,128)(4,1)} %copy.24, s32[128]{0:T(128)S(1)} %broadcast_subtract_fusion, f32[128,9728]{1,0:T(8,128)} %get-tuple-element.21, ...), kind=kLoop, calls=%fused_computation.27 | loop fusion | flops 24903168 | bytes 25025024 | tf_op jit(solution)/shard_map/reduce_sum | solution.py:62
  258.2 5.2 %psum.22 = f32[128]{0:T(128)S(1)} all-reduce(f32[128]{0:T(128)S(1)} %get-tuple-element.8), channel_id=1, replica_groups=mesh['dp'=16,'vocab'=2] {'vocab'}, use_global_device_ids=true, to_apply=%region_11.12 | all-reduce | flops 128 | bytes 1024 | tf_op jit(solution)/shard_map/psum | solution.py:79
  263.4 4.3 %fusion = f32[128,256]{1,0:T(8,128)S(1)} fusion(bf16[256,9728]{1,0:T(8,128)(2,1)} %all-gather.11.cloned.1.call-done, s32[9728]{0:T(1024)S(1)} %get-tuple-element.26, s32[128]{0:T(128)S(1)} %broadcast_subtract_fusion), kind=kOutput, calls=%fused_computation.9 | convolution fusion | flops 638779392 | bytes 5151232 | tf_op jit(solution)/shard_map/dot_general | solution.py:70
  267.8 4.3 %fusion.2 = f32[128,256]{1,0:T(8,128)S(1)} fusion(bf16[256,9728]{1,0:T(8,128)(2,1)} %all-gather.9.cloned.1.call-done, s32[9728]{0:T(1024)S(1)} %get-tuple-element.27, s32[128]{0:T(128)S(1)} %broadcast_subtract_fusion), kind=kOutput, calls=%fused_computation.12 | convolution fusion | flops 638779392 | bytes 5151232 | tf_op jit(solution)/shard_map/dot_general | solution.py:70
  272.1 2.4 fusion.4
  279.4 4.9 %fusion.45 = f32[128,256]{1,0:T(8,128)S(1)} fusion(f32[128,256]{1,0:T(8,128)S(1)} %fusion.51, f32[128,256]{1,0:T(8,128)} %fusion.48, bf16[256,9728]{1,0:T(8,128)(2,1)} %all-gather.5.cloned.1.call-done, f32[128,9728]{1,0:T(8,128)S(1)} %bitcast.63, f32[128]{0:T(128)S(1)} %get-tuple-element.18, f32[128]{0:T(128)S(1)} %get-tuple-element.17, ...), kind=kOutput, calls=%fused_computation.55 | convolution fusion | flops 643858432 | bytes 11601408 | tf_op jit(solution)/shard_map/dot_general | solution.py:64
  288.4 10.5 %all-reduce.3 = bf16[128,256]{1,0:T(8,128)(2,1)S(1)} all-reduce(f32[128,256]{1,0:T(8,128)} %fusion.63), channel_id=1, replica_groups=mesh['dp'=16,'vocab'=2] {'vocab'}, use_global_device_ids=true, to_apply=%region_12.13 | all-reduce | flops 32768 | bytes 196608 | tf_op jit(solution)/shard_map/psum | solution.py:83
  298.9 3.9 %fusion.90 = f32[256,4096]{1,0:T(8,128)} fusion(bf16[128,256]{1,0:T(8,128)(2,1)S(1)} %all-reduce.3, bf16[128,4096]{1,0:T(8,128)(2,1)} %param.16), kind=kOutput, calls=%fused_computation.108 | convolution fusion | flops 268435456 | bytes 5308416 | tf_op jit(solution)/shard_map/dot_general | solution.py:86
  304.0 10.0 %all_to_all.5 = bf16[16,8,256]{2,1,0:T(8,128)(2,1)S(1)} all-to-all(bf16[16,8,256]{2,1,0:T(8,128)(2,1)S(1)} %bitcast_select_fusion), channel_id=1, replica_groups=mesh['dp'=16,'vocab'=2] {'dp'}, dimensions={0} | all-to-all | bytes 131072 | tf_op jit(solution)/shard_map/all_to_all | solution.py:94
  315.3 58.6 %reduce-scatter.2.cloned.1.call-done = f32[16,4096]{1,0:T(8,128)} async-done(((f32[256,4096]{1,0:T(8,128)}), f32[16,4096]{1,0:T(8,128)}) %reduce-scatter.2.cloned.1.call-update) | async-done | bytes 262160 | tf_op jit(solution)/shard_map/reduce_scatter | solution.py:85
  (116 shorter events, 23.3 us)
Async XLA Ops:
  7.2 9.3 %copy-start = (bf16[256,4096]{1,0:T(8,128)(2,1)S(1)}, bf16[256,4096]{1,0:T(8,128)(2,1)}, u32[]{:S(2)}) copy-start(bf16[256,4096]{1,0:T(8,128)(2,1)} %param.17) | copy-start | bytes 6291460
  7.2 61.2 %all-gather.5.cloned.1.call-start = ((), (), s32[]{:S(2)}) async-start(), calls=%async_computation.2 | async-start | bytes 5292032 | tf_op jit(solution)/shard_map/all_gather | solution.py:44
  9.7 8.9 %copy-start.12 = (s32[76]{0:T(128)S(1)}, s32[76]{0:T(128)}, u32[]{:S(2)}) copy-start(s32[76]{0:T(128)} %constant.85) | copy-start | bytes 916
  9.7 9.5 %copy-start.7 = (s32[76]{0:T(128)S(1)}, s32[76]{0:T(128)}, u32[]{:S(2)}) copy-start(s32[76]{0:T(128)} %constant.63.clone) | copy-start | bytes 916
  9.7 114.3 %all-gather.11.cloned.1.call-start = ((), (), s32[]{:S(2)}) async-start(), calls=%async_computation.5 | async-start | bytes 5292032 | tf_op jit(solution)/shard_map/all_gather | solution.py:44
  10.4 169.2 %all-gather.9.cloned.1.call-start = ((), (), s32[]{:S(2)}) async-start(), calls=%async_computation.4 | async-start | bytes 5292032 | tf_op jit(solution)/shard_map/all_gather | solution.py:44
  11.2 223.9 %all-gather.7.cloned.1.call-start = ((), (), s32[]{:S(2)}) async-start(), calls=%async_computation.3 | async-start | bytes 5292032 | tf_op jit(solution)/shard_map/all_gather | solution.py:44
  11.7 362.2 %reduce-scatter.2.cloned.1.call-start = ((), (), s32[]{:S(2)}) async-start(), calls=%async_computation.6 | async-start | bytes 4456448 | tf_op jit(solution)/shard_map/reduce_scatter | solution.py:85
  15.1 7.0 %copy-start.11 = (s32[76]{0:T(128)S(1)}, s32[76]{0:T(128)}, u32[]{:S(2)}) copy-start(s32[76]{0:T(128)} %constant.84) | copy-start | bytes 916
  15.1 7.6 %copy-start.6 = (s32[76]{0:T(128)S(1)}, s32[76]{0:T(128)}, u32[]{:S(2)}) copy-start(s32[76]{0:T(128)} %constant.61.clone) | copy-start | bytes 916
  18.6 7.0 %copy-start.10 = (s32[76]{0:T(128)S(1)}, s32[76]{0:T(128)}, u32[]{:S(2)}) copy-start(s32[76]{0:T(128)} %constant.83) | copy-start | bytes 916
  18.6 7.6 %copy-start.5 = (s32[76]{0:T(128)S(1)}, s32[76]{0:T(128)}, u32[]{:S(2)}) copy-start(s32[76]{0:T(128)} %constant.59.clone) | copy-start | bytes 916
  22.1 18.3 %copy-start.13 = (s32[128]{0:T(128)S(1)}, s32[128]{0:T(128)}, u32[]{:S(2)}) copy-start(s32[128]{0:T(128)} %param.20) | copy-start | bytes 1540
  246.7 16.7 %copy-start.8 = (s32[128]{0:T(128)S(1)}, s32[128]{0:T(128)}, u32[]{:S(2)}) copy-start(s32[128]{0:T(128)} %param.19) | copy-start | bytes 1540
  246.7 16.7 %copy-start.9 = (bf16[128]{0:T(256)(128)(2,1)S(1)}, bf16[128]{0:T(256)(128)(2,1)}, u32[]{:S(2)}) copy-start(bf16[128]{0:T(256)(128)(2,1)} %param.21) | copy-start | bytes 772
  263.4 8.7 %copy-start.4 = (bf16[256,9728]{1,0:T(8,128)(2,1)S(1)}, bf16[256,9728]{1,0:T(8,128)(2,1)}, u32[]{:S(2)}) copy-start(bf16[256,9728]{1,0:T(8,128)(2,1)} %all-gather.7.cloned.1.call-done) | copy-start | bytes 14942212
  263.4 11.1 %slice-start.4 = ((s8[4980736]{0:T(1024)(128)(4,1)}), s8[4194304]{0:T(1024)(128)(4,1)S(1)}, s32[]{:S(2)}) async-start(s8[4980736]{0:T(1024)(128)(4,1)} %bitcast.60), calls=%async_computation.11 | async-start | bytes 8388608
  267.7 6.8 %slice-start.5 = ((s8[4980736]{0:T(1024)(128)(4,1)}), s8[786432]{0:T(1024)(128)(4,1)S(1)}, s32[]{:S(2)}) async-start(s8[4980736]{0:T(1024)(128)(4,1)} %bitcast.60), calls=%async_computation.12 | async-start | bytes 1572864
  267.8 6.8 %copy-start.3 = (pred[128,9728]{1,0:T(32,128)(4,1)S(1)}, pred[128,9728]{1,0:T(32,128)(4,1)}, u32[]{:S(2)}) copy-start(pred[128,9728]{1,0:T(32,128)(4,1)} %copy.25) | copy-start | bytes 3735556
  274.6 9.8 %slice-start.12 = ((s8[4980736]{0:T(1024)(128)(4,1)}), s8[786432]{0:T(1024)(128)(4,1)S(1)}, s32[]{:S(2)}) async-start(s8[4980736]{0:T(1024)(128)(4,1)} %bitcast.68), calls=%async_computation.19 | async-start | bytes 1572864
  276.8 7.5 %slice-start.13 = ((s8[4980736]{0:T(1024)(128)(4,1)}), s8[4194304]{0:T(1024)(128)(4,1)S(1)}, s32[]{:S(2)}) async-start(s8[4980736]{0:T(1024)(128)(4,1)} %bitcast.68), calls=%async_computation.20 | async-start | bytes 8388608
  276.9 9.3 %slice-start = ((s8[4980736]{0:T(1024)(128)(4,1)}), s8[4194304]{0:T(1024)(128)(4,1)S(1)}, s32[]{:S(2)}) async-start(s8[4980736]{0:T(1024)(128)(4,1)} %bitcast.56), calls=%async_computation.7 | async-start | bytes 8388608
  276.9 9.3 %slice-start.8 = ((s8[4980736]{0:T(1024)(128)(4,1)}), s8[786432]{0:T(1024)(128)(4,1)S(1)}, s32[]{:S(2)}) async-start(s8[4980736]{0:T(1024)(128)(4,1)} %bitcast.64), calls=%async_computation.15 | async-start | bytes 1572864
  288.4 14.5 %copy-start.14 = (s32[128]{0:T(128)S(1)}, s32[128]{0:T(128)}, u32[]{:S(2)}) copy-start(s32[128]{0:T(128)} %param.23) | copy-start | bytes 1540
  (11 other events, 43.7 us)
Sparse Core Ops, SparseCore 0:
  10.9 57.4 all-gather.4
  70.7 53.3 all-gather.10
  126.3 53.2 all-gather.8
  181.8 53.2 all-gather.6
  303.0 70.9 reduce-scatter.1

commit v4 on v1

v4 whole, which is shorter than its diff:
```python
import jax
import jax.numpy as jnp
from jax import lax
from jax.sharding import PartitionSpec as P

PREFIX_MAX = 4096


far_below = -1e30


def body(hidden, rank_factor, vocab_factor, lengths, targets, cotangent, grammar, assign):
    row_count = hidden.shape[0]
    rank = rank_factor.shape[0]
    groups = lax.axis_size("dp")
    share = row_count // groups
    width = vocab_factor.shape[1]
    tiles = width // 128
    first = lax.axis_index("vocab") * width
    factor = lax.all_gather(vocab_factor, "dp", axis=0, tiled=True)
    row_words = jnp.repeat(grammar, row_count // grammar.shape[0], axis=0)
    weight = cotangent.astype(jnp.float32) * lengths.astype(jnp.float32) / PREFIX_MAX

    partial_latent = lax.dot_general(
        hidden, rank_factor, (((1,), (1,)), ((), ())), preferred_element_type=jnp.float32
    )
    latent = lax.psum(partial_latent, "vocab").astype(jnp.bfloat16)
    target_local = targets - first
    columns = jnp.arange(width, dtype=jnp.int32)
    shifts = jnp.arange(30, dtype=jnp.int32)

    logits = jnp.dot(latent, factor, preferred_element_type=jnp.float32)
    bits = jnp.right_shift(row_words[:, :, None], shifts) & 1
    bits = bits.reshape(row_count, -1)[:, :tiles]
    tile_on = jnp.broadcast_to((bits == 1)[:, :, None], (row_count, tiles, 128)).reshape(
        row_count, width
    )
    target_hit = columns[None, :] == target_local[:, None]
    allowed = tile_on | target_hit
    masked = jnp.where(allowed, logits, far_below)
    peak = lax.pmax(jnp.max(masked, axis=1), "vocab")
    powers = jnp.where(allowed, jnp.exp(masked - peak[:, None]), 0.0)
    total = lax.psum(jnp.sum(powers, axis=1), "vocab")
    row_probs = powers / total[:, None]
    score_grad = (weight[:, None] * (row_probs - target_hit.astype(jnp.float32))).astype(
        jnp.bfloat16
    )
    rank_partial = lax.dot_general(
        score_grad, factor, (((1,), (1,)), ((), ())), preferred_element_type=jnp.float32
    )
    rank_grad = lax.psum(rank_partial, "vocab").astype(jnp.bfloat16)

    grad_factor = lax.psum_scatter(
        lax.dot_general(
            rank_grad, hidden, (((0,), (0,)), ((), ())), preferred_element_type=jnp.float32
        ),
        "dp",
        scatter_dimension=0,
        tiled=True,
    )
    picked = jnp.take(rank_grad, assign, axis=0).reshape(groups, share, rank)
    slot_rank = lax.all_to_all(picked, "dp", split_axis=0, concat_axis=0, tiled=True).reshape(
        row_count, rank
    )
    grad_hidden = jnp.dot(slot_rank, rank_factor, preferred_element_type=jnp.float32).astype(
        jnp.bfloat16
    )
    return (grad_hidden, grad_factor)


def solution(mesh):
    return jax.shard_map(
        body,
        mesh=mesh,
        in_specs=(
            P("dp", "vocab"),
            P(None, "vocab"),
            P("dp", "vocab"),
            P("dp"),
            P("dp"),
            P("dp"),
            P("dp", "vocab"),
            P("dp"),
        ),
        out_specs=(P("dp", "vocab"), P("dp", "vocab")),
        check_vma=False,
    )
```

time: 365 us -> 273 us (0.75)
  blocking collectives: 166 us -> 42.4 us
  waiting for transfers between devices: 116 us -> 151 us
  matrix products: 23.1 us -> 42.4 us
  other arithmetic: 27.6 us -> 14.3 us
  starting transfers between devices: 7.48 us -> 0.08 us
    all_gather x4 -> x0, blocking collectives: 135 us -> none  [the longest x1 69 us: body(): lax.all_gather(jnp.stack([local_peak, local_total]), ('dp', 'vocab'), axi...]
    all_gather x1, waiting for transfers between devices: 0.01 us -> 92.1 us  [body(): factor = lax.all_gather(vocab_factor, 'dp', axis=0, tiled=True)]
    reduce_scatter x1 -> x0, waiting for transfers between devices: 57.5 us -> none  [body(): lax.psum_scatter(rank_partial, 'dp', scatter_dimension=0, tiled=True)]
    convert_element_type x1 -> x0, other arithmetic: 14.6 us -> none  [body(): (weight_all[:, None] * (row_probs - target_hit.astype(jnp.float32))).asty...]
    dot_general x1, matrix products: 7.65 us -> 18.3 us  [body(): logits = jnp.dot(latent, factor, preferred_element_type=jnp.float32)]
    dot_general x1, matrix products: 8.07 us -> 17.9 us  [body(): lax.dot_general(score_grad, factor, (((1,), (1,)), ((), ())), preferred_e...]
    all_to_all x1 -> x0, starting transfers between devices: 7.36 us -> none  [body(): lax.all_to_all(vocab_factor, 'dp', split_axis=1, concat_axis=0, tiled=True)]
    broadcast_in_dim x0 -> x2, local copies, waits for them, and re-layouts: none -> 6.7 us  [the longest x1 6.63 us: body(): jnp.broadcast_to((bits == 1)[:, :, None], (row_count, tiles, 128))]
  transfers between devices with their start and end apart: 4 -> 2, of which waited for: 2 -> 2; matrix products, arithmetic and copies ran while one was open for 4% -> 3% of each run, Pallas kernels for 0% -> 0%
where the time goes in v4:
time: 273 us
  waiting for transfers between devices  151 us (55%)
  matrix products  42.4 us (16%)
  blocking collectives  42.4 us (16%)
  other arithmetic  14.3 us (5%)
  between operations  14.2 us (5%)
  local copies, waits for them, and re-layouts  8.79 us (3%)
    all_gather x1, waiting for transfers between devices, body(): factor = lax.all_gather(vocab_factor, 'dp', axis=0, tiled=True)  92.1 us
    reduce_scatter x1, waiting for transfers between devices, body(): lax.psum_scatter(lax.dot_general(rank_grad, hidden, (((0,), (0,)), ((), (...  58.2 us
    dot_general x1, matrix products, body(): logits = jnp.dot(latent, factor, preferred_element_type=jnp.float32)  18.3 us
    dot_general x1, matrix products, body(): lax.dot_general(score_grad, factor, (((1,), (1,)), ((), ())), preferred_e...  17.9 us
    reduce_sum x1, other arithmetic, body(): total = lax.psum(jnp.sum(powers, axis=1), 'vocab')  12.7 us
    psum x1, blocking collectives, body(): latent = lax.psum(partial_latent, 'vocab').astype(jnp.bfloat16)  11.4 us
    all_to_all x1, blocking collectives, body(): lax.all_to_all(picked, 'dp', split_axis=0, concat_axis=0, tiled=True)  11.4 us
    psum x1, blocking collectives, body(): rank_grad = lax.psum(rank_partial, 'vocab').astype(jnp.bfloat16)  9.71 us
  transfers between devices with their start and end apart: 2, of which 2 were waited for; matrix products, arithmetic and copies ran while one was open for 3% of the time, Pallas kernels for 0%

profile of v4, /device:TPU:0, one launch (start us, length us, event | category | flops | bytes accessed | tf_op | source)
XLA Modules:
  0.0 273.1 jit_solution(14418873737113928574)
XLA Ops:
  7.2 0.7 all-gather.2.cloned.1.call-update
  8.0 0.8 copy.10
  8.8 0.1 shift_right_arithmetic.22
  9.0 0.1 fusion.4
  9.2 0.2 copy.11
  9.3 2.1 fusion.10
  11.4 11.4 %all-reduce.2 = bf16[128,256]{1,0:T(8,128)(2,1)S(1)} all-reduce(f32[128,256]{1,0:T(8,128)S(1)} %fusion.10), channel_id=1, replica_groups=mesh['dp'=16,'vocab'=2] {'vocab'}, use_global_device_ids=true, to_apply=%region_0.0 | all-reduce | flops 32768 | bytes 196608 | tf_op jit(solution)/shard_map/psum | solution.py:27
  22.8 0.7 broadcast_subtract_fusion
  23.5 0.7 multiply_multiply_fusion
  24.2 92.1 %all-gather.2.cloned.1.call-done = bf16[256,38912]{1,0:T(8,128)(2,1)} async-done(((bf16[16,38912]{1,0:T(8,128)(2,1)}), bf16[256,38912]{1,0:T(8,128)(2,1)}) %all-gather.2.cloned.1.call-update) | async-done | bytes 19922960 | tf_op jit(solution)/shard_map/all_gather | solution.py:20
  116.2 6.6 %broadcast_in_dim.39 = pred[128,304,128]{2,1,0:T(8,128)(4,1)S(1)} broadcast(pred[128,304]{1,0:T(8,128)(4,1)S(1)} %copy.11), dimensions={0,1} | broadcast | bytes 5019648 | tf_op jit(solution)/shard_map/broadcast_in_dim | solution.py:35
  122.9 18.3 %fusion.9 = (f32[128]{0:T(128)S(1)}, f32[128,38912]{1,0:T(8,128)}) fusion(bf16[128,256]{1,0:T(8,128)(2,1)S(1)} %all-reduce.2, bf16[256,38912]{1,0:T(8,128)(2,1)} %all-gather.2.cloned.1.call-done, s32[128]{0:T(128)S(1)} %broadcast_subtract_fusion, pred[16,8,304,128]{3,2,1,0:T(8,128)(4,1)S(1)} %bitcast.28), kind=kOutput, calls=%fused_computation.21 | convolution fusion | flops 2570059776 | bytes 44893184 | tf_op jit(solution)/shard_map/dot_general | solution.py:32
  141.2 4.9 %pmax.7 = f32[128]{0:T(128)S(1)} all-reduce(f32[128]{0:T(128)S(1)} %get-tuple-element.2), channel_id=1, replica_groups=mesh['dp'=16,'vocab'=2] {'vocab'}, use_global_device_ids=true, to_apply=%region_2.3 | all-reduce | flops 128 | bytes 1024 | tf_op jit(solution)/shard_map/pmax | solution.py:41
  146.1 12.7 %fusion.1 = f32[128]{0:T(128)S(1)} fusion(f32[128,38912]{1,0:T(8,128)} %get-tuple-element.3, f32[128]{0:T(128)S(1)} %pmax.7, s32[128]{0:T(128)S(1)} %broadcast_subtract_fusion, pred[16,8,304,128]{3,2,1,0:T(8,128)(4,1)} %bitcast.29), kind=kLoop, calls=%fused_computation.6 | loop fusion | flops 24903552 | bytes 24905216 | tf_op jit(solution)/shard_map/reduce_sum | solution.py:43
  158.9 4.9 %psum.22 = f32[128]{0:T(128)S(1)} all-reduce(f32[128]{0:T(128)S(1)} %fusion.1), channel_id=1, replica_groups=mesh['dp'=16,'vocab'=2] {'vocab'}, use_global_device_ids=true, to_apply=%region_4.5 | all-reduce | flops 128 | bytes 1024 | tf_op jit(solution)/shard_map/psum | solution.py:43
  163.8 17.9 %fusion.2 = f32[128,256]{1,0:T(8,128)S(1)} fusion(bf16[256,38912]{1,0:T(8,128)(2,1)} %all-gather.2.cloned.1.call-done, f32[128,38912]{1,0:T(8,128)} %get-tuple-element.3, f32[128]{0:T(128)S(1)} %psum.22, f32[128]{0:T(128)S(1)} %pmax.7, s32[128]{0:T(128)S(1)} %broadcast_subtract_fusion, f32[128]{0:T(128)S(1)} %multiply_multiply_fusion, ...), kind=kOutput, calls=%fused_computation.7 | convolution fusion | flops 2594963456 | bytes 44959744 | tf_op jit(solution)/shard_map/dot_general | solution.py:48
  181.8 9.7 %all-reduce.3 = bf16[128,256]{1,0:T(8,128)(2,1)S(1)} all-reduce(f32[128,256]{1,0:T(8,128)S(1)} %fusion.2), channel_id=1, replica_groups=mesh['dp'=16,'vocab'=2] {'vocab'}, use_global_device_ids=true, to_apply=%region_5.6 | all-reduce | flops 32768 | bytes 196608 | tf_op jit(solution)/shard_map/psum | solution.py:51
  191.5 2.7 fusion.11
  194.2 0.1 broadcast_in_dim.36
  194.3 0.8 gather_fusion
  195.2 0.1 bitcast_select_fusion
  195.3 11.4 %all_to_all.5 = bf16[16,8,256]{2,1,0:T(8,128)(2,1)S(1)} all-to-all(bf16[16,8,256]{2,1,0:T(8,128)(2,1)S(1)} %bitcast_select_fusion), channel_id=1, replica_groups=mesh['dp'=16,'vocab'=2] {'dp'}, dimensions={0} | all-to-all | bytes 131072 | tf_op jit(solution)/shard_map/all_to_all | solution.py:62
  206.7 1.4 convolution_convert_fusion
  208.1 58.2 %reduce-scatter.2.cloned.1.call-done = f32[16,4096]{1,0:T(8,128)} async-done(((f32[256,4096]{1,0:T(8,128)}), f32[16,4096]{1,0:T(8,128)}) %reduce-scatter.2.cloned.1.call-update) | async-done | bytes 262160 | tf_op jit(solution)/shard_map/reduce_scatter | solution.py:53
  (19 shorter events, 0.3 us)
Async XLA Ops:
  7.2 2.2 copy-start
  7.2 109.1 %all-gather.2.cloned.1.call-start = ((), (), s32[]{:S(2)}) async-start(), calls=%async_computation.2 | async-start | bytes 21168128 | tf_op jit(solution)/shard_map/all_gather | solution.py:20
  7.9 258.4 %reduce-scatter.2.cloned.1.call-start = ((), (), s32[]{:S(2)}) async-start(), calls=%async_computation.3 | async-start | bytes 4456448 | tf_op jit(solution)/shard_map/reduce_scatter | solution.py:53
  122.9 18.3 %copy-start.1 = (pred[128,304,128]{2,1,0:T(8,128)(4,1)}, pred[128,304,128]{2,1,0:T(8,128)(4,1)S(1)}, u32[]{:S(2)}) copy-start(pred[128,304,128]{2,1,0:T(8,128)(4,1)S(1)} %broadcast_in_dim.39) | copy-start | bytes 14942212
  163.8 27.7 %copy-start.2 = (bf16[128,4096]{1,0:T(8,128)(2,1)S(1)}, bf16[128,4096]{1,0:T(8,128)(2,1)}, u32[]{:S(2)}) copy-start(bf16[128,4096]{1,0:T(8,128)(2,1)} %param.8) | copy-start | bytes 3145732
  163.8 30.4 %copy-start.3 = (s32[128]{0:T(128)S(1)}, s32[128]{0:T(128)}, u32[]{:S(2)}) copy-start(s32[128]{0:T(128)} %param.15) | copy-start | bytes 1540
Sparse Core Ops, SparseCore 0:
  9.6 106.5 all-gather.1
  194.3 71.9 reduce-scatter.1

commit v5 on v4

--- a/solution.py
+++ b/solution.py
@@ -53,11 +53,11 @@
     grad_factor = lax.psum_scatter(
         lax.dot_general(
             rank_grad, hidden, (((0,), (0,)), ((), ())), preferred_element_type=jnp.float32
-        ),
+        ).astype(jnp.bfloat16),
         "dp",
         scatter_dimension=0,
         tiled=True,
-    )
+    ).astype(jnp.float32)
     picked = jnp.take(rank_grad, assign, axis=0).reshape(groups, share, rank)
     slot_rank = lax.all_to_all(picked, "dp", split_axis=0, concat_axis=0, tiled=True).reshape(
         row_count, rank

time: 273 us -> 264 us (0.967)
  waiting for transfers between devices: 151 us -> 140 us
    reduce_scatter x1, waiting for transfers between devices: 58.2 us -> 47.4 us  [body(): lax.psum_scatter(lax.dot_general(rank_grad, hidden, (((0,), (0,)), ((), (...]
where the time goes in v5:
time: 264 us; the launch traced here: 263 us
  waiting for transfers between devices  140 us (53%)
  blocking collectives  42.4 us (16%)
  matrix products  41.8 us (16%)
  other arithmetic  15.9 us (6%)
  between operations  14.2 us (5%)
  local copies, waits for them, and re-layouts  8.79 us (3%)
    all_gather x1, waiting for transfers between devices, body(): factor = lax.all_gather(vocab_factor, 'dp', axis=0, tiled=True)  92 us
    reduce_scatter x1, waiting for transfers between devices, body(): lax.psum_scatter(lax.dot_general(rank_grad, hidden, (((0,), (0,)), ((), (...  47.4 us
    dot_general x1, matrix products, body(): logits = jnp.dot(latent, factor, preferred_element_type=jnp.float32)  18.3 us
    dot_general x1, matrix products, body(): lax.dot_general(score_grad, factor, (((1,), (1,)), ((), ())), preferred_e...  17.9 us
    reduce_sum x1, other arithmetic, body(): total = lax.psum(jnp.sum(powers, axis=1), 'vocab')  12.7 us
    psum x1, blocking collectives, body(): latent = lax.psum(partial_latent, 'vocab').astype(jnp.bfloat16)  11.4 us
    all_to_all x1, blocking collectives, body(): lax.all_to_all(picked, 'dp', split_axis=0, concat_axis=0, tiled=True)  11.4 us
    psum x1, blocking collectives, body(): rank_grad = lax.psum(rank_partial, 'vocab').astype(jnp.bfloat16)  9.72 us
  transfers between devices with their start and end apart: 2, of which 2 were waited for; matrix products, arithmetic and copies ran while one was open for 3% of the time, Pallas kernels for 0%

profile of v5, /device:TPU:0, one launch (start us, length us, event | category | flops | bytes accessed | tf_op | source)
XLA Modules:
  0.0 263.4 jit_solution(1974408419297866180)
XLA Ops:
  7.2 0.7 all-gather.2.cloned.1.call-update
  8.0 0.8 copy.10
  9.0 0.1 fusion.4
  9.2 0.2 copy.11
  9.3 2.1 fusion.10
  11.4 11.4 %all-reduce.2 = bf16[128,256]{1,0:T(8,128)(2,1)S(1)} all-reduce(f32[128,256]{1,0:T(8,128)S(1)} %fusion.10), channel_id=1, replica_groups=mesh['dp'=16,'vocab'=2] {'vocab'}, use_global_device_ids=true, to_apply=%region_0.0 | all-reduce | flops 32768 | bytes 196608 | tf_op jit(solution)/shard_map/psum | solution.py:27
  22.9 0.7 broadcast_subtract_fusion
  23.5 0.7 multiply_multiply_fusion
  24.2 92.0 %all-gather.2.cloned.1.call-done = bf16[256,38912]{1,0:T(8,128)(2,1)} async-done(((bf16[16,38912]{1,0:T(8,128)(2,1)}), bf16[256,38912]{1,0:T(8,128)(2,1)}) %all-gather.2.cloned.1.call-update) | async-done | bytes 19922960 | tf_op jit(solution)/shard_map/all_gather | solution.py:20
  116.2 6.6 %broadcast_in_dim.39 = pred[128,304,128]{2,1,0:T(8,128)(4,1)S(1)} broadcast(pred[128,304]{1,0:T(8,128)(4,1)S(1)} %copy.11), dimensions={0,1} | broadcast | bytes 5019648 | tf_op jit(solution)/shard_map/broadcast_in_dim | solution.py:35
  122.9 18.3 %fusion.9 = (f32[128]{0:T(128)S(1)}, f32[128,38912]{1,0:T(8,128)}) fusion(bf16[128,256]{1,0:T(8,128)(2,1)S(1)} %all-reduce.2, bf16[256,38912]{1,0:T(8,128)(2,1)} %all-gather.2.cloned.1.call-done, s32[128]{0:T(128)S(1)} %broadcast_subtract_fusion, pred[16,8,304,128]{3,2,1,0:T(8,128)(4,1)S(1)} %bitcast.28), kind=kOutput, calls=%fused_computation.22 | convolution fusion | flops 2570059776 | bytes 44893184 | tf_op jit(solution)/shard_map/dot_general | solution.py:32
  141.2 4.9 %pmax.7 = f32[128]{0:T(128)S(1)} all-reduce(f32[128]{0:T(128)S(1)} %get-tuple-element.2), channel_id=1, replica_groups=mesh['dp'=16,'vocab'=2] {'vocab'}, use_global_device_ids=true, to_apply=%region_2.3 | all-reduce | flops 128 | bytes 1024 | tf_op jit(solution)/shard_map/pmax | solution.py:41
  146.1 12.7 %fusion.1 = f32[128]{0:T(128)S(1)} fusion(f32[128,38912]{1,0:T(8,128)} %get-tuple-element.3, f32[128]{0:T(128)S(1)} %pmax.7, s32[128]{0:T(128)S(1)} %broadcast_subtract_fusion, pred[16,8,304,128]{3,2,1,0:T(8,128)(4,1)} %bitcast.29), kind=kLoop, calls=%fused_computation.6 | loop fusion | flops 24903552 | bytes 24905216 | tf_op jit(solution)/shard_map/reduce_sum | solution.py:43
  158.9 4.9 %psum.22 = f32[128]{0:T(128)S(1)} all-reduce(f32[128]{0:T(128)S(1)} %fusion.1), channel_id=1, replica_groups=mesh['dp'=16,'vocab'=2] {'vocab'}, use_global_device_ids=true, to_apply=%region_4.5 | all-reduce | flops 128 | bytes 1024 | tf_op jit(solution)/shard_map/psum | solution.py:43
  163.8 17.9 %fusion.2 = f32[128,256]{1,0:T(8,128)S(1)} fusion(bf16[256,38912]{1,0:T(8,128)(2,1)} %all-gather.2.cloned.1.call-done, f32[128,38912]{1,0:T(8,128)} %get-tuple-element.3, f32[128]{0:T(128)S(1)} %psum.22, f32[128]{0:T(128)S(1)} %pmax.7, s32[128]{0:T(128)S(1)} %broadcast_subtract_fusion, f32[128]{0:T(128)S(1)} %multiply_multiply_fusion, ...), kind=kOutput, calls=%fused_computation.7 | convolution fusion | flops 2594963456 | bytes 44959744 | tf_op jit(solution)/shard_map/dot_general | solution.py:48
  181.8 9.7 %all-reduce.3 = bf16[128,256]{1,0:T(8,128)(2,1)S(1)} all-reduce(f32[128,256]{1,0:T(8,128)S(1)} %fusion.2), channel_id=1, replica_groups=mesh['dp'=16,'vocab'=2] {'vocab'}, use_global_device_ids=true, to_apply=%region_5.6 | all-reduce | flops 32768 | bytes 196608 | tf_op jit(solution)/shard_map/psum | solution.py:51
  191.5 2.1 convolution_convert_fusion
  193.6 0.1 broadcast_in_dim.36
  193.7 0.8 gather_fusion
  194.6 0.1 bitcast_select_fusion
  194.7 11.4 %all_to_all.5 = bf16[16,8,256]{2,1,0:T(8,128)(2,1)S(1)} all-to-all(bf16[16,8,256]{2,1,0:T(8,128)(2,1)S(1)} %bitcast_select_fusion), channel_id=1, replica_groups=mesh['dp'=16,'vocab'=2] {'dp'}, dimensions={0} | all-to-all | bytes 131072 | tf_op jit(solution)/shard_map/all_to_all | solution.py:62
  206.1 1.4 convolution_convert_fusion.1
  207.5 47.4 %reduce-scatter.2.cloned.1.call-done = bf16[16,4096]{1,0:T(8,128)(2,1)} async-done(((bf16[256,4096]{1,0:T(8,128)(2,1)}), bf16[16,4096]{1,0:T(8,128)(2,1)}) %reduce-scatter.2.cloned.1.call-update) | async-done | bytes 131088 | tf_op jit(solution)/shard_map/reduce_scatter | solution.py:53
  254.9 1.6 convert_element_type.35
  (20 shorter events, 0.4 us)
Async XLA Ops:
  7.2 2.2 copy-start
  7.2 109.1 %all-gather.2.cloned.1.call-start = ((), (), s32[]{:S(2)}) async-start(), calls=%async_computation.2 | async-start | bytes 21168128 | tf_op jit(solution)/shard_map/all_gather | solution.py:20
  7.9 247.0 %reduce-scatter.2.cloned.1.call-start = ((), (), s32[]{:S(2)}) async-start(), calls=%async_computation.3 | async-start | bytes 2228224 | tf_op jit(solution)/shard_map/reduce_scatter | solution.py:53
  122.9 18.3 %copy-start.1 = (pred[128,304,128]{2,1,0:T(8,128)(4,1)}, pred[128,304,128]{2,1,0:T(8,128)(4,1)S(1)}, u32[]{:S(2)}) copy-start(pred[128,304,128]{2,1,0:T(8,128)(4,1)S(1)} %broadcast_in_dim.39) | copy-start | bytes 14942212
  163.8 27.7 %copy-start.2 = (bf16[128,4096]{1,0:T(8,128)(2,1)S(1)}, bf16[128,4096]{1,0:T(8,128)(2,1)}, u32[]{:S(2)}) copy-start(bf16[128,4096]{1,0:T(8,128)(2,1)} %param.8) | copy-start | bytes 3145732
  163.8 29.8 %copy-start.3 = (s32[128]{0:T(128)S(1)}, s32[128]{0:T(128)}, u32[]{:S(2)}) copy-start(s32[128]{0:T(128)} %param.15) | copy-start | bytes 1540
Sparse Core Ops, SparseCore 0:
  9.6 106.5 all-gather.1
  193.7 61.1 reduce-scatter.1

commit v6 on v4

--- a/solution.py
+++ b/solution.py
@@ -1,12 +1,119 @@
 import jax
 import jax.numpy as jnp
 from jax import lax
+from jax.experimental import pallas as pl
+from jax.experimental.pallas import tpu as pltpu
 from jax.sharding import PartitionSpec as P
+import functools
 
 PREFIX_MAX = 4096
 
 
 far_below = -1e30
+TILE = 128
+
+
+def block_mask(bits_ref, expand_ref, target_ref, block_cols):
+    j = pl.program_id(0)
+    tile_on = jnp.dot(bits_ref[...], expand_ref[...], preferred_element_type=jnp.float32) > 0.5
+    columns = j * block_cols + lax.broadcasted_iota(jnp.int32, tile_on.shape, 1)
+    target_hit = columns == target_ref[...]
+    return tile_on | target_hit, target_hit
+
+
+def stats_kernel(latent_ref, factor_ref, bits_ref, expand_ref, target_ref, peak_ref, total_ref, *, block_cols):
+    @pl.when(pl.program_id(0) == 0)
+    def _():
+        peak_ref[...] = jnp.full(peak_ref.shape, far_below, jnp.float32)
+        total_ref[...] = jnp.zeros(total_ref.shape, jnp.float32)
+
+    allowed, _ = block_mask(bits_ref, expand_ref, target_ref, block_cols)
+    logits = jnp.dot(latent_ref[...], factor_ref[...], preferred_element_type=jnp.float32)
+    masked = jnp.where(allowed, logits, far_below)
+    old = peak_ref[...]
+    new = jnp.maximum(old, jnp.max(masked, axis=1, keepdims=True))
+    powers = jnp.where(allowed, jnp.exp(masked - new), 0.0)
+    total_ref[...] = total_ref[...] * jnp.exp(old - new) + jnp.sum(powers, axis=1, keepdims=True)
+    peak_ref[...] = new
+
+
+def grad_kernel(latent_ref, factor_ref, bits_ref, expand_ref, target_ref, peak_ref, total_ref, weight_ref,
+                out_ref, *, block_cols):
+    @pl.when(pl.program_id(0) == 0)
+    def _():
+        out_ref[...] = jnp.zeros(out_ref.shape, jnp.float32)
+
+    allowed, target_hit = block_mask(bits_ref, expand_ref, target_ref, block_cols)
+    logits = jnp.dot(latent_ref[...], factor_ref[...], preferred_element_type=jnp.float32)
+    masked = jnp.where(allowed, logits, far_below)
+    powers = jnp.where(allowed, jnp.exp(masked - peak_ref[...]), 0.0)
+    row_probs = powers / total_ref[...]
+    score_grad = (weight_ref[...] * (row_probs - target_hit.astype(jnp.float32))).astype(jnp.bfloat16)
+    out_ref[...] += lax.dot_general(
+        score_grad, factor_ref[...], (((1,), (1,)), ((), ())), preferred_element_type=jnp.float32
+    )
+
+
+def tiles_per_block(tiles):
+    for count in (16, 8, 4, 2, 1):
+        if tiles % count == 0:
+            return count
+    return 1
+
+
+def softmax_parts(latent, factor, tile_bits, target_local):
+    rows, rank = latent.shape
+    width = factor.shape[1]
+    tiles = width // TILE
+    per_block = tiles_per_block(tiles)
+    blocks = tiles // per_block
+    block_cols = per_block * TILE
+    padded = jnp.pad(tile_bits.reshape(rows, blocks, per_block), ((0, 0), (0, 0), (0, TILE - per_block)))
+    bits = padded.reshape(rows, blocks * TILE).astype(jnp.bfloat16)
+    expand = (
+        lax.broadcasted_iota(jnp.int32, (TILE, block_cols), 0)
+        == lax.broadcasted_iota(jnp.int32, (TILE, block_cols), 1) // TILE
+    ).astype(jnp.bfloat16)
+    target = target_local[:, None]
+    common_specs = [
+        pl.BlockSpec((rows, rank), lambda j: (0, 0)),
+        pl.BlockSpec((rank, block_cols), lambda j: (0, j)),
+        pl.BlockSpec((rows, TILE), lambda j: (0, j)),
+        pl.BlockSpec((TILE, block_cols), lambda j: (0, 0)),
+        pl.BlockSpec((rows, 1), lambda j: (0, 0)),
+    ]
+    column_spec = pl.BlockSpec((rows, 1), lambda j: (0, 0))
+    params = pltpu.CompilerParams(dimension_semantics=("arbitrary",))
+    matmul_flops = 2 * rows * rank * width + 2 * rows * TILE * width
+    stats = pl.pallas_call(
+        functools.partial(stats_kernel, block_cols=block_cols),
+        grid=(blocks,),
+        in_specs=common_specs,
+        out_specs=[column_spec, column_spec],
+        out_shape=[jax.ShapeDtypeStruct((rows, 1), jnp.float32)] * 2,
+        compiler_params=params,
+        cost_estimate=pl.CostEstimate(
+            flops=matmul_flops, transcendentals=rows * width, bytes_accessed=rank * width * 2
+        ),
+    )
+
+    def grads(peak, total, weight):
+        return pl.pallas_call(
+            functools.partial(grad_kernel, block_cols=block_cols),
+            grid=(blocks,),
+            in_specs=common_specs + [column_spec] * 3,
+            out_specs=pl.BlockSpec((rows, rank), lambda j: (0, 0)),
+            out_shape=jax.ShapeDtypeStruct((rows, rank), jnp.float32),
+            compiler_params=params,
+            cost_estimate=pl.CostEstimate(
+                flops=matmul_flops + 2 * rows * rank * width,
+                transcendentals=rows * width,
+                bytes_accessed=rank * width * 2,
+            ),
+        )(latent, factor, bits, expand, target, peak, total, weight)
+
+    peak, total = stats(latent, factor, bits, expand, target)
+    return peak, total, grads
 
 
 def body(hidden, rank_factor, vocab_factor, lengths, targets, cotangent, grammar, assign):
@@ -26,28 +133,13 @@
     )
     latent = lax.psum(partial_latent, "vocab").astype(jnp.bfloat16)
     target_local = targets - first
-    columns = jnp.arange(width, dtype=jnp.int32)
     shifts = jnp.arange(30, dtype=jnp.int32)
-
-    logits = jnp.dot(latent, factor, preferred_element_type=jnp.float32)
     bits = jnp.right_shift(row_words[:, :, None], shifts) & 1
-    bits = bits.reshape(row_count, -1)[:, :tiles]
-    tile_on = jnp.broadcast_to((bits == 1)[:, :, None], (row_count, tiles, 128)).reshape(
-        row_count, width
-    )
-    target_hit = columns[None, :] == target_local[:, None]
-    allowed = tile_on | target_hit
-    masked = jnp.where(allowed, logits, far_below)
-    peak = lax.pmax(jnp.max(masked, axis=1), "vocab")
-    powers = jnp.where(allowed, jnp.exp(masked - peak[:, None]), 0.0)
-    total = lax.psum(jnp.sum(powers, axis=1), "vocab")
-    row_probs = powers / total[:, None]
-    score_grad = (weight[:, None] * (row_probs - target_hit.astype(jnp.float32))).astype(
-        jnp.bfloat16
-    )
-    rank_partial = lax.dot_general(
-        score_grad, factor, (((1,), (1,)), ((), ())), preferred_element_type=jnp.float32
-    )
+    tile_bits = bits.reshape(row_count, -1)[:, :tiles]
+    local_peak, local_total, grads = softmax_parts(latent, factor, tile_bits, target_local)
+    peak = lax.pmax(local_peak, "vocab")
+    total = lax.psum(local_total * jnp.exp(local_peak - peak), "vocab")
+    rank_partial = grads(peak, total, weight[:, None])
     rank_grad = lax.psum(rank_partial, "vocab").astype(jnp.bfloat16)
 
     grad_factor = lax.psum_scatter(

time: 273 us -> 274 us (level)
  Pallas kernels: 0 us -> 46.4 us
  matrix products: 42.4 us -> 4.92 us
  other arithmetic: 14.3 us -> 2.05 us
  blocking collectives: 42.4 us -> 51.6 us
  waiting for transfers between devices: 151 us -> 146 us
    pallas_call x0 -> x2, Pallas kernels: none -> 46.4 us  [the longest x1 23.5 us: grads(): pl.pallas_call(functools.partial(grad_kernel, block_cols=block_cols), gri...]
    dot_general x2 -> x0, matrix products: 36.3 us -> none  [the longest x1 18.3 us: body(): logits = jnp.dot(latent, factor, preferred_element_type=jnp.float32)]
    reduce_sum x1 -> x0, other arithmetic: 12.7 us -> none  [body(): total = lax.psum(jnp.sum(powers, axis=1), 'vocab')]
    broadcast_in_dim x1 -> x2, local copies, waits for them, and re-layouts: 6.63 us -> 1.46 us  [the longest x1 0.74 us: body(): rank_partial = grads(peak, total, weight[:, None])]
    pmax x1, blocking collectives: 4.92 us -> 9.4 us  [body(): peak = lax.pmax(local_peak, 'vocab')]
    psum x1, blocking collectives: 4.94 us -> 8.59 us  [body(): total = lax.psum(local_total * jnp.exp(local_peak - peak), 'vocab')]
    all_gather x1, waiting for transfers between devices: 92.1 us -> 88.6 us  [body(): factor = lax.all_gather(vocab_factor, 'dp', axis=0, tiled=True)]
  transfers between devices with their start and end apart: 2 -> 2, of which waited for: 2 -> 2; matrix products, arithmetic and copies ran while one was open for 3% -> 4% of each run, Pallas kernels for 0% -> 0%
where the time goes in v6:
time: 274 us; the launch traced here: 273 us
  waiting for transfers between devices  146 us (53%)
  blocking collectives  51.6 us (19%)
  Pallas kernels  46.4 us (17%)
  between operations  14.2 us (5%)
  local copies, waits for them, and re-layouts  7.38 us (3%)
  matrix products  4.92 us (2%)
    all_gather x1, waiting for transfers between devices, body(): factor = lax.all_gather(vocab_factor, 'dp', axis=0, tiled=True)  88.6 us
    reduce_scatter x1, waiting for transfers between devices, body(): lax.psum_scatter(lax.dot_general(rank_grad, hidden, (((0,), (0,)), ((), (...  57.1 us
    pallas_call x1, Pallas kernels, grads(): pl.pallas_call(functools.partial(grad_kernel, block_cols=block_cols), gri...  23.5 us
    pallas_call x1, Pallas kernels, softmax_parts(): peak, total = stats(latent, factor, bits, expand, target)  22.8 us
    psum x1, blocking collectives, body(): latent = lax.psum(partial_latent, 'vocab').astype(jnp.bfloat16)  12 us
    all_to_all x1, blocking collectives, body(): lax.all_to_all(picked, 'dp', split_axis=0, concat_axis=0, tiled=True)  11.4 us
    psum x1, blocking collectives, body(): rank_grad = lax.psum(rank_partial, 'vocab').astype(jnp.bfloat16)  10.3 us
    pmax x1, blocking collectives, body(): peak = lax.pmax(local_peak, 'vocab')  9.4 us
  transfers between devices with their start and end apart: 2, of which 2 were waited for; matrix products, arithmetic and copies ran while one was open for 4% of the time, Pallas kernels for 0%

profile of v6, /device:TPU:0, one launch (start us, length us, event | category | flops | bytes accessed | tf_op | source)
XLA Modules:
  0.0 273.0 jit_solution(5200725641187732508)
XLA Ops:
  7.2 0.7 all-gather.2.cloned.1.call-update
  8.0 0.9 copy.13
  9.2 0.1 fusion.2
  9.3 0.9 pad.5
  10.3 2.2 copy.16.bits_ref
  12.4 0.8 fusion.7
  13.3 0.7 copy.17.target_ref
  14.1 0.7 copy.18.weight_ref
  14.8 12.0 %all-reduce.3.latent_ref = bf16[128,256]{1,0:T(8,128)(2,1)} all-reduce(f32[128,256]{1,0:T(8,128)S(1)} %fusion.7), channel_id=1, replica_groups=mesh['dp'=16,'vocab'=2] {'vocab'}, use_global_device_ids=true, to_apply=%region_0.0 | all-reduce | flops 32768 | bytes 196608 | tf_op jit(solution)/shard_map/psum | solution.py:134
  26.8 0.9 fusion.expand_ref
  27.7 88.6 %all-gather.2.cloned.1.call-done.factor_ref = bf16[256,38912]{1,0:T(8,128)(2,1)} async-done(((bf16[16,38912]{1,0:T(8,128)(2,1)}), bf16[256,38912]{1,0:T(8,128)(2,1)}) %all-gather.2.cloned.1.call-update) | async-done | bytes 19922960 | tf_op jit(solution)/shard_map/all_gather | solution.py:127
  116.2 22.8 %shard_map.95 = (f32[128,1]{1,0:T(8,128)}, f32[128,1]{1,0:T(8,128)}) custom-call(bf16[128,256]{1,0:T(8,128)(2,1)} %all-reduce.3.latent_ref, bf16[256,38912]{1,0:T(8,128)(2,1)} %all-gather.2.cloned.1.call-done.factor_ref, bf16[128,2432]{1,0:T(8,128)(2,1)} %copy.16.bits_ref, bf16[128,2048]{1,0:T(8,128)(2,1)} %fusion.expand_ref, s32[128,1]{1,0:T(8,128)} %copy.17.target_ref), custom_call_target="tpu_custom_call" | custom-call | flops 3825205248 | bytes 19922944 | tf_op jit(solution)/shard_map/pallas_call | solution.py:115
  139.1 9.4 %pmax.7.peak_ref = f32[128,1]{1,0:T(8,128)S(1)} all-reduce(f32[128,1]{1,0:T(8,128)} %get-tuple-element.4), channel_id=1, replica_groups=mesh['dp'=16,'vocab'=2] {'vocab'}, use_global_device_ids=true, to_apply=%region_1.2 | all-reduce | flops 128 | bytes 1024 | tf_op jit(solution)/shard_map/pmax | solution.py:140
  148.5 0.9 exponential_multiply_fusion
  149.4 8.6 %psum.22.total_ref = f32[128,1]{1,0:T(8,128)} all-reduce(f32[128,1]{1,0:T(8,128)S(1)} %exponential_multiply_fusion), channel_id=1, replica_groups=mesh['dp'=16,'vocab'=2] {'vocab'}, use_global_device_ids=true, to_apply=%region_2.3 | all-reduce | flops 128 | bytes 1024 | tf_op jit(solution)/shard_map/psum | solution.py:141
  158.0 23.5 %shard_map.96 = f32[128,256]{1,0:T(8,128)} custom-call(bf16[128,256]{1,0:T(8,128)(2,1)} %all-reduce.3.latent_ref, bf16[256,38912]{1,0:T(8,128)(2,1)} %all-gather.2.cloned.1.call-done.factor_ref, bf16[128,2432]{1,0:T(8,128)(2,1)} %copy.16.bits_ref, bf16[128,2048]{1,0:T(8,128)(2,1)} %fusion.expand_ref, s32[128,1]{1,0:T(8,128)} %copy.17.target_ref, ...), custom_call_target="tpu_custom_call" | custom-call | flops 6375342080 | bytes 19922944 | tf_op jit(solution)/shard_map/pallas_call | solution.py:101
  181.5 10.3 %all-reduce.4 = bf16[128,256]{1,0:T(8,128)(2,1)S(1)} all-reduce(f32[128,256]{1,0:T(8,128)} %shard_map.96), channel_id=1, replica_groups=mesh['dp'=16,'vocab'=2] {'vocab'}, use_global_device_ids=true, to_apply=%region_3.4 | all-reduce | flops 32768 | bytes 196608 | tf_op jit(solution)/shard_map/psum | solution.py:143
  191.8 2.7 fusion.8
  194.5 0.6 copy-done.6
  195.1 0.1 broadcast_in_dim.24
  195.2 0.8 gather_fusion
  196.2 11.4 %all_to_all.5 = bf16[16,8,256]{2,1,0:T(8,128)(2,1)S(1)} all-to-all(bf16[16,8,256]{2,1,0:T(8,128)(2,1)S(1)} %bitcast_select_fusion), channel_id=1, replica_groups=mesh['dp'=16,'vocab'=2] {'dp'}, dimensions={0} | all-to-all | bytes 131072 | tf_op jit(solution)/shard_map/all_to_all | solution.py:154
  207.6 1.4 convolution_convert_fusion
  209.0 57.1 %reduce-scatter.2.cloned.1.call-done = f32[16,4096]{1,0:T(8,128)} async-done(((f32[256,4096]{1,0:T(8,128)}), f32[16,4096]{1,0:T(8,128)}) %reduce-scatter.2.cloned.1.call-update) | async-done | bytes 262160 | tf_op jit(solution)/shard_map/reduce_scatter | solution.py:145
  (30 shorter events, 0.5 us)
Async XLA Ops:
  7.2 5.3 %copy-start = (bf16[256,4096]{1,0:T(8,128)(2,1)S(1)}, bf16[256,4096]{1,0:T(8,128)(2,1)}, u32[]{:S(2)}) copy-start(bf16[256,4096]{1,0:T(8,128)(2,1)} %param.9) | copy-start | bytes 6291460
  7.2 5.3 %copy-start.1 = (bf16[128,4096]{1,0:T(8,128)(2,1)S(1)}, bf16[128,4096]{1,0:T(8,128)(2,1)}, u32[]{:S(2)}) copy-start(bf16[128,4096]{1,0:T(8,128)(2,1)} %param.8) | copy-start | bytes 3145732
  7.2 109.1 %all-gather.2.cloned.1.call-start = ((), (), s32[]{:S(2)}) async-start(), calls=%async_computation.2 | async-start | bytes 21168128 | tf_op jit(solution)/shard_map/all_gather | solution.py:127
  7.9 258.2 %reduce-scatter.2.cloned.1.call-start = ((), (), s32[]{:S(2)}) async-start(), calls=%async_computation.3 | async-start | bytes 4456448 | tf_op jit(solution)/shard_map/reduce_scatter | solution.py:145
  10.3 3.0 %copy-start.3 = (s32[128]{0:T(128)S(1)}, s32[128]{0:T(128)}, u32[]{:S(2)}) copy-start(s32[128]{0:T(128)} %param.12) | copy-start | bytes 1540
  10.3 3.8 %copy-start.4 = (s32[128]{0:T(128)S(1)}, s32[128]{0:T(128)}, u32[]{:S(2)}) copy-start(s32[128]{0:T(128)} %param.11) | copy-start | bytes 1540
  10.3 3.8 %copy-start.5 = (bf16[128]{0:T(256)(128)(2,1)S(1)}, bf16[128]{0:T(256)(128)(2,1)}, u32[]{:S(2)}) copy-start(bf16[128]{0:T(256)(128)(2,1)} %param.13) | copy-start | bytes 772
  148.5 9.5 %copy-start.2 = (f32[128,1]{1,0:T(8,128)}, f32[128,1]{1,0:T(8,128)S(1)}, u32[]{:S(2)}) copy-start(f32[128,1]{1,0:T(8,128)S(1)} %pmax.7.peak_ref) | copy-start | bytes 1540
  194.5 0.7 copy-start.6
Sparse Core Ops, SparseCore 0:
  9.6 106.5 all-gather.1
  194.6 71.4 reduce-scatter.1

commit v7 on v6

--- a/solution.py
+++ b/solution.py
@@ -13,42 +13,38 @@
 TILE = 128
 
 
-def block_mask(bits_ref, expand_ref, target_ref, block_cols):
-    j = pl.program_id(0)
-    tile_on = jnp.dot(bits_ref[...], expand_ref[...], preferred_element_type=jnp.float32) > 0.5
-    columns = j * block_cols + lax.broadcasted_iota(jnp.int32, tile_on.shape, 1)
-    target_hit = columns == target_ref[...]
-    return tile_on | target_hit, target_hit
+def block_scores(latent_ref, factor_ref, bias_ref, expand_ref, target_ref, block_cols):
+    target_rel = target_ref[...] - pl.program_id(0) * block_cols
+    bias = jnp.dot(bias_ref[...], expand_ref[...], preferred_element_type=jnp.float32)
+    logits = jnp.dot(latent_ref[...], factor_ref[...], preferred_element_type=jnp.float32)
+    target_hit = lax.broadcasted_iota(jnp.int32, logits.shape, 1) == target_rel
+    return jnp.where(target_hit, logits, logits + bias), target_hit
 
 
-def stats_kernel(latent_ref, factor_ref, bits_ref, expand_ref, target_ref, peak_ref, total_ref, *, block_cols):
+def stats_kernel(latent_ref, factor_ref, bias_ref, expand_ref, target_ref, peak_ref, total_ref, *, block_cols):
     @pl.when(pl.program_id(0) == 0)
     def _():
         peak_ref[...] = jnp.full(peak_ref.shape, far_below, jnp.float32)
         total_ref[...] = jnp.zeros(total_ref.shape, jnp.float32)
 
-    allowed, _ = block_mask(bits_ref, expand_ref, target_ref, block_cols)
-    logits = jnp.dot(latent_ref[...], factor_ref[...], preferred_element_type=jnp.float32)
-    masked = jnp.where(allowed, logits, far_below)
+    masked, _ = block_scores(latent_ref, factor_ref, bias_ref, expand_ref, target_ref, block_cols)
     old = peak_ref[...]
     new = jnp.maximum(old, jnp.max(masked, axis=1, keepdims=True))
-    powers = jnp.where(allowed, jnp.exp(masked - new), 0.0)
-    total_ref[...] = total_ref[...] * jnp.exp(old - new) + jnp.sum(powers, axis=1, keepdims=True)
+    total_ref[...] = total_ref[...] * jnp.exp(old - new) + jnp.sum(
+        jnp.exp(masked - new), axis=1, keepdims=True
+    )
     peak_ref[...] = new
 
 
-def grad_kernel(latent_ref, factor_ref, bits_ref, expand_ref, target_ref, peak_ref, total_ref, weight_ref,
+def grad_kernel(latent_ref, factor_ref, bias_ref, expand_ref, target_ref, peak_ref, scale_ref, weight_ref,
                 out_ref, *, block_cols):
     @pl.when(pl.program_id(0) == 0)
     def _():
         out_ref[...] = jnp.zeros(out_ref.shape, jnp.float32)
 
-    allowed, target_hit = block_mask(bits_ref, expand_ref, target_ref, block_cols)
-    logits = jnp.dot(latent_ref[...], factor_ref[...], preferred_element_type=jnp.float32)
-    masked = jnp.where(allowed, logits, far_below)
-    powers = jnp.where(allowed, jnp.exp(masked - peak_ref[...]), 0.0)
-    row_probs = powers / total_ref[...]
-    score_grad = (weight_ref[...] * (row_probs - target_hit.astype(jnp.float32))).astype(jnp.bfloat16)
+    masked, target_hit = block_scores(latent_ref, factor_ref, bias_ref, expand_ref, target_ref, block_cols)
+    powers = jnp.exp(masked - peak_ref[...])
+    score_grad = (powers * scale_ref[...] - jnp.where(target_hit, weight_ref[...], 0.0)).astype(jnp.bfloat16)
     out_ref[...] += lax.dot_general(
         score_grad, factor_ref[...], (((1,), (1,)), ((), ())), preferred_element_type=jnp.float32
     )
@@ -69,7 +65,7 @@
     blocks = tiles // per_block
     block_cols = per_block * TILE
     padded = jnp.pad(tile_bits.reshape(rows, blocks, per_block), ((0, 0), (0, 0), (0, TILE - per_block)))
-    bits = padded.reshape(rows, blocks * TILE).astype(jnp.bfloat16)
+    bits = jnp.where(padded.reshape(rows, blocks * TILE) == 1, 0.0, far_below).astype(jnp.bfloat16)
     expand = (
         lax.broadcasted_iota(jnp.int32, (TILE, block_cols), 0)
         == lax.broadcasted_iota(jnp.int32, (TILE, block_cols), 1) // TILE
@@ -97,7 +93,7 @@
         ),
     )
 
-    def grads(peak, total, weight):
+    def grads(peak, scale, weight):
         return pl.pallas_call(
             functools.partial(grad_kernel, block_cols=block_cols),
             grid=(blocks,),
@@ -110,7 +106,7 @@
                 transcendentals=rows * width,
                 bytes_accessed=rank * width * 2,
             ),
-        )(latent, factor, bits, expand, target, peak, total, weight)
+        )(latent, factor, bits, expand, target, peak, scale, weight)
 
     peak, total = stats(latent, factor, bits, expand, target)
     return peak, total, grads
@@ -137,9 +133,10 @@
     bits = jnp.right_shift(row_words[:, :, None], shifts) & 1
     tile_bits = bits.reshape(row_count, -1)[:, :tiles]
     local_peak, local_total, grads = softmax_parts(latent, factor, tile_bits, target_local)
+    local_peak = local_peak[:, 0]
     peak = lax.pmax(local_peak, "vocab")
-    total = lax.psum(local_total * jnp.exp(local_peak - peak), "vocab")
-    rank_partial = grads(peak, total, weight[:, None])
+    total = lax.psum(local_total[:, 0] * jnp.exp(local_peak - peak), "vocab")
+    rank_partial = grads(peak[:, None], (weight / total)[:, None], weight[:, None])
     rank_grad = lax.psum(rank_partial, "vocab").astype(jnp.bfloat16)
 
     grad_factor = lax.psum_scatter(

time: 274 us -> 268 us (0.978)
  blocking collectives: 51.6 us -> 43.6 us
    pmax x1, blocking collectives: 9.4 us -> 4.94 us  [body(): peak = lax.pmax(local_peak, 'vocab')]
    psum x1, blocking collectives: 8.59 us -> 4.94 us  [body(): total = lax.psum(local_total[:, 0] * jnp.exp(local_peak - peak), 'vocab')]
where the time goes in v7:
time: 268 us; the launch traced here: 266 us
  waiting for transfers between devices  148 us (55%)
  Pallas kernels  44.1 us (16%)
  blocking collectives  43.6 us (16%)
  between operations  14.2 us (5%)
  local copies, waits for them, and re-layouts  7.85 us (3%)
  matrix products  4.91 us (2%)
  other arithmetic  3.99 us (1%)
    all_gather x1, waiting for transfers between devices, body(): factor = lax.all_gather(vocab_factor, 'dp', axis=0, tiled=True)  89.4 us
    reduce_scatter x1, waiting for transfers between devices, body(): lax.psum_scatter(lax.dot_general(rank_grad, hidden, (((0,), (0,)), ((), (...  57.7 us
    pallas_call x1, Pallas kernels, grads(): pl.pallas_call(functools.partial(grad_kernel, block_cols=block_cols), gri...  22.7 us
    pallas_call x1, Pallas kernels, softmax_parts(): peak, total = stats(latent, factor, bits, expand, target)  21.3 us
    psum x1, blocking collectives, body(): latent = lax.psum(partial_latent, 'vocab').astype(jnp.bfloat16)  11.9 us
    all_to_all x1, blocking collectives, body(): lax.all_to_all(picked, 'dp', split_axis=0, concat_axis=0, tiled=True)  11.4 us
    psum x1, blocking collectives, body(): rank_grad = lax.psum(rank_partial, 'vocab').astype(jnp.bfloat16)  10.4 us
  transfers between devices with their start and end apart: 2, of which 2 were waited for; matrix products, arithmetic and copies ran while one was open for 4% of the time, Pallas kernels for 0%

profile of v7, /device:TPU:0, one launch (start us, length us, event | category | flops | bytes accessed | tf_op | source)
XLA Modules:
  0.0 266.4 jit_solution(10038898764701512637)
XLA Ops:
  7.2 0.7 all-gather.2.cloned.1.call-update
  8.0 0.9 copy.15
  9.3 1.0 select_convert_fusion
  10.3 2.1 copy.18.bias_ref
  12.4 0.8 fusion.7
  13.3 0.7 copy.19.target_ref
  14.0 11.9 %all-reduce.3.latent_ref = bf16[128,256]{1,0:T(8,128)(2,1)} all-reduce(f32[128,256]{1,0:T(8,128)S(1)} %fusion.7), channel_id=1, replica_groups=mesh['dp'=16,'vocab'=2] {'vocab'}, use_global_device_ids=true, to_apply=%region_0.0 | all-reduce | flops 32768 | bytes 196608 | tf_op jit(solution)/shard_map/psum | solution.py:130
  26.0 0.9 fusion.expand_ref
  26.9 89.4 %all-gather.2.cloned.1.call-done.factor_ref = bf16[256,38912]{1,0:T(8,128)(2,1)} async-done(((bf16[16,38912]{1,0:T(8,128)(2,1)}), bf16[256,38912]{1,0:T(8,128)(2,1)}) %all-gather.2.cloned.1.call-update) | async-done | bytes 19922960 | tf_op jit(solution)/shard_map/all_gather | solution.py:123
  116.2 21.3 %shard_map.95 = (f32[128,1]{1,0:T(8,128)}, f32[128,1]{1,0:T(8,128)}) custom-call(bf16[128,256]{1,0:T(8,128)(2,1)} %all-reduce.3.latent_ref, bf16[256,38912]{1,0:T(8,128)(2,1)} %all-gather.2.cloned.1.call-done.factor_ref, bf16[128,2432]{1,0:T(8,128)(2,1)} %copy.18.bias_ref, bf16[128,2048]{1,0:T(8,128)(2,1)} %fusion.expand_ref, s32[128,1]{1,0:T(8,128)} %copy.19.target_ref), custom_call_target="tpu_custom_call" | custom-call | flops 3825205248 | bytes 19922944 | tf_op jit(solution)/shard_map/pallas_call | solution.py:111
  137.6 0.9 reduce
  138.5 4.9 %pmax.7 = f32[128]{0:T(128)S(1)} all-reduce(f32[128]{0:T(128)S(1)} %reduce), channel_id=1, replica_groups=mesh['dp'=16,'vocab'=2] {'vocab'}, use_global_device_ids=true, to_apply=%region_1.2 | all-reduce | flops 128 | bytes 1024 | tf_op jit(solution)/shard_map/pmax | solution.py:137
  143.5 0.9 reduce.1
  144.4 4.9 %psum.22 = f32[128]{0:T(128)S(1)} all-reduce(f32[128]{0:T(128)S(1)} %exponential_multiply_fusion), channel_id=1, replica_groups=mesh['dp'=16,'vocab'=2] {'vocab'}, use_global_device_ids=true, to_apply=%region_2.3 | all-reduce | flops 128 | bytes 1024 | tf_op jit(solution)/shard_map/psum | solution.py:138
  149.4 0.7 copy.21.scale_ref
  150.1 0.7 copy.22.weight_ref
  150.8 0.7 copy.20.peak_ref
  151.6 22.7 %shard_map.96 = f32[128,256]{1,0:T(8,128)} custom-call(bf16[128,256]{1,0:T(8,128)(2,1)} %all-reduce.3.latent_ref, bf16[256,38912]{1,0:T(8,128)(2,1)} %all-gather.2.cloned.1.call-done.factor_ref, bf16[128,2432]{1,0:T(8,128)(2,1)} %copy.18.bias_ref, bf16[128,2048]{1,0:T(8,128)(2,1)} %fusion.expand_ref, s32[128,1]{1,0:T(8,128)} %copy.19.target_ref, ...), custom_call_target="tpu_custom_call" | custom-call | flops 6375342080 | bytes 19922944 | tf_op jit(solution)/shard_map/pallas_call | solution.py:97
  174.3 10.4 %all-reduce.4 = bf16[128,256]{1,0:T(8,128)(2,1)S(1)} all-reduce(f32[128,256]{1,0:T(8,128)} %shard_map.96), channel_id=1, replica_groups=mesh['dp'=16,'vocab'=2] {'vocab'}, use_global_device_ids=true, to_apply=%region_3.4 | all-reduce | flops 32768 | bytes 196608 | tf_op jit(solution)/shard_map/psum | solution.py:140
  184.7 2.7 fusion.8
  188.1 0.8 gather_fusion
  189.1 11.4 %all_to_all.5 = bf16[16,8,256]{2,1,0:T(8,128)(2,1)S(1)} all-to-all(bf16[16,8,256]{2,1,0:T(8,128)(2,1)S(1)} %bitcast_select_fusion), channel_id=1, replica_groups=mesh['dp'=16,'vocab'=2] {'dp'}, dimensions={0} | all-to-all | bytes 131072 | tf_op jit(solution)/shard_map/all_to_all | solution.py:151
  200.5 1.4 convolution_convert_fusion
  201.9 57.7 %reduce-scatter.2.cloned.1.call-done = f32[16,4096]{1,0:T(8,128)} async-done(((f32[256,4096]{1,0:T(8,128)}), f32[16,4096]{1,0:T(8,128)}) %reduce-scatter.2.cloned.1.call-update) | async-done | bytes 262160 | tf_op jit(solution)/shard_map/reduce_scatter | solution.py:142
  (32 shorter events, 1.4 us)
Async XLA Ops:
  7.2 5.2 %copy-start = (bf16[256,4096]{1,0:T(8,128)(2,1)S(1)}, bf16[256,4096]{1,0:T(8,128)(2,1)}, u32[]{:S(2)}) copy-start(bf16[256,4096]{1,0:T(8,128)(2,1)} %param.9) | copy-start | bytes 6291460
  7.2 5.2 %copy-start.1 = (bf16[128,4096]{1,0:T(8,128)(2,1)S(1)}, bf16[128,4096]{1,0:T(8,128)(2,1)}, u32[]{:S(2)}) copy-start(bf16[128,4096]{1,0:T(8,128)(2,1)} %param.8) | copy-start | bytes 3145732
  7.2 109.1 %all-gather.2.cloned.1.call-start = ((), (), s32[]{:S(2)}) async-start(), calls=%async_computation.2 | async-start | bytes 21168128 | tf_op jit(solution)/shard_map/all_gather | solution.py:123
  7.9 251.7 %reduce-scatter.2.cloned.1.call-start = ((), (), s32[]{:S(2)}) async-start(), calls=%async_computation.3 | async-start | bytes 4456448 | tf_op jit(solution)/shard_map/reduce_scatter | solution.py:142
  10.3 3.0 %copy-start.4 = (s32[128]{0:T(128)S(1)}, s32[128]{0:T(128)}, u32[]{:S(2)}) copy-start(s32[128]{0:T(128)} %param.12) | copy-start | bytes 1540
  26.9 122.5 %copy-start.2 = (s32[128]{0:T(128)S(1)}, s32[128]{0:T(128)}, u32[]{:S(2)}) copy-start(s32[128]{0:T(128)} %param.11) | copy-start | bytes 1540
  26.9 122.5 %copy-start.3 = (bf16[128]{0:T(256)(128)(2,1)S(1)}, bf16[128]{0:T(256)(128)(2,1)}, u32[]{:S(2)}) copy-start(bf16[128]{0:T(256)(128)(2,1)} %param.13) | copy-start | bytes 772
  187.3 0.7 copy-start.5
Sparse Core Ops, SparseCore 0:
  9.6 106.5 all-gather.1
  187.5 72.0 reduce-scatter.1

commit v8 on v7

--- a/solution.py
+++ b/solution.py
@@ -51,7 +51,7 @@
 
 
 def tiles_per_block(tiles):
-    for count in (16, 8, 4, 2, 1):
+    for count in (38, 19, 16, 8, 4, 2, 1):
         if tiles % count == 0:
             return count
     return 1

time: 268 us -> 257 us (0.959)
  Pallas kernels: 44.1 us -> 34 us
    pallas_call x1, Pallas kernels: 21.3 us -> 15.1 us  [softmax_parts(): peak, total = stats(latent, factor, bits, expand, target)]
    pallas_call x1, Pallas kernels: 22.7 us -> 18.9 us  [grads(): pl.pallas_call(functools.partial(grad_kernel, block_cols=block_cols), gri...]
where the time goes in v8:
time: 257 us; the launch traced here: 256 us
  waiting for transfers between devices  148 us (58%)
  blocking collectives  43.6 us (17%)
  Pallas kernels  34 us (13%)
  between operations  14.2 us (6%)
  local copies, waits for them, and re-layouts  7.23 us (3%)
  matrix products  4.91 us (2%)
  other arithmetic  4.37 us (2%)
    all_gather x1, waiting for transfers between devices, body(): factor = lax.all_gather(vocab_factor, 'dp', axis=0, tiled=True)  89.6 us
    reduce_scatter x1, waiting for transfers between devices, body(): lax.psum_scatter(lax.dot_general(rank_grad, hidden, (((0,), (0,)), ((), (...  57.8 us
    pallas_call x1, Pallas kernels, grads(): pl.pallas_call(functools.partial(grad_kernel, block_cols=block_cols), gri...  18.9 us
    pallas_call x1, Pallas kernels, softmax_parts(): peak, total = stats(latent, factor, bits, expand, target)  15.1 us
    psum x1, blocking collectives, body(): latent = lax.psum(partial_latent, 'vocab').astype(jnp.bfloat16)  11.9 us
    all_to_all x1, blocking collectives, body(): lax.all_to_all(picked, 'dp', split_axis=0, concat_axis=0, tiled=True)  11.4 us
    psum x1, blocking collectives, body(): rank_grad = lax.psum(rank_partial, 'vocab').astype(jnp.bfloat16)  10.4 us
  transfers between devices with their start and end apart: 2, of which 2 were waited for; matrix products, arithmetic and copies ran while one was open for 4% of the time, Pallas kernels for 0%

profile of v8, /device:TPU:0, one launch (start us, length us, event | category | flops | bytes accessed | tf_op | source)
XLA Modules:
  0.0 256.4 jit_solution(9185041506299556289)
XLA Ops:
  7.2 0.7 all-gather.2.cloned.1.call-update
  8.0 0.9 copy.15
  10.0 1.0 select_convert_fusion
  10.9 0.9 copy.22.bias_ref
  11.8 0.8 fusion.7
  12.7 0.7 copy.18.target_ref
  13.4 11.9 %all-reduce.3.latent_ref = bf16[128,256]{1,0:T(8,128)(2,1)} all-reduce(f32[128,256]{1,0:T(8,128)S(1)} %fusion.7), channel_id=1, replica_groups=mesh['dp'=16,'vocab'=2] {'vocab'}, use_global_device_ids=true, to_apply=%region_0.0 | all-reduce | flops 32768 | bytes 196608 | tf_op jit(solution)/shard_map/psum | solution.py:130
  25.4 1.3 fusion.expand_ref
  26.6 89.6 %all-gather.2.cloned.1.call-done.factor_ref = bf16[256,38912]{1,0:T(8,128)(2,1)} async-done(((bf16[16,38912]{1,0:T(8,128)(2,1)}), bf16[256,38912]{1,0:T(8,128)(2,1)}) %all-gather.2.cloned.1.call-update) | async-done | bytes 19922960 | tf_op jit(solution)/shard_map/all_gather | solution.py:123
  116.3 15.1 %shard_map.95 = (f32[128,1]{1,0:T(8,128)}, f32[128,1]{1,0:T(8,128)}) custom-call(bf16[128,256]{1,0:T(8,128)(2,1)} %all-reduce.3.latent_ref, bf16[256,38912]{1,0:T(8,128)(2,1)} %all-gather.2.cloned.1.call-done.factor_ref, bf16[128,1024]{1,0:T(8,128)(2,1)} %copy.22.bias_ref, bf16[128,4864]{1,0:T(8,128)(2,1)} %fusion.expand_ref, s32[128,1]{1,0:T(8,128)} %copy.18.target_ref), custom_call_target="tpu_custom_call" | custom-call | flops 3825205248 | bytes 19922944 | tf_op jit(solution)/shard_map/pallas_call | solution.py:111
  131.3 0.9 reduce
  132.3 4.9 %pmax.7 = f32[128]{0:T(128)S(1)} all-reduce(f32[128]{0:T(128)S(1)} %reduce), channel_id=1, replica_groups=mesh['dp'=16,'vocab'=2] {'vocab'}, use_global_device_ids=true, to_apply=%region_1.2 | all-reduce | flops 128 | bytes 1024 | tf_op jit(solution)/shard_map/pmax | solution.py:137
  137.2 0.9 reduce.1
  138.2 4.9 %psum.22 = f32[128]{0:T(128)S(1)} all-reduce(f32[128]{0:T(128)S(1)} %exponential_multiply_fusion), channel_id=1, replica_groups=mesh['dp'=16,'vocab'=2] {'vocab'}, use_global_device_ids=true, to_apply=%region_2.3 | all-reduce | flops 128 | bytes 1024 | tf_op jit(solution)/shard_map/psum | solution.py:138
  143.1 0.7 copy.20.scale_ref
  143.9 0.7 copy.21.weight_ref
  144.6 0.7 copy.19.peak_ref
  145.3 18.9 %shard_map.96 = f32[128,256]{1,0:T(8,128)} custom-call(bf16[128,256]{1,0:T(8,128)(2,1)} %all-reduce.3.latent_ref, bf16[256,38912]{1,0:T(8,128)(2,1)} %all-gather.2.cloned.1.call-done.factor_ref, bf16[128,1024]{1,0:T(8,128)(2,1)} %copy.22.bias_ref, bf16[128,4864]{1,0:T(8,128)(2,1)} %fusion.expand_ref, s32[128,1]{1,0:T(8,128)} %copy.18.target_ref, ...), custom_call_target="tpu_custom_call" | custom-call | flops 6375342080 | bytes 19922944 | tf_op jit(solution)/shard_map/pallas_call | solution.py:97
  164.2 10.4 %all-reduce.4 = bf16[128,256]{1,0:T(8,128)(2,1)S(1)} all-reduce(f32[128,256]{1,0:T(8,128)} %shard_map.96), channel_id=1, replica_groups=mesh['dp'=16,'vocab'=2] {'vocab'}, use_global_device_ids=true, to_apply=%region_3.4 | all-reduce | flops 32768 | bytes 196608 | tf_op jit(solution)/shard_map/psum | solution.py:140
  174.6 2.7 %fusion.8 = f32[256,4096]{1,0:T(8,128)} fusion(bf16[128,256]{1,0:T(8,128)(2,1)S(1)} %all-reduce.4, bf16[128,4096]{1,0:T(8,128)(2,1)S(1)} %copy-done.1), kind=kOutput, calls=%fused_computation.26 | convolution fusion | flops 268435456 | bytes 5308416 | tf_op jit(solution)/shard_map/dot_general | solution.py:143
  178.1 0.8 gather_fusion
  179.0 11.4 %all_to_all.5 = bf16[16,8,256]{2,1,0:T(8,128)(2,1)S(1)} all-to-all(bf16[16,8,256]{2,1,0:T(8,128)(2,1)S(1)} %bitcast_select_fusion), channel_id=1, replica_groups=mesh['dp'=16,'vocab'=2] {'dp'}, dimensions={0} | all-to-all | bytes 131072 | tf_op jit(solution)/shard_map/all_to_all | solution.py:151
  190.4 1.4 convolution_convert_fusion
  191.8 57.8 %reduce-scatter.2.cloned.1.call-done = f32[16,4096]{1,0:T(8,128)} async-done(((f32[256,4096]{1,0:T(8,128)}), f32[16,4096]{1,0:T(8,128)}) %reduce-scatter.2.cloned.1.call-update) | async-done | bytes 262160 | tf_op jit(solution)/shard_map/reduce_scatter | solution.py:142
  (33 shorter events, 2.0 us)
Async XLA Ops:
  7.2 4.6 %copy-start = (bf16[256,4096]{1,0:T(8,128)(2,1)S(1)}, bf16[256,4096]{1,0:T(8,128)(2,1)}, u32[]{:S(2)}) copy-start(bf16[256,4096]{1,0:T(8,128)(2,1)} %param.9) | copy-start | bytes 6291460
  7.2 4.6 %copy-start.1 = (bf16[128,4096]{1,0:T(8,128)(2,1)S(1)}, bf16[128,4096]{1,0:T(8,128)(2,1)}, u32[]{:S(2)}) copy-start(bf16[128,4096]{1,0:T(8,128)(2,1)} %param.8) | copy-start | bytes 3145732
  7.2 109.1 %all-gather.2.cloned.1.call-start = ((), (), s32[]{:S(2)}) async-start(), calls=%async_computation.2 | async-start | bytes 21168128 | tf_op jit(solution)/shard_map/all_gather | solution.py:123
  7.9 241.6 %reduce-scatter.2.cloned.1.call-start = ((), (), s32[]{:S(2)}) async-start(), calls=%async_computation.3 | async-start | bytes 4456448 | tf_op jit(solution)/shard_map/reduce_scatter | solution.py:142
  10.0 2.7 %copy-start.4 = (s32[128]{0:T(128)S(1)}, s32[128]{0:T(128)}, u32[]{:S(2)}) copy-start(s32[128]{0:T(128)} %param.12) | copy-start | bytes 1540
  26.6 116.5 %copy-start.2 = (s32[128]{0:T(128)S(1)}, s32[128]{0:T(128)}, u32[]{:S(2)}) copy-start(s32[128]{0:T(128)} %param.11) | copy-start | bytes 1540
  26.6 116.5 %copy-start.3 = (bf16[128]{0:T(256)(128)(2,1)S(1)}, bf16[128]{0:T(256)(128)(2,1)}, u32[]{:S(2)}) copy-start(bf16[128]{0:T(256)(128)(2,1)} %param.13) | copy-start | bytes 772
  177.3 0.7 copy-start.5
Sparse Core Ops, SparseCore 0:
  9.6 106.5 all-gather.1
  177.4 72.0 reduce-scatter.1

commit v9 on v8

--- a/solution.py
+++ b/solution.py
@@ -51,7 +51,7 @@
 
 
 def tiles_per_block(tiles):
-    for count in (38, 19, 16, 8, 4, 2, 1):
+    for count in (76, 38, 19, 16, 8, 4, 2, 1):
         if tiles % count == 0:
             return count
     return 1

time: 257 us -> 258 us (level)
  transfers between devices with their start and end apart: 2 -> 2, of which waited for: 2 -> 2; matrix products, arithmetic and copies ran while one was open for 4% -> 3% of each run, Pallas kernels for 0% -> 0%
where the time goes in v9:
time: 258 us; the launch traced here: 257 us
  waiting for transfers between devices  149 us (58%)
  blocking collectives  43.6 us (17%)
  Pallas kernels  34.7 us (13%)
  between operations  14.2 us (6%)
  local copies, waits for them, and re-layouts  6.49 us (3%)
  matrix products  4.91 us (2%)
  other arithmetic  4.1 us (2%)
    all_gather x1, waiting for transfers between devices, body(): factor = lax.all_gather(vocab_factor, 'dp', axis=0, tiled=True)  90.6 us
    reduce_scatter x1, waiting for transfers between devices, body(): lax.psum_scatter(lax.dot_general(rank_grad, hidden, (((0,), (0,)), ((), (...  57.7 us
    pallas_call x1, Pallas kernels, grads(): pl.pallas_call(functools.partial(grad_kernel, block_cols=block_cols), gri...  20.6 us
    pallas_call x1, Pallas kernels, softmax_parts(): peak, total = stats(latent, factor, bits, expand, target)  14.1 us
    psum x1, blocking collectives, body(): latent = lax.psum(partial_latent, 'vocab').astype(jnp.bfloat16)  11.9 us
    all_to_all x1, blocking collectives, body(): lax.all_to_all(picked, 'dp', split_axis=0, concat_axis=0, tiled=True)  11.4 us
    psum x1, blocking collectives, body(): rank_grad = lax.psum(rank_partial, 'vocab').astype(jnp.bfloat16)  10.4 us
  transfers between devices with their start and end apart: 2, of which 2 were waited for; matrix products, arithmetic and copies ran while one was open for 3% of the time, Pallas kernels for 0%

profile of v9, /device:TPU:0, one launch (start us, length us, event | category | flops | bytes accessed | tf_op | source)
XLA Modules:
  0.0 257.1 jit_solution(18281516355495482022)
XLA Ops:
  7.2 0.7 all-gather.2.cloned.1.call-update
  8.0 0.9 copy.15
  9.4 0.8 copy.22.bias_ref
  10.1 0.8 fusion.7
  11.0 0.7 copy.18.target_ref
  11.7 11.9 %all-reduce.3.latent_ref = bf16[128,256]{1,0:T(8,128)(2,1)} all-reduce(f32[128,256]{1,0:T(8,128)S(1)} %fusion.7), channel_id=1, replica_groups=mesh['dp'=16,'vocab'=2] {'vocab'}, use_global_device_ids=true, to_apply=%region_0.0 | all-reduce | flops 32768 | bytes 196608 | tf_op jit(solution)/shard_map/psum | solution.py:130
  23.7 1.9 fusion.expand_ref
  25.6 90.6 %all-gather.2.cloned.1.call-done.factor_ref = bf16[256,38912]{1,0:T(8,128)(2,1)} async-done(((bf16[16,38912]{1,0:T(8,128)(2,1)}), bf16[256,38912]{1,0:T(8,128)(2,1)}) %all-gather.2.cloned.1.call-update) | async-done | bytes 19922960 | tf_op jit(solution)/shard_map/all_gather | solution.py:123
  116.3 14.1 %shard_map.95 = (f32[128,1]{1,0:T(8,128)}, f32[128,1]{1,0:T(8,128)}) custom-call(bf16[128,256]{1,0:T(8,128)(2,1)} %all-reduce.3.latent_ref, bf16[256,38912]{1,0:T(8,128)(2,1)} %all-gather.2.cloned.1.call-done.factor_ref, bf16[128,512]{1,0:T(8,128)(2,1)} %copy.22.bias_ref, bf16[128,9728]{1,0:T(8,128)(2,1)} %fusion.expand_ref, s32[128,1]{1,0:T(8,128)} %copy.18.target_ref), custom_call_target="tpu_custom_call" | custom-call | flops 3825205248 | bytes 19922944 | tf_op jit(solution)/shard_map/pallas_call | solution.py:111
  130.3 0.9 reduce
  131.3 4.9 %pmax.7 = f32[128]{0:T(128)S(1)} all-reduce(f32[128]{0:T(128)S(1)} %reduce), channel_id=1, replica_groups=mesh['dp'=16,'vocab'=2] {'vocab'}, use_global_device_ids=true, to_apply=%region_1.2 | all-reduce | flops 128 | bytes 1024 | tf_op jit(solution)/shard_map/pmax | solution.py:137
  136.2 0.9 reduce.1
  137.2 4.9 %psum.22 = f32[128]{0:T(128)S(1)} all-reduce(f32[128]{0:T(128)S(1)} %exponential_multiply_fusion), channel_id=1, replica_groups=mesh['dp'=16,'vocab'=2] {'vocab'}, use_global_device_ids=true, to_apply=%region_2.3 | all-reduce | flops 128 | bytes 1024 | tf_op jit(solution)/shard_map/psum | solution.py:138
  142.2 0.7 copy.20.scale_ref
  142.9 0.7 copy.21.weight_ref
  143.6 0.7 copy.19.peak_ref
  144.3 20.6 %shard_map.96 = f32[128,256]{1,0:T(8,128)} custom-call(bf16[128,256]{1,0:T(8,128)(2,1)} %all-reduce.3.latent_ref, bf16[256,38912]{1,0:T(8,128)(2,1)} %all-gather.2.cloned.1.call-done.factor_ref, bf16[128,512]{1,0:T(8,128)(2,1)} %copy.22.bias_ref, bf16[128,9728]{1,0:T(8,128)(2,1)} %fusion.expand_ref, s32[128,1]{1,0:T(8,128)} %copy.18.target_ref, ...), custom_call_target="tpu_custom_call" | custom-call | flops 6375342080 | bytes 19922944 | tf_op jit(solution)/shard_map/pallas_call | solution.py:97
  165.0 10.4 %all-reduce.4 = bf16[128,256]{1,0:T(8,128)(2,1)S(1)} all-reduce(f32[128,256]{1,0:T(8,128)} %shard_map.96), channel_id=1, replica_groups=mesh['dp'=16,'vocab'=2] {'vocab'}, use_global_device_ids=true, to_apply=%region_3.4 | all-reduce | flops 32768 | bytes 196608 | tf_op jit(solution)/shard_map/psum | solution.py:140
  175.4 2.7 %fusion.8 = f32[256,4096]{1,0:T(8,128)} fusion(bf16[128,256]{1,0:T(8,128)(2,1)S(1)} %all-reduce.4, bf16[128,4096]{1,0:T(8,128)(2,1)S(1)} %copy-done.1), kind=kOutput, calls=%fused_computation.26 | convolution fusion | flops 268435456 | bytes 5308416 | tf_op jit(solution)/shard_map/dot_general | solution.py:143
  178.1 0.6 copy-done.5
  178.8 0.8 gather_fusion
  179.8 11.4 %all_to_all.5 = bf16[16,8,256]{2,1,0:T(8,128)(2,1)S(1)} all-to-all(bf16[16,8,256]{2,1,0:T(8,128)(2,1)S(1)} %bitcast_select_fusion), channel_id=1, replica_groups=mesh['dp'=16,'vocab'=2] {'dp'}, dimensions={0} | all-to-all | bytes 131072 | tf_op jit(solution)/shard_map/all_to_all | solution.py:151
  191.1 1.4 convolution_convert_fusion
  192.6 57.7 %reduce-scatter.2.cloned.1.call-done = f32[16,4096]{1,0:T(8,128)} async-done(((f32[256,4096]{1,0:T(8,128)}), f32[16,4096]{1,0:T(8,128)}) %reduce-scatter.2.cloned.1.call-update) | async-done | bytes 262160 | tf_op jit(solution)/shard_map/reduce_scatter | solution.py:142
  (33 shorter events, 0.8 us)
Async XLA Ops:
  7.2 3.0 %copy-start = (bf16[256,4096]{1,0:T(8,128)(2,1)S(1)}, bf16[256,4096]{1,0:T(8,128)(2,1)}, u32[]{:S(2)}) copy-start(bf16[256,4096]{1,0:T(8,128)(2,1)} %param.9) | copy-start | bytes 6291460
  7.2 3.0 %copy-start.1 = (bf16[128,4096]{1,0:T(8,128)(2,1)S(1)}, bf16[128,4096]{1,0:T(8,128)(2,1)}, u32[]{:S(2)}) copy-start(bf16[128,4096]{1,0:T(8,128)(2,1)} %param.8) | copy-start | bytes 3145732
  7.2 109.1 %all-gather.2.cloned.1.call-start = ((), (), s32[]{:S(2)}) async-start(), calls=%async_computation.2 | async-start | bytes 21168128 | tf_op jit(solution)/shard_map/all_gather | solution.py:123
  7.9 242.4 %reduce-scatter.2.cloned.1.call-start = ((), (), s32[]{:S(2)}) async-start(), calls=%async_computation.3 | async-start | bytes 4456448 | tf_op jit(solution)/shard_map/reduce_scatter | solution.py:142
  9.3 1.7 copy-start.4
  25.6 116.5 %copy-start.2 = (s32[128]{0:T(128)S(1)}, s32[128]{0:T(128)}, u32[]{:S(2)}) copy-start(s32[128]{0:T(128)} %param.11) | copy-start | bytes 1540
  25.6 116.5 %copy-start.3 = (bf16[128]{0:T(256)(128)(2,1)S(1)}, bf16[128]{0:T(256)(128)(2,1)}, u32[]{:S(2)}) copy-start(bf16[128]{0:T(256)(128)(2,1)} %param.13) | copy-start | bytes 772
  178.0 0.7 copy-start.5
Sparse Core Ops, SparseCore 0:
  9.6 106.5 all-gather.1
  178.2 72.0 reduce-scatter.1

commit v10 on v8

--- a/solution.py
+++ b/solution.py
@@ -120,6 +120,11 @@
     width = vocab_factor.shape[1]
     tiles = width // 128
     first = lax.axis_index("vocab") * width
+    pair = lax.axis_size("vocab") == 2
+
+    def partner(x):
+        return lax.ppermute(x, "vocab", perm=[(0, 1), (1, 0)])
+
     factor = lax.all_gather(vocab_factor, "dp", axis=0, tiled=True)
     row_words = jnp.repeat(grammar, row_count // grammar.shape[0], axis=0)
     weight = cotangent.astype(jnp.float32) * lengths.astype(jnp.float32) / PREFIX_MAX
@@ -134,10 +139,19 @@
     tile_bits = bits.reshape(row_count, -1)[:, :tiles]
     local_peak, local_total, grads = softmax_parts(latent, factor, tile_bits, target_local)
     local_peak = local_peak[:, 0]
-    peak = lax.pmax(local_peak, "vocab")
-    total = lax.psum(local_total[:, 0] * jnp.exp(local_peak - peak), "vocab")
+    local_total = local_total[:, 0]
+    if pair:
+        other_peak, other_total = partner(jnp.stack([local_peak, local_total]))
+        peak = jnp.maximum(local_peak, other_peak)
+        total = local_total * jnp.exp(local_peak - peak) + other_total * jnp.exp(other_peak - peak)
+    else:
+        peak = lax.pmax(local_peak, "vocab")
+        total = lax.psum(local_total * jnp.exp(local_peak - peak), "vocab")
     rank_partial = grads(peak[:, None], (weight / total)[:, None], weight[:, None])
-    rank_grad = lax.psum(rank_partial, "vocab").astype(jnp.bfloat16)
+    if pair:
+        rank_grad = (rank_partial + partner(rank_partial)).astype(jnp.bfloat16)
+    else:
+        rank_grad = lax.psum(rank_partial, "vocab").astype(jnp.bfloat16)
 
     grad_factor = lax.psum_scatter(
         lax.dot_general(

time: 257 us -> 247 us (0.961)
  blocking collectives: 43.6 us -> 23.3 us
  waiting for transfers between devices: 148 us -> 154 us
  starting transfers between devices: 0.08 us -> 3.09 us
    psum x2 -> x0, blocking collectives: 15.3 us -> none  [the longest x1 10.4 us: body(): rank_grad = lax.psum(rank_partial, 'vocab').astype(jnp.bfloat16)]
    ppermute x0 -> x2, waiting for transfers between devices: none -> 5.79 us  [partner(): return lax.ppermute(x, 'vocab', perm=[(0, 1), (1, 0)])]
    pmax x1 -> x0, blocking collectives: 4.94 us -> none  [body(): peak = lax.pmax(local_peak, 'vocab')]
    ppermute x0 -> x2, starting transfers between devices: none -> 3.02 us  [partner(): return lax.ppermute(x, 'vocab', perm=[(0, 1), (1, 0)])]
  transfers between devices with their start and end apart: 2 -> 4, of which waited for: 2 -> 4; matrix products, arithmetic and copies ran while one was open for 4% -> 4% of each run, Pallas kernels for 0% -> 0%
where the time goes in v10:
time: 247 us
  waiting for transfers between devices  154 us (62%)
  Pallas kernels  34 us (14%)
  blocking collectives  23.3 us (9%)
  between operations  14.2 us (6%)
  other arithmetic  6.78 us (3%)
  local copies, waits for them, and re-layouts  6.64 us (3%)
  matrix products  4.91 us (2%)
  starting transfers between devices  3.09 us (1%)
    all_gather x1, waiting for transfers between devices, body(): factor = lax.all_gather(vocab_factor, 'dp', axis=0, tiled=True)  89.6 us
    reduce_scatter x1, waiting for transfers between devices, body(): lax.psum_scatter(lax.dot_general(rank_grad, hidden, (((0,), (0,)), ((), (...  57.9 us
    pallas_call x1, Pallas kernels, grads(): pl.pallas_call(functools.partial(grad_kernel, block_cols=block_cols), gri...  18.9 us
    pallas_call x1, Pallas kernels, softmax_parts(): peak, total = stats(latent, factor, bits, expand, target)  15.1 us
    psum x1, blocking collectives, body(): latent = lax.psum(partial_latent, 'vocab').astype(jnp.bfloat16)  11.9 us
    all_to_all x1, blocking collectives, body(): lax.all_to_all(picked, 'dp', split_axis=0, concat_axis=0, tiled=True)  11.4 us
    ppermute x2, waiting for transfers between devices, partner(): return lax.ppermute(x, 'vocab', perm=[(0, 1), (1, 0)])  5.79 us
  transfers between devices with their start and end apart: 4, of which 4 were waited for; matrix products, arithmetic and copies ran while one was open for 4% of the time, Pallas kernels for 0%

profile of v10, /device:TPU:0, one launch (start us, length us, event | category | flops | bytes accessed | tf_op | source)
XLA Modules:
  0.0 247.0 jit_solution(4069285332230078496)
XLA Ops:
  8.0 0.9 copy.15
  10.0 1.0 select_convert_fusion
  10.9 0.9 copy.22.bias_ref
  11.8 0.8 fusion.12
  12.7 0.7 copy.19.target_ref
  13.4 11.9 %all-reduce.2.latent_ref = bf16[128,256]{1,0:T(8,128)(2,1)} all-reduce(f32[128,256]{1,0:T(8,128)S(1)} %fusion.12), channel_id=1, replica_groups=mesh['dp'=16,'vocab'=2] {'vocab'}, use_global_device_ids=true, to_apply=%region_0.0 | all-reduce | flops 32768 | bytes 196608 | tf_op jit(solution)/shard_map/psum | solution.py:135
  25.4 1.3 fusion.expand_ref
  26.7 89.6 %all-gather.2.cloned.1.call-done.factor_ref = bf16[256,38912]{1,0:T(8,128)(2,1)} async-done(((bf16[16,38912]{1,0:T(8,128)(2,1)}), bf16[256,38912]{1,0:T(8,128)(2,1)}) %all-gather.2.cloned.1.call-update) | async-done | bytes 19922960 | tf_op jit(solution)/shard_map/all_gather | solution.py:128
  116.2 15.1 %shard_map.95 = (f32[128,1]{1,0:T(8,128)}, f32[128,1]{1,0:T(8,128)}) custom-call(bf16[128,256]{1,0:T(8,128)(2,1)} %all-reduce.2.latent_ref, bf16[256,38912]{1,0:T(8,128)(2,1)} %all-gather.2.cloned.1.call-done.factor_ref, bf16[128,1024]{1,0:T(8,128)(2,1)} %copy.22.bias_ref, bf16[128,4864]{1,0:T(8,128)(2,1)} %fusion.expand_ref, s32[128,1]{1,0:T(8,128)} %copy.19.target_ref), custom_call_target="tpu_custom_call" | custom-call | flops 3825205248 | bytes 19922944 | tf_op jit(solution)/shard_map/pallas_call | solution.py:111
  131.3 0.9 reduce
  132.3 1.0 reduce.1
  133.2 1.5 collective-permute-start
  134.8 2.1 collective-permute-done
  136.9 0.8 copy.20.scale_ref
  138.5 1.5 max.6.peak_ref
  140.0 18.9 %shard_map.96 = f32[128,256]{1,0:T(8,128)} custom-call(bf16[128,256]{1,0:T(8,128)(2,1)} %all-reduce.2.latent_ref, bf16[256,38912]{1,0:T(8,128)(2,1)} %all-gather.2.cloned.1.call-done.factor_ref, bf16[128,1024]{1,0:T(8,128)(2,1)} %copy.22.bias_ref, bf16[128,4864]{1,0:T(8,128)(2,1)} %fusion.expand_ref, s32[128,1]{1,0:T(8,128)} %copy.19.target_ref, ...), custom_call_target="tpu_custom_call" | custom-call | flops 6375342080 | bytes 19922944 | tf_op jit(solution)/shard_map/pallas_call | solution.py:97
  158.9 1.5 collective-permute-start.1
  160.3 3.7 %collective-permute-done.1 = f32[128,256]{1,0:T(8,128)S(1)} collective-permute-done((f32[128,256]{1,0:T(8,128)}, f32[128,256]{1,0:T(8,128)S(1)}, u32[]{:S(2)}, u32[]{:S(2)}) %collective-permute-start.1) | collective-permute-done | bytes 131104 | tf_op jit(solution)/shard_map/ppermute | solution.py:126
  164.0 0.9 add_convert_fusion
  165.0 2.7 %fusion.13 = f32[256,4096]{1,0:T(8,128)} fusion(bf16[128,256]{1,0:T(8,128)(2,1)S(1)} %add_convert_fusion, bf16[128,4096]{1,0:T(8,128)(2,1)S(1)} %copy-done.1), kind=kOutput, calls=%fused_computation.35 | convolution fusion | flops 268435456 | bytes 5308416 | tf_op jit(solution)/shard_map/dot_general | solution.py:157
  168.4 0.8 gather_fusion
  169.4 11.4 %all_to_all.5 = bf16[16,8,256]{2,1,0:T(8,128)(2,1)S(1)} all-to-all(bf16[16,8,256]{2,1,0:T(8,128)(2,1)S(1)} %bitcast_select_fusion), channel_id=1, replica_groups=mesh['dp'=16,'vocab'=2] {'dp'}, dimensions={0} | all-to-all | bytes 131072 | tf_op jit(solution)/shard_map/all_to_all | solution.py:165
  180.8 1.4 convolution_convert_fusion
  182.2 57.9 %reduce-scatter.2.cloned.1.call-done = f32[16,4096]{1,0:T(8,128)} async-done(((f32[256,4096]{1,0:T(8,128)}), f32[16,4096]{1,0:T(8,128)}) %reduce-scatter.2.cloned.1.call-update) | async-done | bytes 262160 | tf_op jit(solution)/shard_map/reduce_scatter | solution.py:156
  (37 shorter events, 3.6 us)
Async XLA Ops:
  7.2 4.6 %copy-start = (bf16[256,4096]{1,0:T(8,128)(2,1)S(1)}, bf16[256,4096]{1,0:T(8,128)(2,1)}, u32[]{:S(2)}) copy-start(bf16[256,4096]{1,0:T(8,128)(2,1)} %param.9) | copy-start | bytes 6291460
  7.2 4.6 %copy-start.1 = (bf16[128,4096]{1,0:T(8,128)(2,1)S(1)}, bf16[128,4096]{1,0:T(8,128)(2,1)}, u32[]{:S(2)}) copy-start(bf16[128,4096]{1,0:T(8,128)(2,1)} %param.8) | copy-start | bytes 3145732
  7.2 109.1 %all-gather.2.cloned.1.call-start = ((), (), s32[]{:S(2)}) async-start(), calls=%async_computation.2 | async-start | bytes 21168128 | tf_op jit(solution)/shard_map/all_gather | solution.py:128
  7.9 232.2 %reduce-scatter.2.cloned.1.call-start = ((), (), s32[]{:S(2)}) async-start(), calls=%async_computation.3 | async-start | bytes 4456448 | tf_op jit(solution)/shard_map/reduce_scatter | solution.py:156
  10.0 2.7 %copy-start.4 = (s32[128]{0:T(128)S(1)}, s32[128]{0:T(128)}, u32[]{:S(2)}) copy-start(s32[128]{0:T(128)} %param.12) | copy-start | bytes 1540
  26.7 110.2 %copy-start.2 = (s32[128]{0:T(128)S(1)}, s32[128]{0:T(128)}, u32[]{:S(2)}) copy-start(s32[128]{0:T(128)} %param.11) | copy-start | bytes 1540
  26.7 110.2 %copy-start.3 = (bf16[128]{0:T(256)(128)(2,1)S(1)}, bf16[128]{0:T(256)(128)(2,1)}, u32[]{:S(2)}) copy-start(bf16[128]{0:T(256)(128)(2,1)} %param.13) | copy-start | bytes 772
  133.2 3.6 %collective-permute-start = (f32[2,128]{1,0:T(2,128)S(1)}, f32[2,128]{1,0:T(2,128)S(1)}, u32[]{:S(2)}, u32[]{:S(2)}) collective-permute-start(f32[2,128]{1,0:T(2,128)S(1)} %pad_maximum_fusion), channel_id=1, source_target_pairs={{0,1},{1,0},{2,3},{3,2},{4,5},{5,4},{6,7},{7,6},{8,9},{9,8},{10,11... | collective-permute-start | bytes 3080 | tf_op jit(solution)/shard_map/ppermute | solution.py:126
  158.9 5.2 %collective-permute-start.1 = (f32[128,256]{1,0:T(8,128)}, f32[128,256]{1,0:T(8,128)S(1)}, u32[]{:S(2)}, u32[]{:S(2)}) collective-permute-start(f32[128,256]{1,0:T(8,128)} %shard_map.96), channel_id=1, source_target_pairs={{0,1},{1,0},{2,3},{3,2},{4,5},{5,4},{6,7},{7,6},{8,9},{9,8},{10,11... | collective-permute-start | bytes 393224 | tf_op jit(solution)/shard_map/ppermute | solution.py:126
  167.6 0.7 copy-start.5
Sparse Core Ops, SparseCore 0:
  9.6 106.5 all-gather.1
  167.8 72.2 reduce-scatter.1

commit v11 on v10

--- a/solution.py
+++ b/solution.py
@@ -127,7 +127,7 @@
 
     factor = lax.all_gather(vocab_factor, "dp", axis=0, tiled=True)
     row_words = jnp.repeat(grammar, row_count // grammar.shape[0], axis=0)
-    weight = cotangent.astype(jnp.float32) * lengths.astype(jnp.float32) / PREFIX_MAX
+    weight = (cotangent.astype(jnp.float32) * lengths.astype(jnp.float32) / PREFIX_MAX)[:, None]
 
     partial_latent = lax.dot_general(
         hidden, rank_factor, (((1,), (1,)), ((), ())), preferred_element_type=jnp.float32
@@ -138,16 +138,14 @@
     bits = jnp.right_shift(row_words[:, :, None], shifts) & 1
     tile_bits = bits.reshape(row_count, -1)[:, :tiles]
     local_peak, local_total, grads = softmax_parts(latent, factor, tile_bits, target_local)
-    local_peak = local_peak[:, 0]
-    local_total = local_total[:, 0]
     if pair:
-        other_peak, other_total = partner(jnp.stack([local_peak, local_total]))
+        other_peak, other_total = partner(local_peak), partner(local_total)
         peak = jnp.maximum(local_peak, other_peak)
         total = local_total * jnp.exp(local_peak - peak) + other_total * jnp.exp(other_peak - peak)
     else:
         peak = lax.pmax(local_peak, "vocab")
         total = lax.psum(local_total * jnp.exp(local_peak - peak), "vocab")
-    rank_partial = grads(peak[:, None], (weight / total)[:, None], weight[:, None])
+    rank_partial = grads(peak, weight / total, weight)
     if pair:
         rank_grad = (rank_partial + partner(rank_partial)).astype(jnp.bfloat16)
     else:

time: 247 us -> 246 us (level)
    ppermute x2 -> x3, waiting for transfers between devices: 5.79 us -> 7.56 us  [partner(): return lax.ppermute(x, 'vocab', perm=[(0, 1), (1, 0)])]
  transfers between devices with their start and end apart: 4 -> 5, of which waited for: 4 -> 5; matrix products, arithmetic and copies ran while one was open for 4% -> 4% of each run, Pallas kernels for 0% -> 0%
where the time goes in v11:
time: 246 us
  waiting for transfers between devices  156 us (63%)
  Pallas kernels  34 us (14%)
  blocking collectives  23.3 us (9%)
  between operations  14.2 us (6%)
  local copies, waits for them, and re-layouts  5.17 us (2%)
  other arithmetic  4.95 us (2%)
  matrix products  4.93 us (2%)
  starting transfers between devices  3.5 us (1%)
    all_gather x1, waiting for transfers between devices, body(): factor = lax.all_gather(vocab_factor, 'dp', axis=0, tiled=True)  89.6 us
    reduce_scatter x1, waiting for transfers between devices, body(): lax.psum_scatter(lax.dot_general(rank_grad, hidden, (((0,), (0,)), ((), (...  57.9 us
    pallas_call x1, Pallas kernels, grads(): pl.pallas_call(functools.partial(grad_kernel, block_cols=block_cols), gri...  18.9 us
    pallas_call x1, Pallas kernels, softmax_parts(): peak, total = stats(latent, factor, bits, expand, target)  15.1 us
    psum x1, blocking collectives, body(): latent = lax.psum(partial_latent, 'vocab').astype(jnp.bfloat16)  11.9 us
    all_to_all x1, blocking collectives, body(): lax.all_to_all(picked, 'dp', split_axis=0, concat_axis=0, tiled=True)  11.4 us
    ppermute x3, waiting for transfers between devices, partner(): return lax.ppermute(x, 'vocab', perm=[(0, 1), (1, 0)])  7.56 us
  transfers between devices with their start and end apart: 5, of which 5 were waited for; matrix products, arithmetic and copies ran while one was open for 4% of the time, Pallas kernels for 0%

profile of v11, /device:TPU:0, one launch (start us, length us, event | category | flops | bytes accessed | tf_op | source)
XLA Modules:
  0.0 245.8 jit_solution(6558553832872073041)
XLA Ops:
  7.2 0.7 all-gather.2.cloned.1.call-update
  8.0 0.9 copy.14
  9.3 0.7 reshape.33
  10.0 1.0 select_convert_fusion
  10.9 0.9 copy.20.bias_ref
  11.8 0.8 fusion.6
  12.7 0.7 copy.18.target_ref
  13.4 11.9 %all-reduce.2.latent_ref = bf16[128,256]{1,0:T(8,128)(2,1)} all-reduce(f32[128,256]{1,0:T(8,128)S(1)} %fusion.6), channel_id=1, replica_groups=mesh['dp'=16,'vocab'=2] {'vocab'}, use_global_device_ids=true, to_apply=%region_0.0 | all-reduce | flops 32768 | bytes 196608 | tf_op jit(solution)/shard_map/psum | solution.py:135
  25.4 1.3 fusion.expand_ref
  26.6 89.6 %all-gather.2.cloned.1.call-done.factor_ref = bf16[256,38912]{1,0:T(8,128)(2,1)} async-done(((bf16[16,38912]{1,0:T(8,128)(2,1)}), bf16[256,38912]{1,0:T(8,128)(2,1)}) %all-gather.2.cloned.1.call-update) | async-done | bytes 19922960 | tf_op jit(solution)/shard_map/all_gather | solution.py:128
  116.2 15.1 %shard_map.95 = (f32[128,1]{1,0:T(8,128)}, f32[128,1]{1,0:T(8,128)}) custom-call(bf16[128,256]{1,0:T(8,128)(2,1)} %all-reduce.2.latent_ref, bf16[256,38912]{1,0:T(8,128)(2,1)} %all-gather.2.cloned.1.call-done.factor_ref, bf16[128,1024]{1,0:T(8,128)(2,1)} %copy.20.bias_ref, bf16[128,4864]{1,0:T(8,128)(2,1)} %fusion.expand_ref, s32[128,1]{1,0:T(8,128)} %copy.18.target_ref), custom_call_target="tpu_custom_call" | custom-call | flops 3825205248 | bytes 19922944 | tf_op jit(solution)/shard_map/pallas_call | solution.py:111
  131.3 1.5 collective-permute-start
  133.5 2.6 %collective-permute-done = f32[128,1]{1,0:T(8,128)S(1)} collective-permute-done((f32[128,1]{1,0:T(8,128)}, f32[128,1]{1,0:T(8,128)S(1)}, u32[]{:S(2)}, u32[]{:S(2)}) %collective-permute-start) | collective-permute-done | bytes 544 | tf_op jit(solution)/shard_map/ppermute | solution.py:126
  136.1 1.2 collective-permute-done.1
  137.3 1.6 add_divide_fusion
  138.8 18.9 %shard_map.96 = f32[128,256]{1,0:T(8,128)} custom-call(bf16[128,256]{1,0:T(8,128)(2,1)} %all-reduce.2.latent_ref, bf16[256,38912]{1,0:T(8,128)(2,1)} %all-gather.2.cloned.1.call-done.factor_ref, bf16[128,1024]{1,0:T(8,128)(2,1)} %copy.20.bias_ref, bf16[128,4864]{1,0:T(8,128)(2,1)} %fusion.expand_ref, s32[128,1]{1,0:T(8,128)} %copy.18.target_ref, ...), custom_call_target="tpu_custom_call" | custom-call | flops 6375342080 | bytes 19922944 | tf_op jit(solution)/shard_map/pallas_call | solution.py:97
  157.8 1.4 collective-permute-start.2
  159.2 3.8 %collective-permute-done.2 = f32[128,256]{1,0:T(8,128)S(1)} collective-permute-done((f32[128,256]{1,0:T(8,128)}, f32[128,256]{1,0:T(8,128)S(1)}, u32[]{:S(2)}, u32[]{:S(2)}) %collective-permute-start.2) | collective-permute-done | bytes 131104 | tf_op jit(solution)/shard_map/ppermute | solution.py:126
  162.9 0.9 add_convert_fusion
  163.9 2.7 %fusion.7 = f32[256,4096]{1,0:T(8,128)} fusion(bf16[128,256]{1,0:T(8,128)(2,1)S(1)} %add_convert_fusion, bf16[128,4096]{1,0:T(8,128)(2,1)S(1)} %copy-done.1), kind=kOutput, calls=%fused_computation.25 | convolution fusion | flops 268435456 | bytes 5308416 | tf_op jit(solution)/shard_map/dot_general | solution.py:155
  167.3 0.8 gather_fusion
  168.3 11.4 %all_to_all.5 = bf16[16,8,256]{2,1,0:T(8,128)(2,1)S(1)} all-to-all(bf16[16,8,256]{2,1,0:T(8,128)(2,1)S(1)} %bitcast_select_fusion), channel_id=1, replica_groups=mesh['dp'=16,'vocab'=2] {'dp'}, dimensions={0} | all-to-all | bytes 131072 | tf_op jit(solution)/shard_map/all_to_all | solution.py:163
  179.7 1.4 convolution_convert_fusion
  181.1 57.9 %reduce-scatter.2.cloned.1.call-done = f32[16,4096]{1,0:T(8,128)} async-done(((f32[256,4096]{1,0:T(8,128)}), f32[16,4096]{1,0:T(8,128)}) %reduce-scatter.2.cloned.1.call-update) | async-done | bytes 262160 | tf_op jit(solution)/shard_map/reduce_scatter | solution.py:154
  (35 shorter events, 2.0 us)
Async XLA Ops:
  7.2 4.6 %copy-start = (bf16[256,4096]{1,0:T(8,128)(2,1)S(1)}, bf16[256,4096]{1,0:T(8,128)(2,1)}, u32[]{:S(2)}) copy-start(bf16[256,4096]{1,0:T(8,128)(2,1)} %param.9) | copy-start | bytes 6291460
  7.2 4.6 %copy-start.1 = (bf16[128,4096]{1,0:T(8,128)(2,1)S(1)}, bf16[128,4096]{1,0:T(8,128)(2,1)}, u32[]{:S(2)}) copy-start(bf16[128,4096]{1,0:T(8,128)(2,1)} %param.8) | copy-start | bytes 3145732
  7.2 109.1 %all-gather.2.cloned.1.call-start = ((), (), s32[]{:S(2)}) async-start(), calls=%async_computation.2 | async-start | bytes 21168128 | tf_op jit(solution)/shard_map/all_gather | solution.py:128
  7.9 231.1 %reduce-scatter.2.cloned.1.call-start = ((), (), s32[]{:S(2)}) async-start(), calls=%async_computation.3 | async-start | bytes 4456448 | tf_op jit(solution)/shard_map/reduce_scatter | solution.py:154
  10.0 2.7 %copy-start.3 = (s32[128]{0:T(128)S(1)}, s32[128]{0:T(128)}, u32[]{:S(2)}) copy-start(s32[128]{0:T(128)} %param.12) | copy-start | bytes 1540
  26.6 106.7 %copy-start.4 = (s32[128]{0:T(128)S(1)}, s32[128]{0:T(128)}, u32[]{:S(2)}) copy-start(s32[128]{0:T(128)} %param.11) | copy-start | bytes 1540
  26.6 106.7 %copy-start.5 = (bf16[128]{0:T(256)(128)(2,1)S(1)}, bf16[128]{0:T(256)(128)(2,1)}, u32[]{:S(2)}) copy-start(bf16[128]{0:T(256)(128)(2,1)} %param.13) | copy-start | bytes 772
  131.3 4.8 %collective-permute-start = (f32[128,1]{1,0:T(8,128)}, f32[128,1]{1,0:T(8,128)S(1)}, u32[]{:S(2)}, u32[]{:S(2)}) collective-permute-start(f32[128,1]{1,0:T(8,128)} %get-tuple-element.4), channel_id=1, source_target_pairs={{0,1},{1,0},{2,3},{3,2},{4,5},{5,4},{6,7},{7,6},{8,9},{9,8},{10,11... | collective-permute-start | bytes 1544 | tf_op jit(solution)/shard_map/ppermute | solution.py:126
  132.8 4.5 %collective-permute-start.1 = (f32[128,1]{1,0:T(8,128)}, f32[128,1]{1,0:T(8,128)S(1)}, u32[]{:S(2)}, u32[]{:S(2)}) collective-permute-start(f32[128,1]{1,0:T(8,128)} %get-tuple-element.5), channel_id=1, source_target_pairs={{0,1},{1,0},{2,3},{3,2},{4,5},{5,4},{6,7},{7,6},{8,9},{9,8},{10,11... | collective-permute-start | bytes 1544 | tf_op jit(solution)/shard_map/ppermute | solution.py:126
  133.5 5.3 %copy-start.2 = (f32[128,1]{1,0:T(8,128)}, f32[128,1]{1,0:T(8,128)S(1)}, u32[]{:S(2)}) copy-start(f32[128,1]{1,0:T(8,128)S(1)} %copy.17.weight_ref) | copy-start | bytes 1540
  157.8 5.2 %collective-permute-start.2 = (f32[128,256]{1,0:T(8,128)}, f32[128,256]{1,0:T(8,128)S(1)}, u32[]{:S(2)}, u32[]{:S(2)}) collective-permute-start(f32[128,256]{1,0:T(8,128)} %shard_map.96), channel_id=1, source_target_pairs={{0,1},{1,0},{2,3},{3,2},{4,5},{5,4},{6,7},{7,6},{8,9},{9,8},{10,11... | collective-permute-start | bytes 393224 | tf_op jit(solution)/shard_map/ppermute | solution.py:126
  166.5 0.7 copy-start.6
Sparse Core Ops, SparseCore 0:
  9.6 106.5 all-gather.1
  166.7 72.2 reduce-scatter.1

commit v12 on v11

--- a/solution.py
+++ b/solution.py
@@ -50,18 +50,15 @@
     )
 
 
-def tiles_per_block(tiles):
-    for count in (38, 19, 16, 8, 4, 2, 1):
-        if tiles % count == 0:
+def tiles_per_block(tiles, largest):
+    for count in (76, 38, 19, 16, 8, 4, 2, 1):
+        if count <= largest and tiles % count == 0:
             return count
     return 1
 
 
-def softmax_parts(latent, factor, tile_bits, target_local):
-    rows, rank = latent.shape
-    width = factor.shape[1]
-    tiles = width // TILE
-    per_block = tiles_per_block(tiles)
+def block_layout(tile_bits, rows, rank, tiles, largest):
+    per_block = tiles_per_block(tiles, largest)
     blocks = tiles // per_block
     block_cols = per_block * TILE
     padded = jnp.pad(tile_bits.reshape(rows, blocks, per_block), ((0, 0), (0, 0), (0, TILE - per_block)))
@@ -70,34 +67,45 @@
         lax.broadcasted_iota(jnp.int32, (TILE, block_cols), 0)
         == lax.broadcasted_iota(jnp.int32, (TILE, block_cols), 1) // TILE
     ).astype(jnp.bfloat16)
-    target = target_local[:, None]
-    common_specs = [
+    specs = [
         pl.BlockSpec((rows, rank), lambda j: (0, 0)),
         pl.BlockSpec((rank, block_cols), lambda j: (0, j)),
         pl.BlockSpec((rows, TILE), lambda j: (0, j)),
         pl.BlockSpec((TILE, block_cols), lambda j: (0, 0)),
         pl.BlockSpec((rows, 1), lambda j: (0, 0)),
     ]
+    return blocks, block_cols, bits, expand, specs
+
+
+def softmax_parts(latent, factor, tile_bits, target_local):
+    rows, rank = latent.shape
+    width = factor.shape[1]
+    tiles = width // TILE
+    target = target_local[:, None]
     column_spec = pl.BlockSpec((rows, 1), lambda j: (0, 0))
     params = pltpu.CompilerParams(dimension_semantics=("arbitrary",))
     matmul_flops = 2 * rows * rank * width + 2 * rows * TILE * width
-    stats = pl.pallas_call(
+    blocks, block_cols, bits, expand, specs = block_layout(tile_bits, rows, rank, tiles, 76)
+    peak, total = pl.pallas_call(
         functools.partial(stats_kernel, block_cols=block_cols),
         grid=(blocks,),
-        in_specs=common_specs,
+        in_specs=specs,
         out_specs=[column_spec, column_spec],
         out_shape=[jax.ShapeDtypeStruct((rows, 1), jnp.float32)] * 2,
         compiler_params=params,
         cost_estimate=pl.CostEstimate(
             flops=matmul_flops, transcendentals=rows * width, bytes_accessed=rank * width * 2
         ),
+    )(latent, factor, bits, expand, target)
+    grad_blocks, grad_cols, grad_bits, grad_expand, grad_specs = block_layout(
+        tile_bits, rows, rank, tiles, 38
     )
 
     def grads(peak, scale, weight):
         return pl.pallas_call(
-            functools.partial(grad_kernel, block_cols=block_cols),
-            grid=(blocks,),
-            in_specs=common_specs + [column_spec] * 3,
+            functools.partial(grad_kernel, block_cols=grad_cols),
+            grid=(grad_blocks,),
+            in_specs=grad_specs + [column_spec] * 3,
             out_specs=pl.BlockSpec((rows, rank), lambda j: (0, 0)),
             out_shape=jax.ShapeDtypeStruct((rows, rank), jnp.float32),
             compiler_params=params,
@@ -106,9 +114,8 @@
                 transcendentals=rows * width,
                 bytes_accessed=rank * width * 2,
             ),
-        )(latent, factor, bits, expand, target, peak, scale, weight)
+        )(latent, factor, grad_bits, grad_expand, target, peak, scale, weight)
 
-    peak, total = stats(latent, factor, bits, expand, target)
     return peak, total, grads
 
 

time: 246 us -> 245 us (level)
  waiting for transfers between devices: 156 us -> 153 us
  transfers between devices with their start and end apart: 5 -> 5, of which waited for: 5 -> 5; matrix products, arithmetic and copies ran while one was open for 4% -> 5% of each run, Pallas kernels for 0% -> 0%
where the time goes in v12:
time: 245 us
  waiting for transfers between devices  153 us (62%)
  Pallas kernels  33 us (13%)
  blocking collectives  23.3 us (10%)
  between operations  14.2 us (6%)
  other arithmetic  6.93 us (3%)
  local copies, waits for them, and re-layouts  5.95 us (2%)
  matrix products  4.93 us (2%)
  starting transfers between devices  3.49 us (1%)
    all_gather x1, waiting for transfers between devices, body(): factor = lax.all_gather(vocab_factor, 'dp', axis=0, tiled=True)  88.6 us
    reduce_scatter x1, waiting for transfers between devices, body(): lax.psum_scatter(lax.dot_general(rank_grad, hidden, (((0,), (0,)), ((), (...  58 us
    pallas_call x1, Pallas kernels, grads(): pl.pallas_call(functools.partial(grad_kernel, block_cols=grad_cols), grid...  18.9 us
    pallas_call x1, Pallas kernels, softmax_parts(): pl.pallas_call(functools.partial(stats_kernel, block_cols=block_cols), gr...  14.1 us
    psum x1, blocking collectives, body(): latent = lax.psum(partial_latent, 'vocab').astype(jnp.bfloat16)  12 us
    all_to_all x1, blocking collectives, body(): lax.all_to_all(picked, 'dp', split_axis=0, concat_axis=0, tiled=True)  11.4 us
    ppermute x3, waiting for transfers between devices, partner(): return lax.ppermute(x, 'vocab', perm=[(0, 1), (1, 0)])  5.91 us
  transfers between devices with their start and end apart: 5, of which 5 were waited for; matrix products, arithmetic and copies ran while one was open for 5% of the time, Pallas kernels for 0%

profile of v12, /device:TPU:0, one launch (start us, length us, event | category | flops | bytes accessed | tf_op | source)
XLA Modules:
  0.0 245.0 jit_solution(16120453322048062153)
XLA Ops:
  8.0 0.9 copy.14
  10.1 0.8 copy.22.bias_ref
  10.8 0.8 fusion.10
  11.7 0.7 copy.19.target_ref
  12.5 12.0 %all-reduce.3.latent_ref = bf16[128,256]{1,0:T(8,128)(2,1)} all-reduce(f32[128,256]{1,0:T(8,128)S(1)} %fusion.10), channel_id=1, replica_groups=mesh['dp'=16,'vocab'=2] {'vocab'}, use_global_device_ids=true, to_apply=%region_0.0 | all-reduce | flops 32768 | bytes 196608 | tf_op jit(solution)/shard_map/psum | solution.py:142
  24.5 1.3 fusion.1.expand_ref
  25.7 1.9 fusion.expand_ref
  27.7 88.6 %all-gather.2.cloned.1.call-done.factor_ref = bf16[256,38912]{1,0:T(8,128)(2,1)} async-done(((bf16[16,38912]{1,0:T(8,128)(2,1)}), bf16[256,38912]{1,0:T(8,128)(2,1)}) %all-gather.2.cloned.1.call-update) | async-done | bytes 19922960 | tf_op jit(solution)/shard_map/all_gather | solution.py:135
  116.3 14.1 %shard_map.95 = (f32[128,1]{1,0:T(8,128)}, f32[128,1]{1,0:T(8,128)}) custom-call(bf16[128,256]{1,0:T(8,128)(2,1)} %all-reduce.3.latent_ref, bf16[256,38912]{1,0:T(8,128)(2,1)} %all-gather.2.cloned.1.call-done.factor_ref, bf16[128,512]{1,0:T(8,128)(2,1)} %copy.22.bias_ref, bf16[128,9728]{1,0:T(8,128)(2,1)} %fusion.expand_ref, s32[128,1]{1,0:T(8,128)} %copy.19.target_ref), custom_call_target="tpu_custom_call" | custom-call | flops 3825205248 | bytes 19922944 | tf_op jit(solution)/shard_map/pallas_call | solution.py:89
  130.3 1.5 collective-permute-start
  132.4 1.0 select_convert_fusion
  133.4 0.9 copy.21.bias_ref
  134.3 0.8 collective-permute-done
  135.1 1.3 collective-permute-done.1
  136.4 1.6 add_divide_fusion
  138.0 18.9 %shard_map.96 = f32[128,256]{1,0:T(8,128)} custom-call(bf16[128,256]{1,0:T(8,128)(2,1)} %all-reduce.3.latent_ref, bf16[256,38912]{1,0:T(8,128)(2,1)} %all-gather.2.cloned.1.call-done.factor_ref, bf16[128,1024]{1,0:T(8,128)(2,1)} %copy.21.bias_ref, bf16[128,4864]{1,0:T(8,128)(2,1)} %fusion.1.expand_ref, s32[128,1]{1,0:T(8,128)} %copy.19.target_ref, ...), custom_call_target="tpu_custom_call" | custom-call | flops 6375342080 | bytes 19922944 | tf_op jit(solution)/shard_map/pallas_call | solution.py:105
  156.9 1.4 collective-permute-start.2
  158.3 3.8 %collective-permute-done.2 = f32[128,256]{1,0:T(8,128)S(1)} collective-permute-done((f32[128,256]{1,0:T(8,128)}, f32[128,256]{1,0:T(8,128)S(1)}, u32[]{:S(2)}, u32[]{:S(2)}) %collective-permute-start.2) | collective-permute-done | bytes 131104 | tf_op jit(solution)/shard_map/ppermute | solution.py:133
  162.1 0.9 add_convert_fusion
  163.0 2.7 %fusion.11 = f32[256,4096]{1,0:T(8,128)} fusion(bf16[128,256]{1,0:T(8,128)(2,1)S(1)} %add_convert_fusion, bf16[128,4096]{1,0:T(8,128)(2,1)S(1)} %copy-done.1), kind=kOutput, calls=%fused_computation.36 | convolution fusion | flops 268435456 | bytes 5308416 | tf_op jit(solution)/shard_map/dot_general | solution.py:162
  166.5 0.8 gather_fusion
  167.4 11.4 %all_to_all.5 = bf16[16,8,256]{2,1,0:T(8,128)(2,1)S(1)} all-to-all(bf16[16,8,256]{2,1,0:T(8,128)(2,1)S(1)} %bitcast_select_fusion), channel_id=1, replica_groups=mesh['dp'=16,'vocab'=2] {'dp'}, dimensions={0} | all-to-all | bytes 131072 | tf_op jit(solution)/shard_map/all_to_all | solution.py:170
  178.8 1.4 convolution_convert_fusion
  180.2 58.0 %reduce-scatter.2.cloned.1.call-done = f32[16,4096]{1,0:T(8,128)} async-done(((f32[256,4096]{1,0:T(8,128)}), f32[16,4096]{1,0:T(8,128)}) %reduce-scatter.2.cloned.1.call-update) | async-done | bytes 262160 | tf_op jit(solution)/shard_map/reduce_scatter | solution.py:161
  (41 shorter events, 3.4 us)
Async XLA Ops:
  7.2 3.7 %copy-start = (bf16[256,4096]{1,0:T(8,128)(2,1)S(1)}, bf16[256,4096]{1,0:T(8,128)(2,1)}, u32[]{:S(2)}) copy-start(bf16[256,4096]{1,0:T(8,128)(2,1)} %param.9) | copy-start | bytes 6291460
  7.2 3.7 %copy-start.1 = (bf16[128,4096]{1,0:T(8,128)(2,1)S(1)}, bf16[128,4096]{1,0:T(8,128)(2,1)}, u32[]{:S(2)}) copy-start(bf16[128,4096]{1,0:T(8,128)(2,1)} %param.8) | copy-start | bytes 3145732
  7.2 109.1 %all-gather.2.cloned.1.call-start = ((), (), s32[]{:S(2)}) async-start(), calls=%async_computation.2 | async-start | bytes 21168128 | tf_op jit(solution)/shard_map/all_gather | solution.py:135
  7.9 230.3 %reduce-scatter.2.cloned.1.call-start = ((), (), s32[]{:S(2)}) async-start(), calls=%async_computation.3 | async-start | bytes 4456448 | tf_op jit(solution)/shard_map/reduce_scatter | solution.py:161
  9.1 2.6 %copy-start.3 = (s32[128]{0:T(128)S(1)}, s32[128]{0:T(128)}, u32[]{:S(2)}) copy-start(s32[128]{0:T(128)} %param.12) | copy-start | bytes 1540
  9.2 15.2 %copy-start.4 = (s32[128]{0:T(128)S(1)}, s32[128]{0:T(128)}, u32[]{:S(2)}) copy-start(s32[128]{0:T(128)} %param.11) | copy-start | bytes 1540
  9.2 15.2 %copy-start.5 = (bf16[128]{0:T(256)(128)(2,1)S(1)}, bf16[128]{0:T(256)(128)(2,1)}, u32[]{:S(2)}) copy-start(bf16[128]{0:T(256)(128)(2,1)} %param.13) | copy-start | bytes 772
  130.3 4.8 %collective-permute-start = (f32[128,1]{1,0:T(8,128)}, f32[128,1]{1,0:T(8,128)S(1)}, u32[]{:S(2)}, u32[]{:S(2)}) collective-permute-start(f32[128,1]{1,0:T(8,128)} %get-tuple-element.4), channel_id=1, source_target_pairs={{0,1},{1,0},{2,3},{3,2},{4,5},{5,4},{6,7},{7,6},{8,9},{9,8},{10,11... | collective-permute-start | bytes 1544 | tf_op jit(solution)/shard_map/ppermute | solution.py:133
  131.8 4.6 %collective-permute-start.1 = (f32[128,1]{1,0:T(8,128)}, f32[128,1]{1,0:T(8,128)}, u32[]{:S(2)}, u32[]{:S(2)}) collective-permute-start(f32[128,1]{1,0:T(8,128)} %get-tuple-element.5), channel_id=1, source_target_pairs={{0,1},{1,0},{2,3},{3,2},{4,5},{5,4},{6,7},{7,6},{8,9},{9,8},{10,11... | collective-permute-start | bytes 1544 | tf_op jit(solution)/shard_map/ppermute | solution.py:133
  133.4 4.5 %copy-start.2 = (f32[128,1]{1,0:T(8,128)}, f32[128,1]{1,0:T(8,128)S(1)}, u32[]{:S(2)}) copy-start(f32[128,1]{1,0:T(8,128)S(1)} %copy.18.weight_ref) | copy-start | bytes 1540
  156.9 5.2 %collective-permute-start.2 = (f32[128,256]{1,0:T(8,128)}, f32[128,256]{1,0:T(8,128)S(1)}, u32[]{:S(2)}, u32[]{:S(2)}) collective-permute-start(f32[128,256]{1,0:T(8,128)} %shard_map.96), channel_id=1, source_target_pairs={{0,1},{1,0},{2,3},{3,2},{4,5},{5,4},{6,7},{7,6},{8,9},{9,8},{10,11... | collective-permute-start | bytes 393224 | tf_op jit(solution)/shard_map/ppermute | solution.py:133
  165.7 0.7 copy-start.6
Sparse Core Ops, SparseCore 0:
  9.6 106.5 all-gather.1
  165.8 72.3 reduce-scatter.1

commit v13 on v12

--- a/solution.py
+++ b/solution.py
@@ -15,7 +15,11 @@
 
 def block_scores(latent_ref, factor_ref, bias_ref, expand_ref, target_ref, block_cols):
     target_rel = target_ref[...] - pl.program_id(0) * block_cols
-    bias = jnp.dot(bias_ref[...], expand_ref[...], preferred_element_type=jnp.float32)
+    flags = bias_ref[...].astype(jnp.float32)
+    rows = flags.shape[0]
+    bias = jnp.concatenate(
+        [jnp.broadcast_to(flags[:, t : t + 1], (rows, TILE)) for t in range(block_cols // TILE)], axis=1
+    )
     logits = jnp.dot(latent_ref[...], factor_ref[...], preferred_element_type=jnp.float32)
     target_hit = lax.broadcasted_iota(jnp.int32, logits.shape, 1) == target_rel
     return jnp.where(target_hit, logits, logits + bias), target_hit

time: 245 us -> 242 us (0.988)
  Pallas kernels: 33 us -> 29.6 us
    pallas_call x1, Pallas kernels: 18.9 us -> 15.6 us  [grads(): pl.pallas_call(functools.partial(grad_kernel, block_cols=grad_cols), grid...]
where the time goes in v13:
time: 242 us
  waiting for transfers between devices  153 us (63%)
  Pallas kernels  29.6 us (12%)
  blocking collectives  23.3 us (10%)
  between operations  14.2 us (6%)
  other arithmetic  6.93 us (3%)
  local copies, waits for them, and re-layouts  5.95 us (2%)
  matrix products  4.93 us (2%)
  starting transfers between devices  3.49 us (1%)
    all_gather x1, waiting for transfers between devices, body(): factor = lax.all_gather(vocab_factor, 'dp', axis=0, tiled=True)  88.6 us
    reduce_scatter x1, waiting for transfers between devices, body(): lax.psum_scatter(lax.dot_general(rank_grad, hidden, (((0,), (0,)), ((), (...  58 us
    pallas_call x1, Pallas kernels, grads(): pl.pallas_call(functools.partial(grad_kernel, block_cols=grad_cols), grid...  15.6 us
    pallas_call x1, Pallas kernels, softmax_parts(): pl.pallas_call(functools.partial(stats_kernel, block_cols=block_cols), gr...  14 us
    psum x1, blocking collectives, body(): latent = lax.psum(partial_latent, 'vocab').astype(jnp.bfloat16)  12 us
    all_to_all x1, blocking collectives, body(): lax.all_to_all(picked, 'dp', split_axis=0, concat_axis=0, tiled=True)  11.4 us
    ppermute x3, waiting for transfers between devices, partner(): return lax.ppermute(x, 'vocab', perm=[(0, 1), (1, 0)])  5.89 us
  transfers between devices with their start and end apart: 5, of which 5 were waited for; matrix products, arithmetic and copies ran while one was open for 5% of the time, Pallas kernels for 0%

profile of v13, /device:TPU:0, one launch (start us, length us, event | category | flops | bytes accessed | tf_op | source)
XLA Modules:
  0.0 241.6 jit_solution(15042808905815773548)
XLA Ops:
  8.0 0.9 copy.14
  10.1 0.8 copy.22.bias_ref
  10.8 0.8 fusion.10
  11.7 0.7 copy.19.target_ref
  12.5 12.0 %all-reduce.3.latent_ref = bf16[128,256]{1,0:T(8,128)(2,1)} all-reduce(f32[128,256]{1,0:T(8,128)S(1)} %fusion.10), channel_id=1, replica_groups=mesh['dp'=16,'vocab'=2] {'vocab'}, use_global_device_ids=true, to_apply=%region_0.0 | all-reduce | flops 32768 | bytes 196608 | tf_op jit(solution)/shard_map/psum | solution.py:146
  24.5 1.3 fusion.1.expand_ref
  25.7 1.9 fusion.expand_ref
  27.7 88.6 %all-gather.2.cloned.1.call-done.factor_ref = bf16[256,38912]{1,0:T(8,128)(2,1)} async-done(((bf16[16,38912]{1,0:T(8,128)(2,1)}), bf16[256,38912]{1,0:T(8,128)(2,1)}) %all-gather.2.cloned.1.call-update) | async-done | bytes 19922960 | tf_op jit(solution)/shard_map/all_gather | solution.py:139
  116.3 14.0 %shard_map.95 = (f32[128,1]{1,0:T(8,128)}, f32[128,1]{1,0:T(8,128)}) custom-call(bf16[128,256]{1,0:T(8,128)(2,1)} %all-reduce.3.latent_ref, bf16[256,38912]{1,0:T(8,128)(2,1)} %all-gather.2.cloned.1.call-done.factor_ref, bf16[128,512]{1,0:T(8,128)(2,1)} %copy.22.bias_ref, bf16[128,9728]{1,0:T(8,128)(2,1)} %fusion.expand_ref, s32[128,1]{1,0:T(8,128)} %copy.19.target_ref), custom_call_target="tpu_custom_call" | custom-call | flops 3825205248 | bytes 19922944 | tf_op jit(solution)/shard_map/pallas_call | solution.py:93
  130.2 1.5 collective-permute-start
  132.2 1.0 select_convert_fusion
  133.3 0.9 copy.21.bias_ref
  134.2 0.8 collective-permute-done
  135.0 1.3 collective-permute-done.1
  136.3 1.6 add_divide_fusion
  137.8 15.6 %shard_map.96 = f32[128,256]{1,0:T(8,128)} custom-call(bf16[128,256]{1,0:T(8,128)(2,1)} %all-reduce.3.latent_ref, bf16[256,38912]{1,0:T(8,128)(2,1)} %all-gather.2.cloned.1.call-done.factor_ref, bf16[128,1024]{1,0:T(8,128)(2,1)} %copy.21.bias_ref, bf16[128,4864]{1,0:T(8,128)(2,1)} %fusion.1.expand_ref, s32[128,1]{1,0:T(8,128)} %copy.19.target_ref, ...), custom_call_target="tpu_custom_call" | custom-call | flops 6375342080 | bytes 19922944 | tf_op jit(solution)/shard_map/pallas_call | solution.py:109
  153.4 1.4 collective-permute-start.2
  154.8 3.8 %collective-permute-done.2 = f32[128,256]{1,0:T(8,128)S(1)} collective-permute-done((f32[128,256]{1,0:T(8,128)}, f32[128,256]{1,0:T(8,128)S(1)}, u32[]{:S(2)}, u32[]{:S(2)}) %collective-permute-start.2) | collective-permute-done | bytes 131104 | tf_op jit(solution)/shard_map/ppermute | solution.py:137
  158.6 0.9 add_convert_fusion
  159.6 2.7 %fusion.11 = f32[256,4096]{1,0:T(8,128)} fusion(bf16[128,256]{1,0:T(8,128)(2,1)S(1)} %add_convert_fusion, bf16[128,4096]{1,0:T(8,128)(2,1)S(1)} %copy-done.1), kind=kOutput, calls=%fused_computation.36 | convolution fusion | flops 268435456 | bytes 5308416 | tf_op jit(solution)/shard_map/dot_general | solution.py:166
  163.0 0.8 gather_fusion
  164.0 11.4 %all_to_all.5 = bf16[16,8,256]{2,1,0:T(8,128)(2,1)S(1)} all-to-all(bf16[16,8,256]{2,1,0:T(8,128)(2,1)S(1)} %bitcast_select_fusion), channel_id=1, replica_groups=mesh['dp'=16,'vocab'=2] {'dp'}, dimensions={0} | all-to-all | bytes 131072 | tf_op jit(solution)/shard_map/all_to_all | solution.py:174
  175.3 1.4 convolution_convert_fusion
  176.8 58.0 %reduce-scatter.2.cloned.1.call-done = f32[16,4096]{1,0:T(8,128)} async-done(((f32[256,4096]{1,0:T(8,128)}), f32[16,4096]{1,0:T(8,128)}) %reduce-scatter.2.cloned.1.call-update) | async-done | bytes 262160 | tf_op jit(solution)/shard_map/reduce_scatter | solution.py:165
  (41 shorter events, 3.4 us)
Async XLA Ops:
  7.2 3.7 %copy-start = (bf16[256,4096]{1,0:T(8,128)(2,1)S(1)}, bf16[256,4096]{1,0:T(8,128)(2,1)}, u32[]{:S(2)}) copy-start(bf16[256,4096]{1,0:T(8,128)(2,1)} %param.9) | copy-start | bytes 6291460
  7.2 3.7 %copy-start.1 = (bf16[128,4096]{1,0:T(8,128)(2,1)S(1)}, bf16[128,4096]{1,0:T(8,128)(2,1)}, u32[]{:S(2)}) copy-start(bf16[128,4096]{1,0:T(8,128)(2,1)} %param.8) | copy-start | bytes 3145732
  7.2 109.1 %all-gather.2.cloned.1.call-start = ((), (), s32[]{:S(2)}) async-start(), calls=%async_computation.2 | async-start | bytes 21168128 | tf_op jit(solution)/shard_map/all_gather | solution.py:139
  7.9 226.8 %reduce-scatter.2.cloned.1.call-start = ((), (), s32[]{:S(2)}) async-start(), calls=%async_computation.3 | async-start | bytes 4456448 | tf_op jit(solution)/shard_map/reduce_scatter | solution.py:165
  9.1 2.6 %copy-start.3 = (s32[128]{0:T(128)S(1)}, s32[128]{0:T(128)}, u32[]{:S(2)}) copy-start(s32[128]{0:T(128)} %param.12) | copy-start | bytes 1540
  9.2 15.2 %copy-start.4 = (s32[128]{0:T(128)S(1)}, s32[128]{0:T(128)}, u32[]{:S(2)}) copy-start(s32[128]{0:T(128)} %param.11) | copy-start | bytes 1540
  9.2 15.2 %copy-start.5 = (bf16[128]{0:T(256)(128)(2,1)S(1)}, bf16[128]{0:T(256)(128)(2,1)}, u32[]{:S(2)}) copy-start(bf16[128]{0:T(256)(128)(2,1)} %param.13) | copy-start | bytes 772
  130.2 4.8 %collective-permute-start = (f32[128,1]{1,0:T(8,128)}, f32[128,1]{1,0:T(8,128)S(1)}, u32[]{:S(2)}, u32[]{:S(2)}) collective-permute-start(f32[128,1]{1,0:T(8,128)} %get-tuple-element.4), channel_id=1, source_target_pairs={{0,1},{1,0},{2,3},{3,2},{4,5},{5,4},{6,7},{7,6},{8,9},{9,8},{10,11... | collective-permute-start | bytes 1544 | tf_op jit(solution)/shard_map/ppermute | solution.py:137
  131.7 4.6 %collective-permute-start.1 = (f32[128,1]{1,0:T(8,128)}, f32[128,1]{1,0:T(8,128)}, u32[]{:S(2)}, u32[]{:S(2)}) collective-permute-start(f32[128,1]{1,0:T(8,128)} %get-tuple-element.5), channel_id=1, source_target_pairs={{0,1},{1,0},{2,3},{3,2},{4,5},{5,4},{6,7},{7,6},{8,9},{9,8},{10,11... | collective-permute-start | bytes 1544 | tf_op jit(solution)/shard_map/ppermute | solution.py:137
  133.3 4.5 %copy-start.2 = (f32[128,1]{1,0:T(8,128)}, f32[128,1]{1,0:T(8,128)S(1)}, u32[]{:S(2)}) copy-start(f32[128,1]{1,0:T(8,128)S(1)} %copy.18.weight_ref) | copy-start | bytes 1540
  153.4 5.2 %collective-permute-start.2 = (f32[128,256]{1,0:T(8,128)}, f32[128,256]{1,0:T(8,128)S(1)}, u32[]{:S(2)}, u32[]{:S(2)}) collective-permute-start(f32[128,256]{1,0:T(8,128)} %shard_map.96), channel_id=1, source_target_pairs={{0,1},{1,0},{2,3},{3,2},{4,5},{5,4},{6,7},{7,6},{8,9},{9,8},{10,11... | collective-permute-start | bytes 393224 | tf_op jit(solution)/shard_map/ppermute | solution.py:137
  162.2 0.7 copy-start.6
Sparse Core Ops, SparseCore 0:
  9.6 106.5 all-gather.1
  162.4 72.3 reduce-scatter.1

commit v14 on v13

--- a/solution.py
+++ b/solution.py
@@ -13,7 +13,7 @@
 TILE = 128
 
 
-def block_scores(latent_ref, factor_ref, bias_ref, expand_ref, target_ref, block_cols):
+def block_scores(latent_ref, factor_ref, bias_ref, target_ref, block_cols):
     target_rel = target_ref[...] - pl.program_id(0) * block_cols
     flags = bias_ref[...].astype(jnp.float32)
     rows = flags.shape[0]
@@ -25,13 +25,13 @@
     return jnp.where(target_hit, logits, logits + bias), target_hit
 
 
-def stats_kernel(latent_ref, factor_ref, bias_ref, expand_ref, target_ref, peak_ref, total_ref, *, block_cols):
+def stats_kernel(latent_ref, factor_ref, bias_ref, target_ref, peak_ref, total_ref, *, block_cols):
     @pl.when(pl.program_id(0) == 0)
     def _():
         peak_ref[...] = jnp.full(peak_ref.shape, far_below, jnp.float32)
         total_ref[...] = jnp.zeros(total_ref.shape, jnp.float32)
 
-    masked, _ = block_scores(latent_ref, factor_ref, bias_ref, expand_ref, target_ref, block_cols)
+    masked, _ = block_scores(latent_ref, factor_ref, bias_ref, target_ref, block_cols)
     old = peak_ref[...]
     new = jnp.maximum(old, jnp.max(masked, axis=1, keepdims=True))
     total_ref[...] = total_ref[...] * jnp.exp(old - new) + jnp.sum(
@@ -40,13 +40,13 @@
     peak_ref[...] = new
 
 
-def grad_kernel(latent_ref, factor_ref, bias_ref, expand_ref, target_ref, peak_ref, scale_ref, weight_ref,
+def grad_kernel(latent_ref, factor_ref, bias_ref, target_ref, peak_ref, scale_ref, weight_ref,
                 out_ref, *, block_cols):
     @pl.when(pl.program_id(0) == 0)
     def _():
         out_ref[...] = jnp.zeros(out_ref.shape, jnp.float32)
 
-    masked, target_hit = block_scores(latent_ref, factor_ref, bias_ref, expand_ref, target_ref, block_cols)
+    masked, target_hit = block_scores(latent_ref, factor_ref, bias_ref, target_ref, block_cols)
     powers = jnp.exp(masked - peak_ref[...])
     score_grad = (powers * scale_ref[...] - jnp.where(target_hit, weight_ref[...], 0.0)).astype(jnp.bfloat16)
     out_ref[...] += lax.dot_general(
@@ -67,18 +67,13 @@
     block_cols = per_block * TILE
     padded = jnp.pad(tile_bits.reshape(rows, blocks, per_block), ((0, 0), (0, 0), (0, TILE - per_block)))
     bits = jnp.where(padded.reshape(rows, blocks * TILE) == 1, 0.0, far_below).astype(jnp.bfloat16)
-    expand = (
-        lax.broadcasted_iota(jnp.int32, (TILE, block_cols), 0)
-        == lax.broadcasted_iota(jnp.int32, (TILE, block_cols), 1) // TILE
-    ).astype(jnp.bfloat16)
     specs = [
         pl.BlockSpec((rows, rank), lambda j: (0, 0)),
         pl.BlockSpec((rank, block_cols), lambda j: (0, j)),
         pl.BlockSpec((rows, TILE), lambda j: (0, j)),
-        pl.BlockSpec((TILE, block_cols), lambda j: (0, 0)),
         pl.BlockSpec((rows, 1), lambda j: (0, 0)),
     ]
-    return blocks, block_cols, bits, expand, specs
+    return blocks, block_cols, bits, specs
 
 
 def softmax_parts(latent, factor, tile_bits, target_local):
@@ -88,8 +83,8 @@
     target = target_local[:, None]
     column_spec = pl.BlockSpec((rows, 1), lambda j: (0, 0))
     params = pltpu.CompilerParams(dimension_semantics=("arbitrary",))
-    matmul_flops = 2 * rows * rank * width + 2 * rows * TILE * width
-    blocks, block_cols, bits, expand, specs = block_layout(tile_bits, rows, rank, tiles, 76)
+    matmul_flops = 2 * rows * rank * width
+    blocks, block_cols, bits, specs = block_layout(tile_bits, rows, rank, tiles, 76)
     peak, total = pl.pallas_call(
         functools.partial(stats_kernel, block_cols=block_cols),
         grid=(blocks,),
@@ -100,8 +95,8 @@
         cost_estimate=pl.CostEstimate(
             flops=matmul_flops, transcendentals=rows * width, bytes_accessed=rank * width * 2
         ),
-    )(latent, factor, bits, expand, target)
-    grad_blocks, grad_cols, grad_bits, grad_expand, grad_specs = block_layout(
+    )(latent, factor, bits, target)
+    grad_blocks, grad_cols, grad_bits, grad_specs = block_layout(
         tile_bits, rows, rank, tiles, 38
     )
 
@@ -118,7 +113,7 @@
                 transcendentals=rows * width,
                 bytes_accessed=rank * width * 2,
             ),
-        )(latent, factor, grad_bits, grad_expand, target, peak, scale, weight)
+        )(latent, factor, grad_bits, target, peak, scale, weight)
 
     return peak, total, grads
 

time: 242 us -> 241 us (level)
  other arithmetic: 6.93 us -> 3.7 us
  waiting for transfers between devices: 153 us -> 156 us
    all_gather x1, waiting for transfers between devices: 88.6 us -> 91.9 us  [body(): factor = lax.all_gather(vocab_factor, 'dp', axis=0, tiled=True)]
    convert_element_type x2 -> x0, other arithmetic: 3.21 us -> none  [block_layout(): expand = (lax.broadcasted_iota(jnp.int32, (TILE, block_cols), 0) == lax.b...]
  transfers between devices with their start and end apart: 5 -> 5, of which waited for: 5 -> 5; matrix products, arithmetic and copies ran while one was open for 5% -> 4% of each run, Pallas kernels for 0% -> 0%
where the time goes in v14:
time: 241 us; the launch traced here: 240 us
  waiting for transfers between devices  156 us (65%)
  Pallas kernels  28.4 us (12%)
  blocking collectives  23.3 us (10%)
  between operations  14.2 us (6%)
  local copies, waits for them, and re-layouts  5.95 us (2%)
  matrix products  4.94 us (2%)
  other arithmetic  3.7 us (2%)
  starting transfers between devices  3.49 us (1%)
    all_gather x1, waiting for transfers between devices, body(): factor = lax.all_gather(vocab_factor, 'dp', axis=0, tiled=True)  91.9 us
    reduce_scatter x1, waiting for transfers between devices, body(): lax.psum_scatter(lax.dot_general(rank_grad, hidden, (((0,), (0,)), ((), (...  57.9 us
    pallas_call x1, Pallas kernels, grads(): pl.pallas_call(functools.partial(grad_kernel, block_cols=grad_cols), grid...  15.2 us
    pallas_call x1, Pallas kernels, softmax_parts(): pl.pallas_call(functools.partial(stats_kernel, block_cols=block_cols), gr...  13.2 us
    psum x1, blocking collectives, body(): latent = lax.psum(partial_latent, 'vocab').astype(jnp.bfloat16)  11.9 us
    all_to_all x1, blocking collectives, body(): lax.all_to_all(picked, 'dp', split_axis=0, concat_axis=0, tiled=True)  11.4 us
    ppermute x3, waiting for transfers between devices, partner(): return lax.ppermute(x, 'vocab', perm=[(0, 1), (1, 0)])  5.89 us
  transfers between devices with their start and end apart: 5, of which 5 were waited for; matrix products, arithmetic and copies ran while one was open for 4% of the time, Pallas kernels for 0%

profile of v14, /device:TPU:0, one launch (start us, length us, event | category | flops | bytes accessed | tf_op | source)
XLA Modules:
  0.0 240.4 jit_solution(12573637403461678839)
XLA Ops:
  7.2 0.7 all-gather.2.cloned.1.call-update
  8.0 0.9 copy.14
  9.3 0.7 reshape.43
  10.0 0.8 copy.22.bias_ref
  10.8 0.8 fusion.2
  11.7 0.7 copy.19.target_ref
  12.4 11.9 %all-reduce.3.latent_ref = bf16[128,256]{1,0:T(8,128)(2,1)} all-reduce(f32[128,256]{1,0:T(8,128)S(1)} %fusion.2), channel_id=1, replica_groups=mesh['dp'=16,'vocab'=2] {'vocab'}, use_global_device_ids=true, to_apply=%region_0.0 | all-reduce | flops 32768 | bytes 196608 | tf_op jit(solution)/shard_map/psum | solution.py:141
  24.4 91.9 %all-gather.2.cloned.1.call-done.factor_ref = bf16[256,38912]{1,0:T(8,128)(2,1)} async-done(((bf16[16,38912]{1,0:T(8,128)(2,1)}), bf16[256,38912]{1,0:T(8,128)(2,1)}) %all-gather.2.cloned.1.call-update) | async-done | bytes 19922960 | tf_op jit(solution)/shard_map/all_gather | solution.py:134
  116.2 13.2 %shard_map.95 = (f32[128,1]{1,0:T(8,128)}, f32[128,1]{1,0:T(8,128)}) custom-call(bf16[128,256]{1,0:T(8,128)(2,1)} %all-reduce.3.latent_ref, bf16[256,38912]{1,0:T(8,128)(2,1)} %all-gather.2.cloned.1.call-done.factor_ref, bf16[128,512]{1,0:T(8,128)(2,1)} %copy.22.bias_ref, s32[128,1]{1,0:T(8,128)} %copy.19.target_ref), custom_call_target="tpu_custom_call" | custom-call | flops 2550136832 | bytes 19922944 | tf_op jit(solution)/shard_map/pallas_call | solution.py:88
  129.5 1.5 collective-permute-start
  131.5 1.0 select_convert_fusion
  132.6 0.9 copy.21.bias_ref
  133.4 0.8 collective-permute-done
  134.2 1.3 collective-permute-done.1
  135.5 1.6 add_divide_fusion
  137.1 15.2 %shard_map.96 = f32[128,256]{1,0:T(8,128)} custom-call(bf16[128,256]{1,0:T(8,128)(2,1)} %all-reduce.3.latent_ref, bf16[256,38912]{1,0:T(8,128)(2,1)} %all-gather.2.cloned.1.call-done.factor_ref, bf16[128,1024]{1,0:T(8,128)(2,1)} %copy.21.bias_ref, s32[128,1]{1,0:T(8,128)} %copy.19.target_ref, f32[128,1]{1,0:T(8,128)} %get-tuple-element.7.peak_ref, ...), custom_call_target="tpu_custom_call" | custom-call | flops 5100273664 | bytes 19922944 | tf_op jit(solution)/shard_map/pallas_call | solution.py:104
  152.3 1.4 collective-permute-start.2
  153.7 3.8 %collective-permute-done.2 = f32[128,256]{1,0:T(8,128)S(1)} collective-permute-done((f32[128,256]{1,0:T(8,128)}, f32[128,256]{1,0:T(8,128)S(1)}, u32[]{:S(2)}, u32[]{:S(2)}) %collective-permute-start.2) | collective-permute-done | bytes 131104 | tf_op jit(solution)/shard_map/ppermute | solution.py:132
  157.5 0.9 add_convert_fusion
  158.4 2.7 %fusion.3 = f32[256,4096]{1,0:T(8,128)} fusion(bf16[128,256]{1,0:T(8,128)(2,1)S(1)} %add_convert_fusion, bf16[128,4096]{1,0:T(8,128)(2,1)S(1)} %copy-done.1), kind=kOutput, calls=%fused_computation.18 | convolution fusion | flops 268435456 | bytes 5308416 | tf_op jit(solution)/shard_map/dot_general | solution.py:161
  161.9 0.8 gather_fusion
  162.9 11.4 %all_to_all.5 = bf16[16,8,256]{2,1,0:T(8,128)(2,1)S(1)} all-to-all(bf16[16,8,256]{2,1,0:T(8,128)(2,1)S(1)} %bitcast_select_fusion), channel_id=1, replica_groups=mesh['dp'=16,'vocab'=2] {'dp'}, dimensions={0} | all-to-all | bytes 131072 | tf_op jit(solution)/shard_map/all_to_all | solution.py:169
  174.2 1.4 convolution_convert_fusion
  175.7 57.9 %reduce-scatter.2.cloned.1.call-done = f32[16,4096]{1,0:T(8,128)} async-done(((f32[256,4096]{1,0:T(8,128)}), f32[16,4096]{1,0:T(8,128)}) %reduce-scatter.2.cloned.1.call-update) | async-done | bytes 262160 | tf_op jit(solution)/shard_map/reduce_scatter | solution.py:160
  (35 shorter events, 2.0 us)
Async XLA Ops:
  7.2 3.7 %copy-start = (bf16[256,4096]{1,0:T(8,128)(2,1)S(1)}, bf16[256,4096]{1,0:T(8,128)(2,1)}, u32[]{:S(2)}) copy-start(bf16[256,4096]{1,0:T(8,128)(2,1)} %param.9) | copy-start | bytes 6291460
  7.2 3.6 %copy-start.1 = (bf16[128,4096]{1,0:T(8,128)(2,1)S(1)}, bf16[128,4096]{1,0:T(8,128)(2,1)}, u32[]{:S(2)}) copy-start(bf16[128,4096]{1,0:T(8,128)(2,1)} %param.8) | copy-start | bytes 3145732
  7.2 109.1 %all-gather.2.cloned.1.call-start = ((), (), s32[]{:S(2)}) async-start(), calls=%async_computation.2 | async-start | bytes 21168128 | tf_op jit(solution)/shard_map/all_gather | solution.py:134
  7.9 225.6 %reduce-scatter.2.cloned.1.call-start = ((), (), s32[]{:S(2)}) async-start(), calls=%async_computation.3 | async-start | bytes 4456448 | tf_op jit(solution)/shard_map/reduce_scatter | solution.py:160
  9.3 2.4 copy-start.3
  10.0 14.4 %copy-start.4 = (s32[128]{0:T(128)S(1)}, s32[128]{0:T(128)}, u32[]{:S(2)}) copy-start(s32[128]{0:T(128)} %param.11) | copy-start | bytes 1540
  10.0 14.4 %copy-start.5 = (bf16[128]{0:T(256)(128)(2,1)S(1)}, bf16[128]{0:T(256)(128)(2,1)}, u32[]{:S(2)}) copy-start(bf16[128]{0:T(256)(128)(2,1)} %param.13) | copy-start | bytes 772
  129.5 4.8 %collective-permute-start = (f32[128,1]{1,0:T(8,128)}, f32[128,1]{1,0:T(8,128)S(1)}, u32[]{:S(2)}, u32[]{:S(2)}) collective-permute-start(f32[128,1]{1,0:T(8,128)} %get-tuple-element.4), channel_id=1, source_target_pairs={{0,1},{1,0},{2,3},{3,2},{4,5},{5,4},{6,7},{7,6},{8,9},{9,8},{10,11... | collective-permute-start | bytes 1544 | tf_op jit(solution)/shard_map/ppermute | solution.py:132
  130.9 4.6 %collective-permute-start.1 = (f32[128,1]{1,0:T(8,128)}, f32[128,1]{1,0:T(8,128)}, u32[]{:S(2)}, u32[]{:S(2)}) collective-permute-start(f32[128,1]{1,0:T(8,128)} %get-tuple-element.5), channel_id=1, source_target_pairs={{0,1},{1,0},{2,3},{3,2},{4,5},{5,4},{6,7},{7,6},{8,9},{9,8},{10,11... | collective-permute-start | bytes 1544 | tf_op jit(solution)/shard_map/ppermute | solution.py:132
  132.5 4.5 %copy-start.2 = (f32[128,1]{1,0:T(8,128)}, f32[128,1]{1,0:T(8,128)S(1)}, u32[]{:S(2)}) copy-start(f32[128,1]{1,0:T(8,128)S(1)} %copy.18.weight_ref) | copy-start | bytes 1540
  152.3 5.2 %collective-permute-start.2 = (f32[128,256]{1,0:T(8,128)}, f32[128,256]{1,0:T(8,128)S(1)}, u32[]{:S(2)}, u32[]{:S(2)}) collective-permute-start(f32[128,256]{1,0:T(8,128)} %shard_map.96), channel_id=1, source_target_pairs={{0,1},{1,0},{2,3},{3,2},{4,5},{5,4},{6,7},{7,6},{8,9},{9,8},{10,11... | collective-permute-start | bytes 393224 | tf_op jit(solution)/shard_map/ppermute | solution.py:132
  161.1 0.7 copy-start.6
Sparse Core Ops, SparseCore 0:
  9.6 106.5 all-gather.1
  161.3 72.2 reduce-scatter.1

commit v15 on v14

--- a/solution.py
+++ b/solution.py
@@ -97,7 +97,7 @@
         ),
     )(latent, factor, bits, target)
     grad_blocks, grad_cols, grad_bits, grad_specs = block_layout(
-        tile_bits, rows, rank, tiles, 38
+        tile_bits, rows, rank, tiles, 76
     )
 
     def grads(peak, scale, weight):

time: 241 us -> 241 us (level)
  waiting for transfers between devices: 156 us -> 159 us
  transfers between devices with their start and end apart: 5 -> 5, of which waited for: 5 -> 5; matrix products, arithmetic and copies ran while one was open for 4% -> 3% of each run, Pallas kernels for 0% -> 0%
where the time goes in v15:
time: 241 us; the launch traced here: 240 us
  waiting for transfers between devices  159 us (66%)
  Pallas kernels  28.5 us (12%)
  blocking collectives  23.3 us (10%)
  between operations  14.2 us (6%)
  matrix products  4.93 us (2%)
  local copies, waits for them, and re-layouts  4.42 us (2%)
  starting transfers between devices  3.49 us (1%)
  other arithmetic  2.72 us (1%)
    all_gather x1, waiting for transfers between devices, body(): factor = lax.all_gather(vocab_factor, 'dp', axis=0, tiled=True)  92.6 us
    reduce_scatter x1, waiting for transfers between devices, body(): lax.psum_scatter(lax.dot_general(rank_grad, hidden, (((0,), (0,)), ((), (...  58 us
    pallas_call x1, Pallas kernels, grads(): pl.pallas_call(functools.partial(grad_kernel, block_cols=grad_cols), grid...  15.2 us
    pallas_call x1, Pallas kernels, softmax_parts(): pl.pallas_call(functools.partial(stats_kernel, block_cols=block_cols), gr...  13.2 us
    psum x1, blocking collectives, body(): latent = lax.psum(partial_latent, 'vocab').astype(jnp.bfloat16)  11.9 us
    all_to_all x1, blocking collectives, body(): lax.all_to_all(picked, 'dp', split_axis=0, concat_axis=0, tiled=True)  11.4 us
    ppermute x3, waiting for transfers between devices, partner(): return lax.ppermute(x, 'vocab', perm=[(0, 1), (1, 0)])  7.57 us
  transfers between devices with their start and end apart: 5, of which 5 were waited for; matrix products, arithmetic and copies ran while one was open for 3% of the time, Pallas kernels for 0%

profile of v15, /device:TPU:0, one launch (start us, length us, event | category | flops | bytes accessed | tf_op | source)
XLA Modules:
  0.0 240.4 jit_solution(5076520004044635453)
XLA Ops:
  7.2 0.7 all-gather.2.cloned.1.call-update
  8.0 0.9 copy.14
  9.4 0.8 copy.20.bias_ref
  10.1 0.8 fusion.2
  11.0 0.7 copy.18.target_ref
  11.7 11.9 %all-reduce.2.latent_ref = bf16[128,256]{1,0:T(8,128)(2,1)} all-reduce(f32[128,256]{1,0:T(8,128)S(1)} %fusion.2), channel_id=1, replica_groups=mesh['dp'=16,'vocab'=2] {'vocab'}, use_global_device_ids=true, to_apply=%region_0.0 | all-reduce | flops 32768 | bytes 196608 | tf_op jit(solution)/shard_map/psum | solution.py:141
  23.7 92.6 %all-gather.2.cloned.1.call-done.factor_ref = bf16[256,38912]{1,0:T(8,128)(2,1)} async-done(((bf16[16,38912]{1,0:T(8,128)(2,1)}), bf16[256,38912]{1,0:T(8,128)(2,1)}) %all-gather.2.cloned.1.call-update) | async-done | bytes 19922960 | tf_op jit(solution)/shard_map/all_gather | solution.py:134
  116.3 13.2 %shard_map.95 = (f32[128,1]{1,0:T(8,128)}, f32[128,1]{1,0:T(8,128)}) custom-call(bf16[128,256]{1,0:T(8,128)(2,1)} %all-reduce.2.latent_ref, bf16[256,38912]{1,0:T(8,128)(2,1)} %all-gather.2.cloned.1.call-done.factor_ref, bf16[128,512]{1,0:T(8,128)(2,1)} %copy.20.bias_ref, s32[128,1]{1,0:T(8,128)} %copy.18.target_ref), custom_call_target="tpu_custom_call" | custom-call | flops 2550136832 | bytes 19922944 | tf_op jit(solution)/shard_map/pallas_call | solution.py:88
  129.5 1.5 collective-permute-start
  130.9 0.6 collective-permute-start.1
  131.5 0.1 copy.17.weight_ref
  131.6 2.6 %collective-permute-done = f32[128,1]{1,0:T(8,128)S(1)} collective-permute-done((f32[128,1]{1,0:T(8,128)}, f32[128,1]{1,0:T(8,128)S(1)}, u32[]{:S(2)}, u32[]{:S(2)}) %collective-permute-start) | collective-permute-done | bytes 544 | tf_op jit(solution)/shard_map/ppermute | solution.py:132
  134.3 1.2 collective-permute-done.1
  135.4 1.5 add_divide_fusion
  137.0 15.2 %shard_map.96 = f32[128,256]{1,0:T(8,128)} custom-call(bf16[128,256]{1,0:T(8,128)(2,1)} %all-reduce.2.latent_ref, bf16[256,38912]{1,0:T(8,128)(2,1)} %all-gather.2.cloned.1.call-done.factor_ref, bf16[128,512]{1,0:T(8,128)(2,1)} %copy.20.bias_ref, s32[128,1]{1,0:T(8,128)} %copy.18.target_ref, f32[128,1]{1,0:T(8,128)} %get-tuple-element.7.peak_ref, ...), custom_call_target="tpu_custom_call" | custom-call | flops 5100273664 | bytes 19922944 | tf_op jit(solution)/shard_map/pallas_call | solution.py:104
  152.2 1.4 collective-permute-start.2
  153.6 3.8 %collective-permute-done.2 = f32[128,256]{1,0:T(8,128)S(1)} collective-permute-done((f32[128,256]{1,0:T(8,128)}, f32[128,256]{1,0:T(8,128)S(1)}, u32[]{:S(2)}, u32[]{:S(2)}) %collective-permute-start.2) | collective-permute-done | bytes 131104 | tf_op jit(solution)/shard_map/ppermute | solution.py:132
  157.4 0.9 add_convert_fusion
  158.3 2.7 %fusion.3 = f32[256,4096]{1,0:T(8,128)} fusion(bf16[128,256]{1,0:T(8,128)(2,1)S(1)} %add_convert_fusion, bf16[128,4096]{1,0:T(8,128)(2,1)S(1)} %copy-done.1), kind=kOutput, calls=%fused_computation.16 | convolution fusion | flops 268435456 | bytes 5308416 | tf_op jit(solution)/shard_map/dot_general | solution.py:161
  161.0 0.6 copy-done.6
  161.8 0.8 gather_fusion
  162.7 11.4 %all_to_all.5 = bf16[16,8,256]{2,1,0:T(8,128)(2,1)S(1)} all-to-all(bf16[16,8,256]{2,1,0:T(8,128)(2,1)S(1)} %bitcast_select_fusion), channel_id=1, replica_groups=mesh['dp'=16,'vocab'=2] {'dp'}, dimensions={0} | all-to-all | bytes 131072 | tf_op jit(solution)/shard_map/all_to_all | solution.py:169
  174.1 1.4 convolution_convert_fusion
  175.5 58.0 %reduce-scatter.2.cloned.1.call-done = f32[16,4096]{1,0:T(8,128)} async-done(((f32[256,4096]{1,0:T(8,128)}), f32[16,4096]{1,0:T(8,128)}) %reduce-scatter.2.cloned.1.call-update) | async-done | bytes 262160 | tf_op jit(solution)/shard_map/reduce_scatter | solution.py:160
  (32 shorter events, 0.8 us)
Async XLA Ops:
  7.2 3.0 %copy-start = (bf16[256,4096]{1,0:T(8,128)(2,1)S(1)}, bf16[256,4096]{1,0:T(8,128)(2,1)}, u32[]{:S(2)}) copy-start(bf16[256,4096]{1,0:T(8,128)(2,1)} %param.9) | copy-start | bytes 6291460
  7.2 3.0 %copy-start.1 = (bf16[128,4096]{1,0:T(8,128)(2,1)S(1)}, bf16[128,4096]{1,0:T(8,128)(2,1)}, u32[]{:S(2)}) copy-start(bf16[128,4096]{1,0:T(8,128)(2,1)} %param.8) | copy-start | bytes 3145732
  7.2 109.1 %all-gather.2.cloned.1.call-start = ((), (), s32[]{:S(2)}) async-start(), calls=%async_computation.2 | async-start | bytes 21168128 | tf_op jit(solution)/shard_map/all_gather | solution.py:134
  7.9 225.6 %reduce-scatter.2.cloned.1.call-start = ((), (), s32[]{:S(2)}) async-start(), calls=%async_computation.3 | async-start | bytes 4456448 | tf_op jit(solution)/shard_map/reduce_scatter | solution.py:160
  9.3 1.7 copy-start.3
  23.7 107.8 %copy-start.4 = (s32[128]{0:T(128)S(1)}, s32[128]{0:T(128)}, u32[]{:S(2)}) copy-start(s32[128]{0:T(128)} %param.11) | copy-start | bytes 1540
  23.7 107.8 %copy-start.5 = (bf16[128]{0:T(256)(128)(2,1)S(1)}, bf16[128]{0:T(256)(128)(2,1)}, u32[]{:S(2)}) copy-start(bf16[128]{0:T(256)(128)(2,1)} %param.13) | copy-start | bytes 772
  129.5 4.8 %collective-permute-start = (f32[128,1]{1,0:T(8,128)}, f32[128,1]{1,0:T(8,128)S(1)}, u32[]{:S(2)}, u32[]{:S(2)}) collective-permute-start(f32[128,1]{1,0:T(8,128)} %get-tuple-element.4), channel_id=1, source_target_pairs={{0,1},{1,0},{2,3},{3,2},{4,5},{5,4},{6,7},{7,6},{8,9},{9,8},{10,11... | collective-permute-start | bytes 1544 | tf_op jit(solution)/shard_map/ppermute | solution.py:132
  130.9 4.5 %collective-permute-start.1 = (f32[128,1]{1,0:T(8,128)}, f32[128,1]{1,0:T(8,128)S(1)}, u32[]{:S(2)}, u32[]{:S(2)}) collective-permute-start(f32[128,1]{1,0:T(8,128)} %get-tuple-element.5), channel_id=1, source_target_pairs={{0,1},{1,0},{2,3},{3,2},{4,5},{5,4},{6,7},{7,6},{8,9},{9,8},{10,11... | collective-permute-start | bytes 1544 | tf_op jit(solution)/shard_map/ppermute | solution.py:132
  131.6 5.3 %copy-start.2 = (f32[128,1]{1,0:T(8,128)}, f32[128,1]{1,0:T(8,128)S(1)}, u32[]{:S(2)}) copy-start(f32[128,1]{1,0:T(8,128)S(1)} %copy.17.weight_ref) | copy-start | bytes 1540
  152.2 5.2 %collective-permute-start.2 = (f32[128,256]{1,0:T(8,128)}, f32[128,256]{1,0:T(8,128)S(1)}, u32[]{:S(2)}, u32[]{:S(2)}) collective-permute-start(f32[128,256]{1,0:T(8,128)} %shard_map.96), channel_id=1, source_target_pairs={{0,1},{1,0},{2,3},{3,2},{4,5},{5,4},{6,7},{7,6},{8,9},{9,8},{10,11... | collective-permute-start | bytes 393224 | tf_op jit(solution)/shard_map/ppermute | solution.py:132
  161.0 0.7 copy-start.6
Sparse Core Ops, SparseCore 0:
  9.6 106.5 all-gather.1
  161.2 72.3 reduce-scatter.1

commit v16 on v14

--- a/solution.py
+++ b/solution.py
@@ -84,7 +84,7 @@
     column_spec = pl.BlockSpec((rows, 1), lambda j: (0, 0))
     params = pltpu.CompilerParams(dimension_semantics=("arbitrary",))
     matmul_flops = 2 * rows * rank * width
-    blocks, block_cols, bits, specs = block_layout(tile_bits, rows, rank, tiles, 76)
+    blocks, block_cols, bits, specs = block_layout(tile_bits, rows, rank, tiles, 38)
     peak, total = pl.pallas_call(
         functools.partial(stats_kernel, block_cols=block_cols),
         grid=(blocks,),

time: 241 us -> 242 us (level)
  transfers between devices with their start and end apart: 5 -> 5, of which waited for: 5 -> 5; matrix products, arithmetic and copies ran while one was open for 4% -> 3% of each run, Pallas kernels for 0% -> 0%
where the time goes in v16:
time: 242 us
  waiting for transfers between devices  157 us (65%)
  Pallas kernels  29.7 us (12%)
  blocking collectives  23.3 us (10%)
  between operations  14.2 us (6%)
  local copies, waits for them, and re-layouts  5.16 us (2%)
  matrix products  4.93 us (2%)
  other arithmetic  3.66 us (2%)
  starting transfers between devices  3.5 us (1%)
    all_gather x1, waiting for transfers between devices, body(): factor = lax.all_gather(vocab_factor, 'dp', axis=0, tiled=True)  90.9 us
    reduce_scatter x1, waiting for transfers between devices, body(): lax.psum_scatter(lax.dot_general(rank_grad, hidden, (((0,), (0,)), ((), (...  58.2 us
    pallas_call x1, Pallas kernels, grads(): pl.pallas_call(functools.partial(grad_kernel, block_cols=grad_cols), grid...  15.2 us
    pallas_call x1, Pallas kernels, softmax_parts(): pl.pallas_call(functools.partial(stats_kernel, block_cols=block_cols), gr...  14.5 us
    psum x1, blocking collectives, body(): latent = lax.psum(partial_latent, 'vocab').astype(jnp.bfloat16)  11.9 us
    all_to_all x1, blocking collectives, body(): lax.all_to_all(picked, 'dp', split_axis=0, concat_axis=0, tiled=True)  11.4 us
    ppermute x3, waiting for transfers between devices, partner(): return lax.ppermute(x, 'vocab', perm=[(0, 1), (1, 0)])  7.57 us
  transfers between devices with their start and end apart: 5, of which 5 were waited for; matrix products, arithmetic and copies ran while one was open for 3% of the time, Pallas kernels for 0%

profile of v16, /device:TPU:0, one launch (start us, length us, event | category | flops | bytes accessed | tf_op | source)
XLA Modules:
  0.0 241.8 jit_solution(15780406701453454557)
XLA Ops:
  7.2 0.7 all-gather.2.cloned.1.call-update
  8.0 0.9 copy.14
  9.3 0.7 reshape.35
  10.0 1.0 select_convert_fusion
  10.9 0.9 copy.20.bias_ref
  11.8 0.8 fusion.2
  12.7 0.7 copy.18.target_ref
  13.4 11.9 %all-reduce.2.latent_ref = bf16[128,256]{1,0:T(8,128)(2,1)} all-reduce(f32[128,256]{1,0:T(8,128)S(1)} %fusion.2), channel_id=1, replica_groups=mesh['dp'=16,'vocab'=2] {'vocab'}, use_global_device_ids=true, to_apply=%region_0.0 | all-reduce | flops 32768 | bytes 196608 | tf_op jit(solution)/shard_map/psum | solution.py:141
  25.3 90.9 %all-gather.2.cloned.1.call-done.factor_ref = bf16[256,38912]{1,0:T(8,128)(2,1)} async-done(((bf16[16,38912]{1,0:T(8,128)(2,1)}), bf16[256,38912]{1,0:T(8,128)(2,1)}) %all-gather.2.cloned.1.call-update) | async-done | bytes 19922960 | tf_op jit(solution)/shard_map/all_gather | solution.py:134
  116.2 14.5 %shard_map.95 = (f32[128,1]{1,0:T(8,128)}, f32[128,1]{1,0:T(8,128)}) custom-call(bf16[128,256]{1,0:T(8,128)(2,1)} %all-reduce.2.latent_ref, bf16[256,38912]{1,0:T(8,128)(2,1)} %all-gather.2.cloned.1.call-done.factor_ref, bf16[128,1024]{1,0:T(8,128)(2,1)} %copy.20.bias_ref, s32[128,1]{1,0:T(8,128)} %copy.18.target_ref), custom_call_target="tpu_custom_call" | custom-call | flops 2550136832 | bytes 19922944 | tf_op jit(solution)/shard_map/pallas_call | solution.py:88
  130.7 1.5 collective-permute-start
  132.9 2.6 %collective-permute-done = f32[128,1]{1,0:T(8,128)S(1)} collective-permute-done((f32[128,1]{1,0:T(8,128)}, f32[128,1]{1,0:T(8,128)S(1)}, u32[]{:S(2)}, u32[]{:S(2)}) %collective-permute-start) | collective-permute-done | bytes 544 | tf_op jit(solution)/shard_map/ppermute | solution.py:132
  135.5 1.2 collective-permute-done.1
  136.7 1.5 add_divide_fusion
  138.2 15.2 %shard_map.96 = f32[128,256]{1,0:T(8,128)} custom-call(bf16[128,256]{1,0:T(8,128)(2,1)} %all-reduce.2.latent_ref, bf16[256,38912]{1,0:T(8,128)(2,1)} %all-gather.2.cloned.1.call-done.factor_ref, bf16[128,1024]{1,0:T(8,128)(2,1)} %copy.20.bias_ref, s32[128,1]{1,0:T(8,128)} %copy.18.target_ref, f32[128,1]{1,0:T(8,128)} %get-tuple-element.7.peak_ref, ...), custom_call_target="tpu_custom_call" | custom-call | flops 5100273664 | bytes 19922944 | tf_op jit(solution)/shard_map/pallas_call | solution.py:104
  153.5 1.4 collective-permute-start.2
  154.9 3.8 %collective-permute-done.2 = f32[128,256]{1,0:T(8,128)S(1)} collective-permute-done((f32[128,256]{1,0:T(8,128)}, f32[128,256]{1,0:T(8,128)S(1)}, u32[]{:S(2)}, u32[]{:S(2)}) %collective-permute-start.2) | collective-permute-done | bytes 131104 | tf_op jit(solution)/shard_map/ppermute | solution.py:132
  158.6 0.9 add_convert_fusion
  159.6 2.7 %fusion.3 = f32[256,4096]{1,0:T(8,128)} fusion(bf16[128,256]{1,0:T(8,128)(2,1)S(1)} %add_convert_fusion, bf16[128,4096]{1,0:T(8,128)(2,1)S(1)} %copy-done.1), kind=kOutput, calls=%fused_computation.16 | convolution fusion | flops 268435456 | bytes 5308416 | tf_op jit(solution)/shard_map/dot_general | solution.py:161
  162.3 0.6 copy-done.6
  163.0 0.8 gather_fusion
  164.0 11.4 %all_to_all.5 = bf16[16,8,256]{2,1,0:T(8,128)(2,1)S(1)} all-to-all(bf16[16,8,256]{2,1,0:T(8,128)(2,1)S(1)} %bitcast_select_fusion), channel_id=1, replica_groups=mesh['dp'=16,'vocab'=2] {'dp'}, dimensions={0} | all-to-all | bytes 131072 | tf_op jit(solution)/shard_map/all_to_all | solution.py:169
  175.4 1.4 convolution_convert_fusion
  176.8 58.2 %reduce-scatter.2.cloned.1.call-done = f32[16,4096]{1,0:T(8,128)} async-done(((f32[256,4096]{1,0:T(8,128)}), f32[16,4096]{1,0:T(8,128)}) %reduce-scatter.2.cloned.1.call-update) | async-done | bytes 262160 | tf_op jit(solution)/shard_map/reduce_scatter | solution.py:160
  (32 shorter events, 1.4 us)
Async XLA Ops:
  7.2 4.6 %copy-start = (bf16[256,4096]{1,0:T(8,128)(2,1)S(1)}, bf16[256,4096]{1,0:T(8,128)(2,1)}, u32[]{:S(2)}) copy-start(bf16[256,4096]{1,0:T(8,128)(2,1)} %param.9) | copy-start | bytes 6291460
  7.2 4.6 %copy-start.1 = (bf16[128,4096]{1,0:T(8,128)(2,1)S(1)}, bf16[128,4096]{1,0:T(8,128)(2,1)}, u32[]{:S(2)}) copy-start(bf16[128,4096]{1,0:T(8,128)(2,1)} %param.8) | copy-start | bytes 3145732
  7.2 109.1 %all-gather.2.cloned.1.call-start = ((), (), s32[]{:S(2)}) async-start(), calls=%async_computation.2 | async-start | bytes 21168128 | tf_op jit(solution)/shard_map/all_gather | solution.py:134
  7.9 227.1 %reduce-scatter.2.cloned.1.call-start = ((), (), s32[]{:S(2)}) async-start(), calls=%async_computation.3 | async-start | bytes 4456448 | tf_op jit(solution)/shard_map/reduce_scatter | solution.py:160
  10.0 2.7 %copy-start.3 = (s32[128]{0:T(128)S(1)}, s32[128]{0:T(128)}, u32[]{:S(2)}) copy-start(s32[128]{0:T(128)} %param.12) | copy-start | bytes 1540
  25.3 107.4 %copy-start.4 = (s32[128]{0:T(128)S(1)}, s32[128]{0:T(128)}, u32[]{:S(2)}) copy-start(s32[128]{0:T(128)} %param.11) | copy-start | bytes 1540
  25.3 107.4 %copy-start.5 = (bf16[128]{0:T(256)(128)(2,1)S(1)}, bf16[128]{0:T(256)(128)(2,1)}, u32[]{:S(2)}) copy-start(bf16[128]{0:T(256)(128)(2,1)} %param.13) | copy-start | bytes 772
  130.7 4.8 %collective-permute-start = (f32[128,1]{1,0:T(8,128)}, f32[128,1]{1,0:T(8,128)S(1)}, u32[]{:S(2)}, u32[]{:S(2)}) collective-permute-start(f32[128,1]{1,0:T(8,128)} %get-tuple-element.4), channel_id=1, source_target_pairs={{0,1},{1,0},{2,3},{3,2},{4,5},{5,4},{6,7},{7,6},{8,9},{9,8},{10,11... | collective-permute-start | bytes 1544 | tf_op jit(solution)/shard_map/ppermute | solution.py:132
  132.2 4.5 %collective-permute-start.1 = (f32[128,1]{1,0:T(8,128)}, f32[128,1]{1,0:T(8,128)S(1)}, u32[]{:S(2)}, u32[]{:S(2)}) collective-permute-start(f32[128,1]{1,0:T(8,128)} %get-tuple-element.5), channel_id=1, source_target_pairs={{0,1},{1,0},{2,3},{3,2},{4,5},{5,4},{6,7},{7,6},{8,9},{9,8},{10,11... | collective-permute-start | bytes 1544 | tf_op jit(solution)/shard_map/ppermute | solution.py:132
  132.9 5.3 %copy-start.2 = (f32[128,1]{1,0:T(8,128)}, f32[128,1]{1,0:T(8,128)S(1)}, u32[]{:S(2)}) copy-start(f32[128,1]{1,0:T(8,128)S(1)} %copy.17.weight_ref) | copy-start | bytes 1540
  153.5 5.2 %collective-permute-start.2 = (f32[128,256]{1,0:T(8,128)}, f32[128,256]{1,0:T(8,128)S(1)}, u32[]{:S(2)}, u32[]{:S(2)}) collective-permute-start(f32[128,256]{1,0:T(8,128)} %shard_map.96), channel_id=1, source_target_pairs={{0,1},{1,0},{2,3},{3,2},{4,5},{5,4},{6,7},{7,6},{8,9},{9,8},{10,11... | collective-permute-start | bytes 393224 | tf_op jit(solution)/shard_map/ppermute | solution.py:132
  162.3 0.7 copy-start.6
Sparse Core Ops, SparseCore 0:
  9.6 106.5 all-gather.1
  162.4 72.5 reduce-scatter.1

commit v17 on v15

--- a/solution.py
+++ b/solution.py
@@ -97,7 +97,7 @@
         ),
     )(latent, factor, bits, target)
     grad_blocks, grad_cols, grad_bits, grad_specs = block_layout(
-        tile_bits, rows, rank, tiles, 76
+        tile_bits, rows, rank, tiles, 19
     )
 
     def grads(peak, scale, weight):

time: 241 us -> 245 us (1.017)
  waiting for transfers between devices: 159 us -> 151 us
  local copies, waits for them, and re-layouts: 4.42 us -> 8.71 us
  Pallas kernels: 28.5 us -> 32.5 us
  other arithmetic: 2.72 us -> 5.18 us
    all_gather x1, waiting for transfers between devices: 92.6 us -> 87.7 us  [body(): factor = lax.all_gather(vocab_factor, 'dp', axis=0, tiled=True)]
    pallas_call x1, Pallas kernels: 15.2 us -> 19.4 us  [grads(): pl.pallas_call(functools.partial(grad_kernel, block_cols=grad_cols), grid...]
    ppermute x3, waiting for transfers between devices: 7.57 us -> 4.62 us  [partner(): return lax.ppermute(x, 'vocab', perm=[(0, 1), (1, 0)])]
    convert_element_type x1 -> x2, local copies, waits for them, and re-layouts: 0.77 us -> 3.71 us  [block_layout(): jnp.where(padded.reshape(rows, blocks * TILE) == 1, 0.0, far_below)]
  transfers between devices with their start and end apart: 5 -> 5, of which waited for: 5 -> 4; matrix products, arithmetic and copies ran while one was open for 3% -> 6% of each run, Pallas kernels for 0% -> 0%
where the time goes in v17:
time: 245 us; the launch traced here: 244 us
  waiting for transfers between devices  151 us (62%)
  Pallas kernels  32.5 us (13%)
  blocking collectives  23.7 us (10%)
  between operations  14.2 us (6%)
  local copies, waits for them, and re-layouts  8.71 us (4%)
  matrix products  5.59 us (2%)
  other arithmetic  5.18 us (2%)
  starting transfers between devices  3.5 us (1%)
    all_gather x1, waiting for transfers between devices, body(): factor = lax.all_gather(vocab_factor, 'dp', axis=0, tiled=True)  87.7 us
    reduce_scatter x1, waiting for transfers between devices, body(): lax.psum_scatter(lax.dot_general(rank_grad, hidden, (((0,), (0,)), ((), (...  57.9 us
    pallas_call x1, Pallas kernels, grads(): pl.pallas_call(functools.partial(grad_kernel, block_cols=grad_cols), grid...  19.4 us
    pallas_call x1, Pallas kernels, softmax_parts(): pl.pallas_call(functools.partial(stats_kernel, block_cols=block_cols), gr...  13.1 us
    psum x1, blocking collectives, body(): latent = lax.psum(partial_latent, 'vocab').astype(jnp.bfloat16)  12.4 us
    all_to_all x1, blocking collectives, body(): lax.all_to_all(picked, 'dp', split_axis=0, concat_axis=0, tiled=True)  11.4 us
  transfers between devices with their start and end apart: 5, of which 4 were waited for; matrix products, arithmetic and copies ran while one was open for 6% of the time, Pallas kernels for 0%

profile of v17, /device:TPU:0, one launch (start us, length us, event | category | flops | bytes accessed | tf_op | source)
XLA Modules:
  0.0 244.3 jit_solution(322085563613060904)
XLA Ops:
  8.0 0.9 copy.14
  9.1 0.7 shift_right_arithmetic.24
  9.9 1.0 fusion
  11.6 1.5 fusion.2
  13.1 0.7 copy.19.target_ref
  13.8 0.7 select_convert_fusion.1
  14.5 1.7 copy.22.bias_ref
  16.2 12.4 %all-reduce.3.latent_ref = bf16[128,256]{1,0:T(8,128)(2,1)} all-reduce(f32[128,256]{1,0:T(8,128)} %fusion.2), channel_id=1, replica_groups=mesh['dp'=16,'vocab'=2] {'vocab'}, use_global_device_ids=true, to_apply=%region_0.0 | all-reduce | flops 32768 | bytes 196608 | tf_op jit(solution)/shard_map/psum | solution.py:141
  28.6 87.7 %all-gather.2.cloned.1.call-done.factor_ref = bf16[256,38912]{1,0:T(8,128)(2,1)} async-done(((bf16[16,38912]{1,0:T(8,128)(2,1)}), bf16[256,38912]{1,0:T(8,128)(2,1)}) %all-gather.2.cloned.1.call-update) | async-done | bytes 19922960 | tf_op jit(solution)/shard_map/all_gather | solution.py:134
  116.2 13.1 %shard_map.95 = (f32[128,1]{1,0:T(8,128)}, f32[128,1]{1,0:T(8,128)}) custom-call(bf16[128,256]{1,0:T(8,128)(2,1)} %all-reduce.3.latent_ref, bf16[256,38912]{1,0:T(8,128)(2,1)} %all-gather.2.cloned.1.call-done.factor_ref, bf16[128,512]{1,0:T(8,128)(2,1)} %copy.22.bias_ref, s32[128,1]{1,0:T(8,128)} %copy.19.target_ref), custom_call_target="tpu_custom_call" | custom-call | flops 2550136832 | bytes 19922944 | tf_op jit(solution)/shard_map/pallas_call | solution.py:88
  129.4 1.5 collective-permute-start.1
  131.4 0.9 select_convert_fusion
  132.3 2.1 copy.21.bias_ref
  134.5 0.8 collective-permute-done
  135.3 1.5 add_divide_fusion
  136.9 19.4 %shard_map.96 = f32[128,256]{1,0:T(8,128)} custom-call(bf16[128,256]{1,0:T(8,128)(2,1)} %all-reduce.3.latent_ref, bf16[256,38912]{1,0:T(8,128)(2,1)} %all-gather.2.cloned.1.call-done.factor_ref, bf16[128,2048]{1,0:T(8,128)(2,1)} %copy.21.bias_ref, s32[128,1]{1,0:T(8,128)} %copy.19.target_ref, f32[128,1]{1,0:T(8,128)} %get-tuple-element.7.peak_ref, ...), custom_call_target="tpu_custom_call" | custom-call | flops 5100273664 | bytes 19922944 | tf_op jit(solution)/shard_map/pallas_call | solution.py:104
  156.3 1.4 collective-permute-start.2
  157.7 3.8 %collective-permute-done.2 = f32[128,256]{1,0:T(8,128)S(1)} collective-permute-done((f32[128,256]{1,0:T(8,128)}, f32[128,256]{1,0:T(8,128)S(1)}, u32[]{:S(2)}, u32[]{:S(2)}) %collective-permute-start.2) | collective-permute-done | bytes 131104 | tf_op jit(solution)/shard_map/ppermute | solution.py:132
  161.4 0.9 add_convert_fusion
  162.4 2.7 %fusion.3 = f32[256,4096]{1,0:T(8,128)} fusion(bf16[128,256]{1,0:T(8,128)(2,1)S(1)} %add_convert_fusion, bf16[128,4096]{1,0:T(8,128)(2,1)S(1)} %copy-done.1), kind=kOutput, calls=%fused_computation.18 | convolution fusion | flops 268435456 | bytes 5308416 | tf_op jit(solution)/shard_map/dot_general | solution.py:161
  165.8 0.8 gather_fusion
  166.8 11.4 %all_to_all.5 = bf16[16,8,256]{2,1,0:T(8,128)(2,1)S(1)} all-to-all(bf16[16,8,256]{2,1,0:T(8,128)(2,1)S(1)} %bitcast_select_fusion), channel_id=1, replica_groups=mesh['dp'=16,'vocab'=2] {'dp'}, dimensions={0} | all-to-all | bytes 131072 | tf_op jit(solution)/shard_map/all_to_all | solution.py:169
  178.2 1.4 convolution_convert_fusion
  179.6 57.9 %reduce-scatter.2.cloned.1.call-done = f32[16,4096]{1,0:T(8,128)} async-done(((f32[256,4096]{1,0:T(8,128)}), f32[16,4096]{1,0:T(8,128)}) %reduce-scatter.2.cloned.1.call-update) | async-done | bytes 262160 | tf_op jit(solution)/shard_map/reduce_scatter | solution.py:160
  (37 shorter events, 3.3 us)
Async XLA Ops:
  7.2 4.4 %copy-start = (bf16[256,4096]{1,0:T(8,128)(2,1)S(1)}, bf16[256,4096]{1,0:T(8,128)(2,1)}, u32[]{:S(2)}) copy-start(bf16[256,4096]{1,0:T(8,128)(2,1)} %param.9) | copy-start | bytes 6291460
  7.2 4.4 %copy-start.1 = (bf16[128,4096]{1,0:T(8,128)(2,1)S(1)}, bf16[128,4096]{1,0:T(8,128)(2,1)}, u32[]{:S(2)}) copy-start(bf16[128,4096]{1,0:T(8,128)(2,1)} %param.8) | copy-start | bytes 3145732
  7.2 109.1 %all-gather.2.cloned.1.call-start = ((), (), s32[]{:S(2)}) async-start(), calls=%async_computation.2 | async-start | bytes 21168128 | tf_op jit(solution)/shard_map/all_gather | solution.py:134
  7.9 229.6 %reduce-scatter.2.cloned.1.call-start = ((), (), s32[]{:S(2)}) async-start(), calls=%async_computation.3 | async-start | bytes 4456448 | tf_op jit(solution)/shard_map/reduce_scatter | solution.py:160
  9.8 3.3 %copy-start.4 = (s32[128]{0:T(128)S(1)}, s32[128]{0:T(128)}, u32[]{:S(2)}) copy-start(s32[128]{0:T(128)} %param.12) | copy-start | bytes 1540
  11.6 2.3 copy-start.2
  11.6 17.0 %copy-start.5 = (s32[128]{0:T(128)S(1)}, s32[128]{0:T(128)}, u32[]{:S(2)}) copy-start(s32[128]{0:T(128)} %param.11) | copy-start | bytes 1540
  11.6 17.0 %copy-start.6 = (bf16[128]{0:T(256)(128)(2,1)S(1)}, bf16[128]{0:T(256)(128)(2,1)}, u32[]{:S(2)}) copy-start(bf16[128]{0:T(256)(128)(2,1)} %param.13) | copy-start | bytes 772
  129.4 5.1 %collective-permute-start.1 = (f32[128,1]{1,0:T(8,128)}, f32[128,1]{1,0:T(8,128)S(1)}, u32[]{:S(2)}, u32[]{:S(2)}) collective-permute-start(f32[128,1]{1,0:T(8,128)} %get-tuple-element.5), channel_id=1, source_target_pairs={{0,1},{1,0},{2,3},{3,2},{4,5},{5,4},{6,7},{7,6},{8,9},{9,8},{10,11... | collective-permute-start | bytes 1544 | tf_op jit(solution)/shard_map/ppermute | solution.py:132
  130.9 4.5 %collective-permute-start = (f32[128,1]{1,0:T(8,128)}, f32[128,1]{1,0:T(8,128)S(1)}, u32[]{:S(2)}, u32[]{:S(2)}) collective-permute-start(f32[128,1]{1,0:T(8,128)} %get-tuple-element.4), channel_id=1, source_target_pairs={{0,1},{1,0},{2,3},{3,2},{4,5},{5,4},{6,7},{7,6},{8,9},{9,8},{10,11... | collective-permute-start | bytes 1544 | tf_op jit(solution)/shard_map/ppermute | solution.py:132
  134.5 2.4 copy-start.3
  156.3 5.2 %collective-permute-start.2 = (f32[128,256]{1,0:T(8,128)}, f32[128,256]{1,0:T(8,128)S(1)}, u32[]{:S(2)}, u32[]{:S(2)}) collective-permute-start(f32[128,256]{1,0:T(8,128)} %shard_map.96), channel_id=1, source_target_pairs={{0,1},{1,0},{2,3},{3,2},{4,5},{5,4},{6,7},{7,6},{8,9},{9,8},{10,11... | collective-permute-start | bytes 393224 | tf_op jit(solution)/shard_map/ppermute | solution.py:132
  165.0 0.7 copy-start.7
Sparse Core Ops, SparseCore 0:
  9.6 106.5 all-gather.1
  165.2 72.2 reduce-scatter.1
